TPU v7x, 256 devices: a whole 4x4x8 slice. The times are simulated.
256 devices in a mesh: ctx: 16 (over x, z_hi, core), exp: 16 (over z_lo, y).
Axes of the slice: x: 4, y: 4, z: 8 (z_hi: 2, z_lo: 4; z = z_hi * 4 + z_lo), core: 2. Of those that a mesh axis runs over, the one named last changes fastest.
Arguments:
- queries: bfloat16 [16, 1024, 2560], P('exp', 'ctx'), may hold values from -4.5 to 4.5
- keys: bfloat16 [16, 1024, 512], P('exp', 'ctx'), may hold values from -4.5 to 4.5
- values: bfloat16 [16, 1024, 512], P('exp', 'ctx'), may hold values from -6 to 6
- doc_lengths: int32 [16, 4], P('exp'), may hold values from 1 to 512, 1024 in all within a row
- resid: bfloat16 [16, 1024, 5120], P('exp', 'ctx'), may hold values from -6 to 6
- out_weight: bfloat16 [2560, 5120], P(('ctx', 'exp')), may hold values from -1 to 1
- norm_gain: bfloat16 [5120], replicated, may hold values from 0.099609375 to 1.8984375
- router_weight: bfloat16 [5120, 16], replicated, may hold values from -0.078125 to 0.078125
- expert_ids: int32 [16, 1024, 1], P('exp', 'ctx'), may hold values from 0 to 15; in each aligned block of 64 rows (0 to 63, 64 to 127, ..., all dimensions but the last counted through in order) at most 5 rows name the same one
- gate_weight: bfloat16 [16, 5120, 4096], P('exp', None, 'ctx'), may hold values from -0.078125 to 0.078125
- up_weight: bfloat16 [16, 5120, 4096], P('exp', None, 'ctx'), may hold values from -0.078125 to 0.078125
- down_weight: bfloat16 [16, 4096, 5120], P('exp', 'ctx'), may hold values from -0.375 to 0.375
Outputs:
- layer_out: bfloat16 [16, 1024, 5120], P('exp', 'ctx')
Inputs may be any that keep to these rules, and one draw needn't show every extreme that they name: `expert_ids`: among the 64 positions p = c * 64 .. c * 64 + 63 of one sequence, for any c, no expert is named more than 5 times.
All inputs are finite; a program needn't handle non-finite values.
Results may differ from a plain program's by a relative error of at most 0.017.
Values may be sent and summed in bfloat16 or wider, within the bound.
No kernel may reach another device: no remote copies, remote signals or barrier semaphores. Data moves between devices by JAX's collectives and lax.ppermute only.
A program may use at most 128 MiB of HBM per device.

v0:
```python
import math

import jax
import jax.numpy as jnp
from jax import lax
from jax.sharding import PartitionSpec as P

HEAD_SIZE = 128


def doc_number(positions, bounds):
    return jnp.sum((positions[:, None] >= bounds[None, :]).astype(jnp.int32), axis=1)


def local(
    queries,
    keys,
    values,
    doc_lengths,
    resid,
    out_weight,
    norm_gain,
    router_weight,
    expert_ids,
    gate_weight,
    up_weight,
    down_weight,
):
    tok_rows = queries.shape[1]
    width = resid.shape[2]
    n_ctx = lax.axis_size("ctx")
    n_exp = lax.axis_size("exp")
    positions = lax.axis_index("ctx") * tok_rows + jnp.arange(tok_rows, dtype=jnp.int32)
    bounds = jnp.cumsum(doc_lengths[0])
    query_doc = doc_number(positions, bounds)
    kv_heads = keys.shape[2] // HEAD_SIZE
    head_groups = queries.shape[2] // keys.shape[2]
    heads_of_query = queries[0].reshape(tok_rows, kv_heads, head_groups, HEAD_SIZE)
    scale = 1.0 / math.sqrt(HEAD_SIZE)
    best = jnp.full((kv_heads, head_groups, tok_rows), -1e30, jnp.float32)
    key_piece = lax.all_gather(keys[0], "ctx", axis=0, tiled=True)
    value_piece = lax.all_gather(values[0], "ctx", axis=0, tiled=True)
    count = key_piece.shape[0]
    heads_of_key = key_piece.reshape(count, kv_heads, HEAD_SIZE)
    heads_of_value = value_piece.reshape(count, kv_heads, HEAD_SIZE)
    scores = (
        jnp.einsum(
            "tkgd,nkd->kgtn", heads_of_query, heads_of_key, preferred_element_type=jnp.float32
        )
        * scale
    )
    key_pos = jnp.arange(count, dtype=jnp.int32)
    visible = (key_pos[None, :] <= positions[:, None]) & (
        doc_number(key_pos, bounds)[None, :] == query_doc[:, None]
    )
    masked = jnp.where(visible, scores, -1e30)
    newbest = jnp.maximum(best, jnp.max(masked, axis=-1))
    weights = jnp.where(visible, jnp.exp(masked - newbest[..., None]), 0.0)
    total = jnp.sum(weights, axis=-1)
    accum = jnp.einsum(
        "kgtn,nkd->kgtd",
        weights.astype(jnp.bfloat16),
        heads_of_value,
        preferred_element_type=jnp.float32,
    )
    best, total, accum = (newbest, total, accum)
    attended = (
        (accum / total[..., None]).transpose(2, 0, 1, 3).reshape(tok_rows, -1).astype(jnp.bfloat16)
    )
    qwidth = attended.shape[1]
    proj_rows = lax.all_gather(out_weight, "exp", axis=0, tiled=True)
    feature_block = lax.all_to_all(
        attended.reshape(tok_rows, n_ctx, qwidth // n_ctx),
        "ctx",
        split_axis=1,
        concat_axis=0,
        tiled=True,
    )
    feature_rows = feature_block.reshape(n_ctx * tok_rows, -1)
    attn_sum = lax.psum_scatter(
        jnp.dot(feature_rows, proj_rows, preferred_element_type=jnp.float32).astype(jnp.bfloat16),
        "ctx",
        scatter_dimension=0,
        tiled=True,
    )
    hidden_state = resid[0].astype(jnp.float32) + attn_sum.astype(jnp.float32)
    mean_square = jnp.mean(hidden_state * hidden_state, axis=-1, keepdims=True)
    normed = hidden_state * lax.rsqrt(mean_square + 1e-05) * norm_gain.astype(jnp.float32)
    normed_b = normed.astype(jnp.bfloat16)
    logits = jnp.dot(normed_b, router_weight, preferred_element_type=jnp.float32)
    n_experts = router_weight.shape[1]
    chosen = expert_ids[0, :, 0]
    picked = chosen[:, None] == jnp.arange(n_experts, dtype=jnp.int32)[None, :]
    score = jax.nn.sigmoid(jnp.sum(jnp.where(picked, logits, 0.0), axis=-1))
    routed = (normed * score[:, None]).astype(jnp.bfloat16)
    capacity = max(2, tok_rows // n_experts + tok_rows // (4 * n_experts))
    lower = jnp.tril(jnp.ones((tok_rows, tok_rows), jnp.float32), -1)
    earlier = jnp.dot(lower, picked.astype(jnp.float32), preferred_element_type=jnp.float32)
    slot_rank = jnp.sum(jnp.where(picked, earlier, 0.0), axis=-1).astype(jnp.int32)
    selector = picked[:, :, None] & (
        slot_rank[:, None, None] == jnp.arange(capacity, dtype=jnp.int32)[None, None, :]
    )
    selector_b = selector.astype(jnp.bfloat16)
    outgoing = jnp.einsum(
        "tes,td->esd", selector_b, routed, preferred_element_type=jnp.float32
    ).astype(jnp.bfloat16)
    arrived = lax.all_to_all(outgoing, "exp", split_axis=0, concat_axis=0, tiled=True)
    arrived_rows = arrived.reshape(-1, width)
    gate_local = gate_weight[0]
    up_local = up_weight[0]
    down_local = down_weight[0]
    piece = lax.all_gather(arrived_rows, "ctx", axis=0, tiled=True)
    gate = jnp.dot(piece, gate_local, preferred_element_type=jnp.float32)
    up = jnp.dot(piece, up_local, preferred_element_type=jnp.float32)
    inner = (jax.nn.silu(gate) * up).astype(jnp.bfloat16)
    summed = lax.psum_scatter(
        jnp.dot(inner, down_local, preferred_element_type=jnp.float32).astype(jnp.bfloat16),
        "ctx",
        scatter_dimension=0,
        tiled=True,
    )
    expert_out = summed.reshape(n_exp, capacity, width)
    returned = lax.all_to_all(expert_out, "exp", split_axis=0, concat_axis=0, tiled=True)
    combined = jnp.einsum("tes,esd->td", selector_b, returned, preferred_element_type=jnp.float32)
    layer_out = (hidden_state + combined).astype(jnp.bfloat16)
    return layer_out[None]


def solution(mesh):
    in_specs = (
        P("exp", "ctx", None),
        P("exp", "ctx", None),
        P("exp", "ctx", None),
        P("exp", None),
        P("exp", "ctx", None),
        P(("ctx", "exp"), None),
        P(),
        P(),
        P("exp", "ctx", None),
        P("exp", None, "ctx"),
        P("exp", None, "ctx"),
        P("exp", "ctx", None),
    )
    out_specs = P("exp", "ctx", None)
    return jax.shard_map(local, mesh=mesh, in_specs=in_specs, out_specs=out_specs, check_vma=False)
```

profile of v0, /device:TPU:1, one launch (start us, length us, event | category | flops | bytes accessed | tf_op | source)
XLA Modules:
  0.0 811.8 jit_solution(17532757584282745511)
XLA Ops:
  6.5 0.7 all-gather.10.cloned.1.call-update
  7.3 0.0 all-gather.12.cloned.1.call-start
  7.3 0.7 all-gather.12.cloned.1.call-update
  8.0 0.0 all-gather.14.cloned.1.call-start
  8.1 0.7 all-gather.14.cloned.1.call-update
  8.7 1.4 reshape_squeeze.3
  10.1 0.8 reduce-window.8
  11.0 0.1 convert_reduce_fusion
  11.0 0.1 convert_reduce_fusion.1
  11.1 0.1 fusion.49
  11.3 58.4 %all-gather.10.cloned.1.call-done = bf16[1,1024,512]{2,1,0:T(8,128)(2,1)} async-done(((bf16[1,64,512]{2,1,0:T(8,128)(2,1)}), bf16[1,1024,512]{2,1,0:T(8,128)(2,1)}) %all-gather.10.cloned.1.call-update) | async-done | bytes 1048592 | tf_op jit(solution)/shard_map/all_gather | solution.py:41
  69.7 2.3 copy.34
  72.0 51.5 %all-gather.12.cloned.1.call-done = bf16[1,1024,512]{2,1,0:T(8,128)(2,1)} async-done(((bf16[1,64,512]{2,1,0:T(8,128)(2,1)}), bf16[1,1024,512]{2,1,0:T(8,128)(2,1)}) %all-gather.12.cloned.1.call-update) | async-done | bytes 1048592 | tf_op jit(solution)/shard_map/all_gather | solution.py:42
  123.5 2.3 copy.37
  125.8 2.4 fusion.3
  128.2 1.6 fusion.4
  129.8 1.5 fusion.32
  131.3 0.2 copy.39
  131.6 1.4 convert_element_type.64
  133.0 2.0 copy.40
  135.0 4.0 all-to-all-start
  139.0 0.0 reduce-scatter.3.cloned.1.call-start
  139.0 61.7 %all-gather.14.cloned.1.call-done = bf16[16,10,5120]{2,1,0:T(8,128)(2,1)} async-done(((bf16[1,10,5120]{2,1,0:T(8,128)(2,1)}), bf16[16,10,5120]{2,1,0:T(8,128)(2,1)}) %all-gather.14.cloned.1.call-update) | async-done | bytes 1638416 | tf_op jit(solution)/shard_map/all_gather | solution.py:71
  200.7 4.0 reshape.133
  204.8 0.0 all-to-all-done
  204.8 6.9 convolution_convert_fusion.1
  211.7 0.0 reduce-scatter.3.cloned.1.call-update
  211.7 0.0 all-gather.8.cloned.1.call-start
  211.8 0.6 copy-done.6
  212.4 0.2 fusion.28
  212.6 0.0 copy-done.5
  212.6 162.6 %reduce-scatter.3.cloned.1.call-done = bf16[64,5120]{1,0:T(8,128)(2,1)} async-done(((bf16[1024,5120]{1,0:T(8,128)(2,1)}), bf16[64,5120]{1,0:T(8,128)(2,1)}) %reduce-scatter.3.cloned.1.call-update) | async-done | bytes 655376 | tf_op jit(solution)/shard_map/reduce_scatter | solution.py:80
  375.2 1.5 multiply_reduce_fusion
  376.7 1.5 fusion.27
  378.2 0.5 convolution_convert_fusion.2
  378.7 0.5 copy.42
  379.2 35.8 %all_to_all.25 = bf16[16,5,5120]{2,1,0:T(8,128)(2,1)} all-to-all(bf16[16,5,5120]{2,1,0:T(8,128)(2,1)S(1)} %copy.42), channel_id=1, replica_groups=mesh['ctx'=16,'exp'=16] {'exp'}, dimensions={0} | all-to-all | bytes 1638400 | tf_op jit(solution)/shard_map/all_to_all | solution.py:107
  415.0 2.2 reshape.125
  417.2 0.0 all-gather.8.cloned.1.call-update
  417.2 0.2 reduce-scatter.5.cloned.1.call-start
  417.5 142.7 %all-gather.8.cloned.1.call-done = bf16[1280,5120]{1,0:T(8,128)(2,1)} async-done(((bf16[80,5120]{1,0:T(8,128)(2,1)}), bf16[1280,5120]{1,0:T(8,128)(2,1)}) %all-gather.8.cloned.1.call-update) | async-done | bytes 13107216 | tf_op jit(solution)/shard_map/all_gather | solution.py:112
  560.1 10.1 %fusion.8 = f32[1280,256]{1,0:T(8,128)} fusion(bf16[1280,5120]{1,0:T(8,128)(2,1)} %all-gather.8.cloned.1.call-done, bf16[1,5120,256]{2,1,0:T(8,128)(2,1)} %param.21), kind=kOutput, calls=%fused_computation.15 | convolution fusion | flops 3355443200 | bytes 17039360 | tf_op jit(solution)/shard_map/dot_general | solution.py:113
  570.2 20.4 %convolution_convert_fusion = bf16[1280,5120]{1,0:T(8,128)(2,1)} fusion(bf16[1,256,5120]{2,1,0:T(8,128)(2,1)S(1)} %copy-done, bf16[1280,5120]{1,0:T(8,128)(2,1)} %all-gather.8.cloned.1.call-done, bf16[1,5120,256]{2,1,0:T(8,128)(2,1)} %param.22, f32[1280,256]{1,0:T(8,128)} %fusion.8), kind=kOutput, calls=%fused_computation | convolution fusion | flops 6719406080 | bytes 32768000 | tf_op jit(solution)/shard_map/dot_general | solution.py:117
  590.6 0.0 reduce-scatter.5.cloned.1.call-update
  590.6 172.4 %reduce-scatter.5.cloned.1.call-done = bf16[80,5120]{1,0:T(8,128)(2,1)} async-done(((bf16[1280,5120]{1,0:T(8,128)(2,1)}), bf16[80,5120]{1,0:T(8,128)(2,1)}) %reduce-scatter.5.cloned.1.call-update) | async-done | bytes 819216 | tf_op jit(solution)/shard_map/reduce_scatter | solution.py:116
  763.0 2.2 reshape.126
  765.3 38.1 %all_to_all.26 = bf16[16,5,5120]{2,1,0:T(8,128)(2,1)S(1)} all-to-all(bf16[16,5,5120]{2,1,0:T(8,128)(2,1)} %reshape.126), channel_id=1, replica_groups=mesh['ctx'=16,'exp'=16] {'exp'}, dimensions={0} | all-to-all | bytes 1638400 | tf_op jit(solution)/shard_map/all_to_all | solution.py:123
  803.3 1.6 fusion.2
  (24 shorter events, 0.1 us)
Async XLA Ops:
  6.5 563.7 %copy-start = (bf16[1,256,5120]{2,1,0:T(8,128)(2,1)S(1)}, bf16[1,256,5120]{2,1,0:T(8,128)(2,1)}, u32[]{:S(2)}) copy-start(bf16[1,256,5120]{2,1,0:T(8,128)(2,1)} %param.23) | copy-start | bytes 7864324
  6.5 63.2 %all-gather.10.cloned.1.call-start = ((), (), s32[]{:S(2)}) async-start(), calls=%async_computation.8 | async-start | bytes 1114112 | tf_op jit(solution)/shard_map/all_gather | solution.py:41
  7.3 116.3 %all-gather.12.cloned.1.call-start = ((), (), s32[]{:S(2)}) async-start(), calls=%async_computation.9 | async-start | bytes 1114112 | tf_op jit(solution)/shard_map/all_gather | solution.py:42
  8.0 192.7 %all-gather.14.cloned.1.call-start = ((), (), s32[]{:S(2)}) async-start(), calls=%async_computation.10 | async-start | bytes 2785280 | tf_op jit(solution)/shard_map/all_gather | solution.py:71
  128.2 1.6 copy-start.4
  135.0 69.8 %all-to-all-start = ((bf16[64,16,160]{2,0,1:T(8,128)(2,1)}), bf16[64,16,160]{2,0,1:T(8,128)(2,1)S(1)}, u32[]{:S(2)}, u32[]{:S(2)}) async-start(bf16[64,16,160]{2,0,1:T(8,128)(2,1)} %copy.40), calls=%async_computation | async-start | bytes 1048576 | tf_op jit(solution)/shard_map/all_to_all | solution.py:72
  139.0 236.2 %reduce-scatter.3.cloned.1.call-start = ((), (), s32[]{:S(2)}) async-start(), calls=%async_computation.5 | async-start | bytes 11141120 | tf_op jit(solution)/shard_map/reduce_scatter | solution.py:80
  211.7 0.7 copy-start.6
  211.7 0.9 copy-start.5
  211.7 163.5 %copy-start.1 = (bf16[1,64,5120]{2,1,0:T(8,128)(2,1)S(1)}, bf16[1,64,5120]{2,1,0:T(8,128)(2,1)}, u32[]{:S(2)}) copy-start(bf16[1,64,5120]{2,1,0:T(8,128)(2,1)} %param.16) | copy-start | bytes 1966084
  211.7 165.0 %copy-start.7 = (bf16[5120,16]{0,1:T(8,128)(2,1)S(1)}, bf16[5120,16]{0,1:T(8,128)(2,1)}, u32[]{:S(2)}) copy-start(bf16[5120,16]{0,1:T(8,128)(2,1)} %param.19) | copy-start | bytes 491524
  211.7 348.4 %all-gather.8.cloned.1.call-start = ((), (), s32[]{:S(2)}) async-start(), calls=%async_computation.6 | async-start | bytes 13926400 | tf_op jit(solution)/shard_map/all_gather | solution.py:112
  375.2 3.0 copy-start.2
  417.2 345.8 %reduce-scatter.5.cloned.1.call-start = ((), (), s32[]{:S(2)}) async-start(), calls=%async_computation.7 | async-start | bytes 13926400 | tf_op jit(solution)/shard_map/reduce_scatter | solution.py:116
  765.3 38.1 %copy-start.3 = (bf16[64,5120]{1,0:T(8,128)(2,1)S(1)}, bf16[64,5120]{1,0:T(8,128)(2,1)}, u32[]{:S(2)}) copy-start(bf16[64,5120]{1,0:T(8,128)(2,1)} %reduce-scatter.3.cloned.1.call-done) | copy-start | bytes 1966084
Sparse Core Ops, SparseCore 0:
  10.0 59.6 all-gather.9
  72.4 51.0 all-gather.11
  125.3 75.3 all-gather.13
  211.9 163.2 reduce-scatter.2
  417.4 142.7 all-gather.7
  590.8 172.2 reduce-scatter.4
where the time goes:
time: 813 us; the launch traced here: 812 us
  waiting for transfers between devices  651 us (80%)
  blocking collectives  73.9 us (9%)
  matrix products  45.1 us (6%)
  local copies, waits for them, and re-layouts  19.1 us (2%)
  between operations  13.6 us (2%)
    reduce_scatter x1, waiting for transfers between devices, local(): lax.psum_scatter(jnp.dot(inner, down_local, preferred_element_type=jnp.fl...  172 us
    reduce_scatter x1, waiting for transfers between devices, local(): lax.psum_scatter(jnp.dot(feature_rows, proj_rows, preferred_element_type=...  163 us
    all_gather x1, waiting for transfers between devices, local(): piece = lax.all_gather(arrived_rows, 'ctx', axis=0, tiled=True)  143 us
    all_gather x1, waiting for transfers between devices, local(): proj_rows = lax.all_gather(out_weight, 'exp', axis=0, tiled=True)  61.7 us
    all_gather x1, waiting for transfers between devices, local(): key_piece = lax.all_gather(keys[0], 'ctx', axis=0, tiled=True)  58.4 us
    all_gather x1, waiting for transfers between devices, local(): value_piece = lax.all_gather(values[0], 'ctx', axis=0, tiled=True)  51.5 us
    all_to_all x1, blocking collectives, local(): lax.all_to_all(expert_out, 'exp', split_axis=0, concat_axis=0, tiled=True)  38.1 us
    all_to_all x1, blocking collectives, local(): lax.all_to_all(outgoing, 'exp', split_axis=0, concat_axis=0, tiled=True)  35.8 us
  transfers between devices with their start and end apart: 7, of which 6 were waited for; matrix products, arithmetic and copies ran while one was open for 3% of the time, Pallas kernels for 0%

commit v1 on v0

v1 whole, which is shorter than its diff:
```python
import math

import jax
import jax.numpy as jnp
from jax import lax
from jax.sharding import Mesh
from jax.sharding import PartitionSpec as P

HEAD_SIZE = 128
CTX = ("x", "zh", "core")
EXP = ("zl", "y")


def doc_number(positions, bounds):
    return jnp.sum((positions[:, None] >= bounds[None, :]).astype(jnp.int32), axis=1)


def _pp(v, axis, n, shift):
    return lax.ppermute(v, axis, [(i, (i + shift) % n) for i in range(n)])


def rel_index():
    x = lax.axis_index("x")
    zh = lax.axis_index("zh")
    c = lax.axis_index("core")
    dx = jnp.array([0, 0, -1, -1, 1, 1, -2, -2], jnp.int32)
    other_z = jnp.array([0, 1, 0, 1, 0, 1, 0, 1], jnp.int32)
    xs = (x + dx) % 4
    zs = (zh + other_z) % 2
    col = xs * 4 + zs * 2
    return jnp.concatenate([col + c, col + (1 - c)])


def ag_rel(b):
    zo = _pp(b, "zh", 2, 1)
    l1 = _pp(b, "x", 4, 1)
    r1 = _pp(b, "x", 4, -1)
    l1o = _pp(zo, "x", 4, 1)
    r1o = _pp(zo, "x", 4, -1)
    l2 = _pp(l1, "x", 4, 1)
    r2o = _pp(r1o, "x", 4, -1)
    first = jnp.concatenate([b, zo, l1, l1o, r1, r1o], 0)
    last = jnp.concatenate([l2, r2o], 0)
    return jnp.concatenate([first, last, _pp(first, "core", 2, 1), _pp(last, "core", 2, 1)], 0)


def rs_rel(p):
    r = p.shape[0] // 16
    got = _pp(p[8 * r:], "core", 2, 1).astype(jnp.float32)
    s = p[: 8 * r].astype(jnp.float32) + got
    blk = [s[i * r:(i + 1) * r] for i in range(8)]
    a = _pp(blk[6].astype(jnp.bfloat16), "x", 4, -1)
    b = _pp(blk[7].astype(jnp.bfloat16), "x", 4, 1)
    s2 = blk[2] + a.astype(jnp.float32)
    s5 = blk[5] + b.astype(jnp.float32)
    to_left = jnp.concatenate([s2, blk[3]], 0).astype(jnp.bfloat16)
    to_right = jnp.concatenate([blk[4], s5], 0).astype(jnp.bfloat16)
    from_right = _pp(to_left, "x", 4, -1).astype(jnp.float32)
    from_left = _pp(to_right, "x", 4, 1).astype(jnp.float32)
    t = jnp.concatenate([blk[0], blk[1]], 0) + from_right + from_left
    z = _pp(t[r:].astype(jnp.bfloat16), "zh", 2, 1).astype(jnp.float32)
    return t[:r] + z


def local(
    queries,
    keys,
    values,
    doc_lengths,
    resid,
    out_weight,
    norm_gain,
    router_weight,
    expert_ids,
    gate_weight,
    up_weight,
    down_weight,
):
    tok_rows = queries.shape[1]
    width = resid.shape[2]
    n_ctx = 16
    n_exp = 16
    my_ctx = lax.axis_index("x") * 4 + lax.axis_index("zh") * 2 + lax.axis_index("core")
    positions = my_ctx * tok_rows + jnp.arange(tok_rows, dtype=jnp.int32)
    bounds = jnp.cumsum(doc_lengths[0])
    query_doc = doc_number(positions, bounds)
    kv_heads = keys.shape[2] // HEAD_SIZE
    kw = keys.shape[2]
    head_groups = queries.shape[2] // keys.shape[2]
    heads_of_query = queries[0].reshape(tok_rows, kv_heads, head_groups, HEAD_SIZE)
    scale = 1.0 / math.sqrt(HEAD_SIZE)
    order = rel_index()
    kv_piece = ag_rel(jnp.concatenate([keys[0], values[0]], axis=1))
    key_piece = kv_piece[:, :kw]
    value_piece = kv_piece[:, kw:]
    count = key_piece.shape[0]
    heads_of_key = key_piece.reshape(count, kv_heads, HEAD_SIZE)
    heads_of_value = value_piece.reshape(count, kv_heads, HEAD_SIZE)
    scores = (
        jnp.einsum(
            "tkgd,nkd->kgtn", heads_of_query, heads_of_key, preferred_element_type=jnp.float32
        )
        * scale
    )
    key_pos = (order[:, None] * tok_rows + jnp.arange(tok_rows, dtype=jnp.int32)[None, :]).reshape(-1)
    visible = (key_pos[None, :] <= positions[:, None]) & (
        doc_number(key_pos, bounds)[None, :] == query_doc[:, None]
    )
    masked = jnp.where(visible, scores, -1e30)
    best = jnp.max(masked, axis=-1)
    weights = jnp.where(visible, jnp.exp(masked - best[..., None]), 0.0)
    total = jnp.sum(weights, axis=-1)
    accum = jnp.einsum(
        "kgtn,nkd->kgtd",
        weights.astype(jnp.bfloat16),
        heads_of_value,
        preferred_element_type=jnp.float32,
    )
    attended = (
        (accum / total[..., None]).transpose(2, 0, 1, 3).reshape(tok_rows, -1).astype(jnp.bfloat16)
    )
    qwidth = attended.shape[1]
    proj_rows = lax.all_gather(out_weight, EXP, axis=0, tiled=True)
    feature_block = lax.all_to_all(
        attended.reshape(tok_rows, n_ctx, qwidth // n_ctx),
        CTX,
        split_axis=1,
        concat_axis=0,
        tiled=True,
    )
    feature_rows = jnp.take(
        feature_block.reshape(n_ctx, tok_rows, -1), order, axis=0
    ).reshape(n_ctx * tok_rows, -1)
    attn_sum = rs_rel(
        jnp.dot(feature_rows, proj_rows, preferred_element_type=jnp.float32).astype(jnp.bfloat16)
    )
    hidden_state = resid[0].astype(jnp.float32) + attn_sum.astype(jnp.bfloat16).astype(jnp.float32)
    mean_square = jnp.mean(hidden_state * hidden_state, axis=-1, keepdims=True)
    normed = hidden_state * lax.rsqrt(mean_square + 1e-05) * norm_gain.astype(jnp.float32)
    normed_b = normed.astype(jnp.bfloat16)
    logits = jnp.dot(normed_b, router_weight, preferred_element_type=jnp.float32)
    n_experts = router_weight.shape[1]
    chosen = expert_ids[0, :, 0]
    picked = chosen[:, None] == jnp.arange(n_experts, dtype=jnp.int32)[None, :]
    score = jax.nn.sigmoid(jnp.sum(jnp.where(picked, logits, 0.0), axis=-1))
    routed = (normed * score[:, None]).astype(jnp.bfloat16)
    capacity = max(2, tok_rows // n_experts + tok_rows // (4 * n_experts))
    lower = jnp.tril(jnp.ones((tok_rows, tok_rows), jnp.float32), -1)
    earlier = jnp.dot(lower, picked.astype(jnp.float32), preferred_element_type=jnp.float32)
    slot_rank = jnp.sum(jnp.where(picked, earlier, 0.0), axis=-1).astype(jnp.int32)
    selector = picked[:, :, None] & (
        slot_rank[:, None, None] == jnp.arange(capacity, dtype=jnp.int32)[None, None, :]
    )
    selector_b = selector.astype(jnp.bfloat16)
    outgoing = jnp.einsum(
        "tes,td->esd", selector_b, routed, preferred_element_type=jnp.float32
    ).astype(jnp.bfloat16)
    arrived = lax.all_to_all(outgoing, EXP, split_axis=0, concat_axis=0, tiled=True)
    arrived_rows = arrived.reshape(-1, width)
    gate_local = gate_weight[0]
    up_local = up_weight[0]
    down_local = down_weight[0]
    piece = ag_rel(arrived_rows)
    gate = jnp.dot(piece, gate_local, preferred_element_type=jnp.float32)
    up = jnp.dot(piece, up_local, preferred_element_type=jnp.float32)
    inner = (jax.nn.silu(gate) * up).astype(jnp.bfloat16)
    summed = rs_rel(
        jnp.dot(inner, down_local, preferred_element_type=jnp.float32).astype(jnp.bfloat16)
    ).astype(jnp.bfloat16)
    expert_out = summed.reshape(n_exp, capacity, width)
    returned = lax.all_to_all(expert_out, EXP, split_axis=0, concat_axis=0, tiled=True)
    combined = jnp.einsum("tes,esd->td", selector_b, returned, preferred_element_type=jnp.float32)
    layer_out = (hidden_state + combined).astype(jnp.bfloat16)
    return layer_out[None]


def solution(mesh):
    fine = Mesh(mesh.devices.reshape(4, 2, 2, 4, 4), CTX + EXP)
    in_specs = (
        P(EXP, CTX, None),
        P(EXP, CTX, None),
        P(EXP, CTX, None),
        P(EXP, None),
        P(EXP, CTX, None),
        P(CTX + EXP, None),
        P(),
        P(),
        P(EXP, CTX, None),
        P(EXP, None, CTX),
        P(EXP, None, CTX),
        P(EXP, CTX, None),
    )
    out_specs = P(EXP, CTX, None)
    return jax.shard_map(local, mesh=fine, in_specs=in_specs, out_specs=out_specs, check_vma=False)
```

time: 813 us -> 569 us (0.70)
  waiting for transfers between devices: 651 us -> 234 us
  starting transfers between devices: 4.34 us -> 62.4 us
  blocking collectives: 73.9 us -> 127 us
  local copies, waits for them, and re-layouts: 19.1 us -> 52.7 us
  other arithmetic: 4.27 us -> 28.7 us
    reduce_scatter x2 -> x0, waiting for transfers between devices: 335 us -> none  [the longest x1 172 us: local(): lax.psum_scatter(jnp.dot(inner, down_local, preferred_element_type=jnp.fl...]
    all_gather x4 -> x1, waiting for transfers between devices: 314 us -> 0.02 us  [local(): proj_rows = lax.all_gather(out_weight, EXP, axis=0, tiled=True)]
    ppermute x0 -> x30, waiting for transfers between devices: none -> 220 us  [_pp(): return lax.ppermute(v, axis, [(i, (i + shift) % n) for i in range(n)])]
    all_to_all x2, blocking collectives: 73.9 us -> 127 us  [the longest x1 70.6 us: local(): lax.all_to_all(expert_out, EXP, split_axis=0, concat_axis=0, tiled=True)]
    ppermute x0 -> x30, starting transfers between devices: none -> 49.5 us  [_pp(): return lax.ppermute(v, axis, [(i, (i + shift) % n) for i in range(n)])]
    another operation x2 -> x5, other arithmetic: 0.83 us -> 19.4 us
    unnamed x17 -> x37, local copies, waits for them, and re-layouts: 4.63 us -> 20.6 us
    all_to_all x1, waiting for transfers between devices: 0.01 us -> 14.6 us  [local(): lax.all_to_all(attended.reshape(tok_rows, n_ctx, qwidth // n_ctx), CTX, s...]
  transfers between devices with their start and end apart: 7 -> 32, of which waited for: 6 -> 20; matrix products, arithmetic and copies ran while one was open for 3% -> 7% of each run, Pallas kernels for 0% -> 0%
where the time goes in v1:
time: 569 us; the launch traced here: 562 us
  waiting for transfers between devices  234 us (41%)
  blocking collectives  127 us (22%)
  starting transfers between devices  62.4 us (11%)
  local copies, waits for them, and re-layouts  52.7 us (9%)
  matrix products  43.1 us (8%)
  other arithmetic  28.7 us (5%)
  between operations  14 us (2%)
    ppermute x30, waiting for transfers between devices, _pp(): return lax.ppermute(v, axis, [(i, (i + shift) % n) for i in range(n)])  220 us
    all_to_all x1, blocking collectives, local(): lax.all_to_all(expert_out, EXP, split_axis=0, concat_axis=0, tiled=True)  70.6 us
    all_to_all x1, blocking collectives, local(): lax.all_to_all(outgoing, EXP, split_axis=0, concat_axis=0, tiled=True)  56.5 us
    ppermute x30, starting transfers between devices, _pp(): return lax.ppermute(v, axis, [(i, (i + shift) % n) for i in range(n)])  49.5 us
    unnamed x37, local copies, waits for them, and re-layouts  20.6 us
    dot_general x1, matrix products, local(): jnp.dot(inner, down_local, preferred_element_type=jnp.float32)  20.4 us
    another operation x5, other arithmetic  19.4 us
    all_to_all x1, waiting for transfers between devices, local(): lax.all_to_all(attended.reshape(tok_rows, n_ctx, qwidth // n_ctx), CTX, s...  14.6 us
  transfers between devices with their start and end apart: 32, of which 20 were waited for; matrix products, arithmetic and copies ran while one was open for 7% of the time, Pallas kernels for 0%

profile of v1, /device:TPU:1, one launch (start us, length us, event | category | flops | bytes accessed | tf_op | source)
XLA Modules:
  0.0 562.3 jit_solution(8994114849716741180)
XLA Ops:
  8.7 7.8 %collective-permute-start = (bf16[64,1024]{0,1:T(8,128)(2,1)S(1)}, bf16[64,1024]{0,1:T(8,128)(2,1)S(1)}, u32[]{:S(2)}, u32[]{:S(2)}) collective-permute-start(bf16[64,1024]{0,1:T(8,128)(2,1)S(1)} %pad_maximum_fusion.5), channel_id=1, source_target_pairs={{0,32},{32,0},{1,33},{33,1},{2,34},{34,2},{3,35},{35,3},{4,36},{36... | collective-permute-start | bytes 393224 | tf_op jit(solution)/shard_map/ppermute | solution.py:19
  19.9 3.1 collective-permute-done
  23.1 2.9 collective-permute-start.4
  26.1 4.2 collective-permute-done.4
  31.0 2.5 collective-permute-done.2
  33.5 3.8 concatenate.81
  37.3 2.5 collective-permute-start.7
  39.9 2.7 collective-permute-start.6
  42.9 6.1 %collective-permute-done.5 = bf16[64,1024]{0,1:T(8,128)(2,1)} collective-permute-done((bf16[64,1024]{0,1:T(8,128)(2,1)S(1)}, bf16[64,1024]{0,1:T(8,128)(2,1)}, u32[]{:S(2)}, u32[]{:S(2)}) %collective-permute-start.5) | collective-permute-done | bytes 131104 | tf_op jit(solution)/shard_map/ppermute | solution.py:19
  54.4 5.6 concatenate.83
  59.9 3.1 fusion.88
  63.0 4.9 fusion.89
  68.0 2.9 fusion.29
  74.5 12.9 %all-to-all-start = ((bf16[64,16,160]{2,0,1:T(8,128)(2,1)}), bf16[64,16,160]{2,0,1:T(8,128)(2,1)S(1)}, u32[]{:S(2)}, u32[]{:S(2)}) async-start(bf16[64,16,160]{2,0,1:T(8,128)(2,1)} %copy.41), calls=%async_computation | async-start | bytes 1048576 | tf_op jit(solution)/shard_map/all_to_all | solution.py:124
  87.7 14.6 %all-to-all-done = bf16[64,16,160]{2,0,1:T(8,128)(2,1)S(1)} async-done(((bf16[64,16,160]{2,0,1:T(8,128)(2,1)}), bf16[64,16,160]{2,0,1:T(8,128)(2,1)S(1)}, u32[]{:S(2)}, u32[]{:S(2)}) %all-to-all-start) | async-done | bytes 327712 | tf_op jit(solution)/shard_map/all_to_all | solution.py:124
  105.0 4.0 reshape.274
  109.0 4.5 convolution_convert_fusion.1
  113.8 3.7 copy-done.1
  118.6 8.4 %collective-permute-done.9 = bf16[512,5120]{1,0:T(8,128)(2,1)} collective-permute-done((bf16[512,5120]{1,0:T(8,128)(2,1)S(1)}, bf16[512,5120]{1,0:T(8,128)(2,1)}, u32[]{:S(2)}, u32[]{:S(2)}) %collective-permute-start.9) | collective-permute-done | bytes 5242912 | tf_op jit(solution)/shard_map/ppermute | solution.py:19
  127.0 11.9 %fusion.82 = (bf16[512,5120]{1,0:T(8,128)(2,1)}, f32[512,5120]{1,0:T(8,128)}) fusion(bf16[512,5120]{1,0:T(8,128)(2,1)} %collective-permute-done.9, bf16[1024,5120]{1,0:T(8,128)(2,1)} %copy-done.1), kind=kLoop, calls=%fused_computation.140 | loop fusion | flops 10485760 | bytes 26214400 | tf_op jit(solution)/shard_map/convert.18
  142.5 14.3 %collective-permute-done.10 = bf16[64,5120]{1,0:T(8,128)(2,1)S(1)} collective-permute-done((bf16[64,5120]{1,0:T(8,128)(2,1)S(1)}, bf16[64,5120]{1,0:T(8,128)(2,1)S(1)}, u32[]{:S(2)}, u32[]{:S(2)}) %collective-permute-start.10) | collective-permute-done | bytes 655392 | tf_op jit(solution)/shard_map/ppermute | solution.py:19
  162.4 27.2 %collective-permute-done.11 = bf16[128,5120]{1,0:T(8,128)(2,1)S(1)} collective-permute-done((bf16[128,5120]{1,0:T(8,128)(2,1)S(1)}, bf16[128,5120]{1,0:T(8,128)(2,1)S(1)}, u32[]{:S(2)}, u32[]{:S(2)}) %collective-permute-start.11) | collective-permute-done | bytes 1310752 | tf_op jit(solution)/shard_map/ppermute | solution.py:19
  191.0 2.2 fusion.6
  193.3 2.8 collective-permute-start.14
  196.4 14.9 %collective-permute-done.14 = bf16[64,5120]{1,0:T(8,128)(2,1)S(1)} collective-permute-done((bf16[64,5120]{1,0:T(8,128)(2,1)S(1)}, bf16[64,5120]{1,0:T(8,128)(2,1)S(1)}, u32[]{:S(2)}, u32[]{:S(2)}) %collective-permute-start.14) | collective-permute-done | bytes 655392 | tf_op jit(solution)/shard_map/ppermute | solution.py:19
  213.2 56.5 %all_to_all.25 = bf16[16,5,5120]{2,1,0:T(8,128)(2,1)} all-to-all(bf16[16,5,5120]{2,1,0:T(8,128)(2,1)S(1)} %copy.42), channel_id=1, replica_groups=mesh['x'=4,'zh'=2,'core'=2,'zl'=4,'y'=4] {'zl','y'}, dimensions={0} | all-to-all | bytes 1638400 | tf_op jit(solution)/shard_map/all_to_all | solution.py:158
  274.9 2.7 collective-permute-start.18
  277.6 16.2 %collective-permute-done.15 = bf16[80,5120]{1,0:T(8,128)(2,1)S(1)} collective-permute-done((bf16[80,5120]{1,0:T(8,128)(2,1)}, bf16[80,5120]{1,0:T(8,128)(2,1)S(1)}, u32[]{:S(2)}, u32[]{:S(2)}) %collective-permute-start.15) | collective-permute-done | bytes 819232 | tf_op jit(solution)/shard_map/ppermute | solution.py:19
  293.8 2.7 collective-permute-start.19
  296.7 14.7 %collective-permute-done.17 = bf16[80,5120]{1,0:T(8,128)(2,1)S(1)} collective-permute-done((bf16[80,5120]{1,0:T(8,128)(2,1)S(1)}, bf16[80,5120]{1,0:T(8,128)(2,1)S(1)}, u32[]{:S(2)}, u32[]{:S(2)}) %collective-permute-start.17) | collective-permute-done | bytes 819232 | tf_op jit(solution)/shard_map/ppermute | solution.py:19
  311.9 4.3 collective-permute-start.22
  316.2 2.7 collective-permute-start.21
  318.8 18.2 %collective-permute-done.20 = bf16[80,5120]{1,0:T(8,128)(2,1)S(1)} collective-permute-done((bf16[80,5120]{1,0:T(8,128)(2,1)S(1)}, bf16[80,5120]{1,0:T(8,128)(2,1)S(1)}, u32[]{:S(2)}, u32[]{:S(2)}) %collective-permute-start.20) | collective-permute-done | bytes 819232 | tf_op jit(solution)/shard_map/ppermute | solution.py:19
  338.8 4.7 copy-done.7
  343.5 2.5 constant_dynamic-update-slice_fusion.7
  348.3 7.7 %fusion.8 = f32[1280,256]{1,0:T(8,128)} fusion(bf16[1280,5120]{1,0:T(8,128)(2,1)} %constant_dynamic-update-slice_fusion.6, bf16[1,5120,256]{2,1,0:T(8,128)(2,1)S(1)} %copy-done.10), kind=kOutput, calls=%fused_computation.19 | convolution fusion | flops 3355443200 | bytes 17039360 | tf_op jit(solution)/shard_map/dot_general | solution.py:165
  356.0 20.4 %convolution_convert_fusion = bf16[1280,5120]{1,0:T(8,128)(2,1)} fusion(bf16[1,256,5120]{2,1,0:T(8,128)(2,1)S(1)} %copy-done, f32[1280,256]{1,0:T(8,128)} %fusion.8, bf16[1280,5120]{1,0:T(8,128)(2,1)} %constant_dynamic-update-slice_fusion.6, bf16[1,5120,256]{2,1,0:T(8,128)(2,1)} %param.23), kind=kOutput, calls=%fused_computation.2 | convolution fusion | flops 6719406080 | bytes 32768000 | tf_op jit(solution)/shard_map/dot_general | solution.py:168
  376.4 3.3 slice.119
  379.8 10.5 %collective-permute-done.24 = bf16[640,5120]{1,0:T(8,128)(2,1)S(1)} collective-permute-done((bf16[640,5120]{1,0:T(8,128)(2,1)S(1)}, bf16[640,5120]{1,0:T(8,128)(2,1)S(1)}, u32[]{:S(2)}, u32[]{:S(2)}) %collective-permute-start.24) | collective-permute-done | bytes 6553632 | tf_op jit(solution)/shard_map/ppermute | solution.py:19
  390.3 4.9 fusion.83
  395.4 2.8 collective-permute-start.25
  398.2 17.5 %collective-permute-done.25 = bf16[80,5120]{1,0:T(8,128)(2,1)S(1)} collective-permute-done((bf16[80,5120]{1,0:T(8,128)(2,1)S(1)}, bf16[80,5120]{1,0:T(8,128)(2,1)S(1)}, u32[]{:S(2)}, u32[]{:S(2)}) %collective-permute-start.25) | collective-permute-done | bytes 819232 | tf_op jit(solution)/shard_map/ppermute | solution.py:19
  415.7 3.1 collective-permute-done.27
  421.2 34.3 %collective-permute-done.26 = bf16[160,5120]{1,0:T(8,128)(2,1)S(1)} collective-permute-done((bf16[160,5120]{1,0:T(8,128)(2,1)S(1)}, bf16[160,5120]{1,0:T(8,128)(2,1)S(1)}, u32[]{:S(2)}, u32[]{:S(2)}) %collective-permute-start.26) | collective-permute-done | bytes 1638432 | tf_op jit(solution)/shard_map/ppermute | solution.py:19
  458.0 2.4 collective-permute-start.29
  460.5 19.3 %collective-permute-done.29 = bf16[80,5120]{1,0:T(8,128)(2,1)S(1)} collective-permute-done((bf16[80,5120]{1,0:T(8,128)(2,1)S(1)}, bf16[80,5120]{1,0:T(8,128)(2,1)S(1)}, u32[]{:S(2)}, u32[]{:S(2)}) %collective-permute-start.29) | collective-permute-done | bytes 819232 | tf_op jit(solution)/shard_map/ppermute | solution.py:19
  480.8 2.3 reshape.263
  483.0 70.6 %all_to_all.26 = bf16[16,5,5120]{2,1,0:T(8,128)(2,1)S(1)} all-to-all(bf16[16,5,5120]{2,1,0:T(8,128)(2,1)} %reshape.263), channel_id=1, replica_groups=mesh['x'=4,'zh'=2,'core'=2,'zl'=4,'y'=4] {'zl','y'}, dimensions={0} | all-to-all | bytes 1638400 | tf_op jit(solution)/shard_map/all_to_all | solution.py:171
  (123 shorter events, 50.5 us)
Async XLA Ops:
  6.5 349.5 %copy-start = (bf16[1,256,5120]{2,1,0:T(8,128)(2,1)S(1)}, bf16[1,256,5120]{2,1,0:T(8,128)(2,1)}, u32[]{:S(2)}) copy-start(bf16[1,256,5120]{2,1,0:T(8,128)(2,1)} %param.25) | copy-start | bytes 7864324
  6.5 36.1 %copy-start.12 = (s32[1,4]{1,0:T(1,128)S(1)}, s32[1,4]{1,0:T(1,128)}, u32[]{:S(2)}) copy-start(s32[1,4]{1,0:T(1,128)} %param.17) | copy-start | bytes 52
  6.5 98.4 %all-gather.3.cloned.1.call-start = ((), (), s32[]{:S(2)}) async-start(), calls=%async_computation.3 | async-start | bytes 2785280 | tf_op jit(solution)/shard_map/all_gather | solution.py:123
  8.7 14.4 %collective-permute-start = (bf16[64,1024]{0,1:T(8,128)(2,1)S(1)}, bf16[64,1024]{0,1:T(8,128)(2,1)S(1)}, u32[]{:S(2)}, u32[]{:S(2)}) collective-permute-start(bf16[64,1024]{0,1:T(8,128)(2,1)S(1)} %pad_maximum_fusion.5), channel_id=1, source_target_pairs={{0,32},{32,0},{1,33},{33,1},{2,34},{34,2},{3,35},{35,3},{4,36},{36... | collective-permute-start | bytes 393224 | tf_op jit(solution)/shard_map/ppermute | solution.py:19
  16.5 9.6 %collective-permute-start.1 = (bf16[64,1024]{0,1:T(8,128)(2,1)S(1)}, bf16[64,1024]{0,1:T(8,128)(2,1)S(1)}, u32[]{:S(2)}, u32[]{:S(2)}) collective-permute-start(bf16[64,1024]{0,1:T(8,128)(2,1)S(1)} %pad_maximum_fusion.5), channel_id=1, source_target_pairs={{0,64},{64,128},{128,192},{192,0},{1,65},{65,129},{129,193},{193,1... | collective-permute-start | bytes 393224 | tf_op jit(solution)/shard_map/ppermute | solution.py:19
  17.7 8.4 %collective-permute-start.3 = (bf16[64,1024]{0,1:T(8,128)(2,1)S(1)}, bf16[64,1024]{0,1:T(8,128)(2,1)}, u32[]{:S(2)}, u32[]{:S(2)}) collective-permute-start(bf16[64,1024]{0,1:T(8,128)(2,1)S(1)} %pad_maximum_fusion.5), channel_id=1, source_target_pairs={{0,192},{64,0},{128,64},{192,128},{1,193},{65,1},{129,65},{193,129... | collective-permute-start | bytes 393224 | tf_op jit(solution)/shard_map/ppermute | solution.py:19
  23.1 7.2 %collective-permute-start.4 = (bf16[64,1024]{0,1:T(8,128)(2,1)S(1)}, bf16[64,1024]{0,1:T(8,128)(2,1)S(1)}, u32[]{:S(2)}, u32[]{:S(2)}) collective-permute-start(bf16[64,1024]{0,1:T(8,128)(2,1)S(1)} %collective-permute-done), channel_id=1, source_target_pairs={{0,192},{64,0},{128,64},{192,128},{1,193},{65,1},{129,65},{193,129... | collective-permute-start | bytes 393224 | tf_op jit(solution)/shard_map/ppermute | solution.py:19
  26.0 7.5 %collective-permute-start.2 = (bf16[64,1024]{0,1:T(8,128)(2,1)S(1)}, bf16[64,1024]{0,1:T(8,128)(2,1)}, u32[]{:S(2)}, u32[]{:S(2)}) collective-permute-start(bf16[64,1024]{0,1:T(8,128)(2,1)S(1)} %collective-permute-done), channel_id=1, source_target_pairs={{0,64},{64,128},{128,192},{192,0},{1,65},{65,129},{129,193},{193,1... | collective-permute-start | bytes 393224 | tf_op jit(solution)/shard_map/ppermute | solution.py:19
  30.3 0.7 copy-start.5
  37.3 17.1 %collective-permute-start.7 = (bf16[384,1024]{0,1:T(8,128)(2,1)}, bf16[384,1024]{0,1:T(8,128)(2,1)}, u32[]{:S(2)}, u32[]{:S(2)}) collective-permute-start(bf16[384,1024]{0,1:T(8,128)(2,1)} %concatenate.81), channel_id=1, source_target_pairs={{0,16},{16,0},{1,17},{17,1},{2,18},{18,2},{3,19},{19,3},{4,20},{20... | collective-permute-start | bytes 2359304 | tf_op jit(solution)/shard_map/ppermute | solution.py:19
  39.9 9.1 %collective-permute-start.5 = (bf16[64,1024]{0,1:T(8,128)(2,1)S(1)}, bf16[64,1024]{0,1:T(8,128)(2,1)}, u32[]{:S(2)}, u32[]{:S(2)}) collective-permute-start(bf16[64,1024]{0,1:T(8,128)(2,1)S(1)} %collective-permute-done.1), channel_id=1, source_target_pairs={{0,64},{64,128},{128,192},{192,0},{1,65},{65,129},{129,193},{193,1... | collective-permute-start | bytes 393224 | tf_op jit(solution)/shard_map/ppermute | solution.py:19
  39.9 9.1 %collective-permute-start.6 = (bf16[64,1024]{0,1:T(8,128)(2,1)}, bf16[64,1024]{0,1:T(8,128)(2,1)}, u32[]{:S(2)}, u32[]{:S(2)}) collective-permute-start(bf16[64,1024]{0,1:T(8,128)(2,1)} %copy-done.5), channel_id=1, source_target_pairs={{0,192},{64,0},{128,64},{192,128},{1,193},{65,1},{129,65},{193,129... | collective-permute-start | bytes 393224 | tf_op jit(solution)/shard_map/ppermute | solution.py:19
  50.9 3.4 collective-permute-start.8
  59.9 3.1 copy-start.6
  74.5 27.8 %all-to-all-start = ((bf16[64,16,160]{2,0,1:T(8,128)(2,1)}), bf16[64,16,160]{2,0,1:T(8,128)(2,1)S(1)}, u32[]{:S(2)}, u32[]{:S(2)}) async-start(bf16[64,16,160]{2,0,1:T(8,128)(2,1)} %copy.41), calls=%async_computation | async-start | bytes 1048576 | tf_op jit(solution)/shard_map/all_to_all | solution.py:124
  113.5 4.0 copy-start.1
  117.5 9.5 %collective-permute-start.9 = (bf16[512,5120]{1,0:T(8,128)(2,1)S(1)}, bf16[512,5120]{1,0:T(8,128)(2,1)}, u32[]{:S(2)}, u32[]{:S(2)}) collective-permute-start(bf16[512,5120]{1,0:T(8,128)(2,1)S(1)} %slice.109), channel_id=1, source_target_pairs={{0,16},{16,0},{1,17},{17,1},{2,18},{18,2},{3,19},{19,3},{4,20},{20... | collective-permute-start | bytes 15728648 | tf_op jit(solution)/shard_map/ppermute | solution.py:19
  140.8 16.0 %collective-permute-start.10 = (bf16[64,5120]{1,0:T(8,128)(2,1)S(1)}, bf16[64,5120]{1,0:T(8,128)(2,1)S(1)}, u32[]{:S(2)}, u32[]{:S(2)}) collective-permute-start(bf16[64,5120]{1,0:T(8,128)(2,1)S(1)} %get-tuple-element.21), channel_id=1, source_target_pairs={{0,192},{64,0},{128,64},{192,128},{1,193},{65,1},{129,65},{193,129... | collective-permute-start | bytes 1966088 | tf_op jit(solution)/shard_map/ppermute | solution.py:19
  141.4 17.0 %collective-permute-start.12 = (bf16[64,5120]{1,0:T(8,128)(2,1)S(1)}, bf16[64,5120]{1,0:T(8,128)(2,1)S(1)}, u32[]{:S(2)}, u32[]{:S(2)}) collective-permute-start(bf16[64,5120]{1,0:T(8,128)(2,1)S(1)} %get-tuple-element.22), channel_id=1, source_target_pairs={{0,64},{64,128},{128,192},{192,0},{1,65},{65,129},{129,193},{193,1... | collective-permute-start | bytes 1966088 | tf_op jit(solution)/shard_map/ppermute | solution.py:19
  160.5 1.8 copy-start.8
  160.6 28.9 %collective-permute-start.11 = (bf16[128,5120]{1,0:T(8,128)(2,1)S(1)}, bf16[128,5120]{1,0:T(8,128)(2,1)S(1)}, u32[]{:S(2)}, u32[]{:S(2)}) collective-permute-start(bf16[128,5120]{1,0:T(8,128)(2,1)S(1)} %pad_maximum_fusion.3), channel_id=1, source_target_pairs={{0,192},{64,0},{128,64},{192,128},{1,193},{65,1},{129,65},{193,129... | collective-permute-start | bytes 3932168 | tf_op jit(solution)/shard_map/ppermute | solution.py:19
  160.9 30.1 %collective-permute-start.13 = (bf16[128,5120]{1,0:T(8,128)(2,1)S(1)}, bf16[128,5120]{1,0:T(8,128)(2,1)S(1)}, u32[]{:S(2)}, u32[]{:S(2)}) collective-permute-start(bf16[128,5120]{1,0:T(8,128)(2,1)S(1)} %pad_maximum_fusion.4), channel_id=1, source_target_pairs={{0,64},{64,128},{128,192},{192,0},{1,65},{65,129},{129,193},{193,1... | collective-permute-start | bytes 3932168 | tf_op jit(solution)/shard_map/ppermute | solution.py:19
  162.3 33.8 %copy-start.9 = (s32[1,64,1]{1,2,0:T(1,128)S(1)}, s32[1,64,1]{1,2,0:T(1,128)}, u32[]{:S(2)}) copy-start(s32[1,64,1]{1,2,0:T(1,128)} %param.22) | copy-start | bytes 772
  162.4 49.0 %copy-start.2 = (bf16[1,64,5120]{2,1,0:T(8,128)(2,1)S(1)}, bf16[1,64,5120]{2,1,0:T(8,128)(2,1)}, u32[]{:S(2)}) copy-start(bf16[1,64,5120]{2,1,0:T(8,128)(2,1)} %param.18) | copy-start | bytes 1966084
  193.3 18.5 %copy-start.11 = (bf16[5120,16]{0,1:T(8,128)(2,1)S(1)}, bf16[5120,16]{0,1:T(8,128)(2,1)}, u32[]{:S(2)}) copy-start(bf16[5120,16]{0,1:T(8,128)(2,1)} %param.21) | copy-start | bytes 491524
  193.3 18.0 %collective-permute-start.14 = (bf16[64,5120]{1,0:T(8,128)(2,1)S(1)}, bf16[64,5120]{1,0:T(8,128)(2,1)S(1)}, u32[]{:S(2)}, u32[]{:S(2)}) collective-permute-start(bf16[64,5120]{1,0:T(8,128)(2,1)S(1)} %slice.155), channel_id=1, source_target_pairs={{0,32},{32,0},{1,33},{33,1},{2,34},{34,2},{3,35},{35,3},{4,36},{36... | collective-permute-start | bytes 1966088 | tf_op jit(solution)/shard_map/ppermute | solution.py:19
  211.8 1.4 copy-start.3
  271.9 21.9 %collective-permute-start.15 = (bf16[80,5120]{1,0:T(8,128)(2,1)}, bf16[80,5120]{1,0:T(8,128)(2,1)S(1)}, u32[]{:S(2)}, u32[]{:S(2)}) collective-permute-start(bf16[80,5120]{1,0:T(8,128)(2,1)} %reshape.262), channel_id=1, source_target_pairs={{0,32},{32,0},{1,33},{33,1},{2,34},{34,2},{3,35},{35,3},{4,36},{36... | collective-permute-start | bytes 2457608 | tf_op jit(solution)/shard_map/ppermute | solution.py:19
  273.5 23.1 %collective-permute-start.16 = (bf16[80,5120]{1,0:T(8,128)(2,1)}, bf16[80,5120]{1,0:T(8,128)(2,1)S(1)}, u32[]{:S(2)}, u32[]{:S(2)}) collective-permute-start(bf16[80,5120]{1,0:T(8,128)(2,1)} %reshape.262), channel_id=1, source_target_pairs={{0,64},{64,128},{128,192},{192,0},{1,65},{65,129},{129,193},{193,1... | collective-permute-start | bytes 2457608 | tf_op jit(solution)/shard_map/ppermute | solution.py:19
  274.9 36.7 %collective-permute-start.18 = (bf16[80,5120]{1,0:T(8,128)(2,1)}, bf16[80,5120]{1,0:T(8,128)(2,1)S(1)}, u32[]{:S(2)}, u32[]{:S(2)}) collective-permute-start(bf16[80,5120]{1,0:T(8,128)(2,1)} %reshape.262), channel_id=1, source_target_pairs={{0,192},{64,0},{128,64},{192,128},{1,193},{65,1},{129,65},{193,129... | collective-permute-start | bytes 2457608 | tf_op jit(solution)/shard_map/ppermute | solution.py:19
  293.8 17.7 %collective-permute-start.17 = (bf16[80,5120]{1,0:T(8,128)(2,1)S(1)}, bf16[80,5120]{1,0:T(8,128)(2,1)S(1)}, u32[]{:S(2)}, u32[]{:S(2)}) collective-permute-start(bf16[80,5120]{1,0:T(8,128)(2,1)S(1)} %collective-permute-done.15), channel_id=1, source_target_pairs={{0,64},{64,128},{128,192},{192,0},{1,65},{65,129},{129,193},{193,1... | collective-permute-start | bytes 2457608 | tf_op jit(solution)/shard_map/ppermute | solution.py:19
  293.8 17.9 %collective-permute-start.19 = (bf16[80,5120]{1,0:T(8,128)(2,1)S(1)}, bf16[80,5120]{1,0:T(8,128)(2,1)S(1)}, u32[]{:S(2)}, u32[]{:S(2)}) collective-permute-start(bf16[80,5120]{1,0:T(8,128)(2,1)S(1)} %collective-permute-done.15), channel_id=1, source_target_pairs={{0,192},{64,0},{128,64},{192,128},{1,193},{65,1},{129,65},{193,129... | collective-permute-start | bytes 2457608 | tf_op jit(solution)/shard_map/ppermute | solution.py:19
  311.9 31.6 %collective-permute-start.22 = (bf16[480,5120]{1,0:T(8,128)(2,1)S(1)}, bf16[480,5120]{1,0:T(8,128)(2,1)S(1)}, u32[]{:S(2)}, u32[]{:S(2)}) collective-permute-start(bf16[480,5120]{1,0:T(8,128)(2,1)S(1)} %get-tuple-element.27), channel_id=1, source_target_pairs={{0,16},{16,0},{1,17},{17,1},{2,18},{18,2},{3,19},{19,3},{4,20},{20... | collective-permute-start | bytes 14745608 | tf_op jit(solution)/shard_map/ppermute | solution.py:19
  316.1 20.9 %collective-permute-start.20 = (bf16[80,5120]{1,0:T(8,128)(2,1)S(1)}, bf16[80,5120]{1,0:T(8,128)(2,1)S(1)}, u32[]{:S(2)}, u32[]{:S(2)}) collective-permute-start(bf16[80,5120]{1,0:T(8,128)(2,1)S(1)} %collective-permute-done.16), channel_id=1, source_target_pairs={{0,64},{64,128},{128,192},{192,0},{1,65},{65,129},{129,193},{193,1... | collective-permute-start | bytes 2457608 | tf_op jit(solution)/shard_map/ppermute | solution.py:19
  316.2 20.9 %collective-permute-start.21 = (bf16[80,5120]{1,0:T(8,128)(2,1)S(1)}, bf16[80,5120]{1,0:T(8,128)(2,1)S(1)}, u32[]{:S(2)}, u32[]{:S(2)}) collective-permute-start(bf16[80,5120]{1,0:T(8,128)(2,1)S(1)} %collective-permute-done.19), channel_id=1, source_target_pairs={{0,192},{64,0},{128,64},{192,128},{1,193},{65,1},{129,65},{193,129... | collective-permute-start | bytes 2457608 | tf_op jit(solution)/shard_map/ppermute | solution.py:19
  337.2 8.8 %collective-permute-start.23 = (bf16[160,5120]{1,0:T(8,128)(2,1)S(1)}, bf16[160,5120]{1,0:T(8,128)(2,1)S(1)}, u32[]{:S(2)}, u32[]{:S(2)}) collective-permute-start(bf16[160,5120]{1,0:T(8,128)(2,1)S(1)} %pad_maximum_fusion), channel_id=1, source_target_pairs={{0,16},{16,0},{1,17},{17,1},{2,18},{18,2},{3,19},{19,3},{4,20},{20... | collective-permute-start | bytes 4915208 | tf_op jit(solution)/shard_map/ppermute | solution.py:19
  338.8 4.7 copy-start.7
  346.0 2.3 copy-start.10
  379.7 10.6 %collective-permute-start.24 = (bf16[640,5120]{1,0:T(8,128)(2,1)S(1)}, bf16[640,5120]{1,0:T(8,128)(2,1)S(1)}, u32[]{:S(2)}, u32[]{:S(2)}) collective-permute-start(bf16[640,5120]{1,0:T(8,128)(2,1)S(1)} %slice.119), channel_id=1, source_target_pairs={{0,16},{16,0},{1,17},{17,1},{2,18},{18,2},{3,19},{19,3},{4,20},{20... | collective-permute-start | bytes 19660808 | tf_op jit(solution)/shard_map/ppermute | solution.py:19
  395.4 20.2 %collective-permute-start.25 = (bf16[80,5120]{1,0:T(8,128)(2,1)S(1)}, bf16[80,5120]{1,0:T(8,128)(2,1)S(1)}, u32[]{:S(2)}, u32[]{:S(2)}) collective-permute-start(bf16[80,5120]{1,0:T(8,128)(2,1)S(1)} %get-tuple-element.17), channel_id=1, source_target_pairs={{0,192},{64,0},{128,64},{192,128},{1,193},{65,1},{129,65},{193,129... | collective-permute-start | bytes 2457608 | tf_op jit(solution)/shard_map/ppermute | solution.py:19
  398.2 20.6 %collective-permute-start.27 = (bf16[80,5120]{1,0:T(8,128)(2,1)S(1)}, bf16[80,5120]{1,0:T(8,128)(2,1)S(1)}, u32[]{:S(2)}, u32[]{:S(2)}) collective-permute-start(bf16[80,5120]{1,0:T(8,128)(2,1)S(1)} %get-tuple-element.18), channel_id=1, source_target_pairs={{0,64},{64,128},{128,192},{192,0},{1,65},{65,129},{129,193},{193,1... | collective-permute-start | bytes 2457608 | tf_op jit(solution)/shard_map/ppermute | solution.py:19
  419.3 36.2 %collective-permute-start.26 = (bf16[160,5120]{1,0:T(8,128)(2,1)S(1)}, bf16[160,5120]{1,0:T(8,128)(2,1)S(1)}, u32[]{:S(2)}, u32[]{:S(2)}) collective-permute-start(bf16[160,5120]{1,0:T(8,128)(2,1)S(1)} %pad_maximum_fusion.1), channel_id=1, source_target_pairs={{0,192},{64,0},{128,64},{192,128},{1,193},{65,1},{129,65},{193,129... | collective-permute-start | bytes 4915208 | tf_op jit(solution)/shard_map/ppermute | solution.py:19
  419.8 37.5 %collective-permute-start.28 = (bf16[160,5120]{1,0:T(8,128)(2,1)S(1)}, bf16[160,5120]{1,0:T(8,128)(2,1)S(1)}, u32[]{:S(2)}, u32[]{:S(2)}) collective-permute-start(bf16[160,5120]{1,0:T(8,128)(2,1)S(1)} %pad_maximum_fusion.2), channel_id=1, source_target_pairs={{0,64},{64,128},{128,192},{192,0},{1,65},{65,129},{129,193},{193,1... | collective-permute-start | bytes 4915208 | tf_op jit(solution)/shard_map/ppermute | solution.py:19
  458.0 21.7 %collective-permute-start.29 = (bf16[80,5120]{1,0:T(8,128)(2,1)S(1)}, bf16[80,5120]{1,0:T(8,128)(2,1)S(1)}, u32[]{:S(2)}, u32[]{:S(2)}) collective-permute-start(bf16[80,5120]{1,0:T(8,128)(2,1)S(1)} %slice.154), channel_id=1, source_target_pairs={{0,32},{32,0},{1,33},{33,1},{2,34},{34,2},{3,35},{35,3},{4,36},{36... | collective-permute-start | bytes 2457608 | tf_op jit(solution)/shard_map/ppermute | solution.py:19
  483.0 70.6 %copy-start.4 = (bf16[64,5120]{1,0:T(8,128)(2,1)S(1)}, bf16[64,5120]{1,0:T(8,128)(2,1)}, u32[]{:S(2)}) copy-start(bf16[64,5120]{1,0:T(8,128)(2,1)} %copy-done.3) | copy-start | bytes 1966084
Sparse Core Ops, SparseCore 0:
  19.3 71.4 all-gather.2

commit v2 on v1

--- a/solution.py
+++ b/solution.py
@@ -60,6 +60,22 @@
     t = jnp.concatenate([blk[0], blk[1]], 0) + from_right + from_left
     z = _pp(t[r:].astype(jnp.bfloat16), "zh", 2, 1).astype(jnp.float32)
     return t[:r] + z
+
+
+def a2a_send(out_rel):
+    g = out_rel.reshape(4, 4, *out_rel.shape[1:])
+    cols = [g[:, 0]] + [_pp(g[:, dy], "y", 4, dy) for dy in range(1, 4)]
+    m = jnp.stack(cols, 1)
+    rows = [m[0]] + [_pp(m[dz], "zl", 4, dz) for dz in range(1, 4)]
+    return jnp.stack(rows, 0).reshape(out_rel.shape)
+
+
+def a2a_back(res_rel):
+    g = res_rel.reshape(4, 4, *res_rel.shape[1:])
+    rows = [g[0]] + [_pp(g[dz], "zl", 4, -dz) for dz in range(1, 4)]
+    n = jnp.stack(rows, 0)
+    cols = [n[:, 0]] + [_pp(n[:, dy], "y", 4, -dy) for dy in range(1, 4)]
+    return jnp.stack(cols, 1).reshape(res_rel.shape)
 
 
 def local(
@@ -141,8 +157,10 @@
     logits = jnp.dot(normed_b, router_weight, preferred_element_type=jnp.float32)
     n_experts = router_weight.shape[1]
     chosen = expert_ids[0, :, 0]
-    picked = chosen[:, None] == jnp.arange(n_experts, dtype=jnp.int32)[None, :]
-    score = jax.nn.sigmoid(jnp.sum(jnp.where(picked, logits, 0.0), axis=-1))
+    shift = jnp.arange(n_experts, dtype=jnp.int32)
+    expert_of_shift = ((lax.axis_index("zl") + shift // 4) % 4) * 4 + (lax.axis_index("y") + shift % 4) % 4
+    picked = chosen[:, None] == expert_of_shift[None, :]
+    score = jax.nn.sigmoid(jnp.sum(jnp.where(picked, logits[:, expert_of_shift], 0.0), axis=-1))
     routed = (normed * score[:, None]).astype(jnp.bfloat16)
     capacity = max(2, tok_rows // n_experts + tok_rows // (4 * n_experts))
     lower = jnp.tril(jnp.ones((tok_rows, tok_rows), jnp.float32), -1)
@@ -155,7 +173,7 @@
     outgoing = jnp.einsum(
         "tes,td->esd", selector_b, routed, preferred_element_type=jnp.float32
     ).astype(jnp.bfloat16)
-    arrived = lax.all_to_all(outgoing, EXP, split_axis=0, concat_axis=0, tiled=True)
+    arrived = a2a_send(outgoing)
     arrived_rows = arrived.reshape(-1, width)
     gate_local = gate_weight[0]
     up_local = up_weight[0]
@@ -168,7 +186,7 @@
         jnp.dot(inner, down_local, preferred_element_type=jnp.float32).astype(jnp.bfloat16)
     ).astype(jnp.bfloat16)
     expert_out = summed.reshape(n_exp, capacity, width)
-    returned = lax.all_to_all(expert_out, EXP, split_axis=0, concat_axis=0, tiled=True)
+    returned = a2a_back(expert_out)
     combined = jnp.einsum("tes,esd->td", selector_b, returned, preferred_element_type=jnp.float32)
     layer_out = (hidden_state + combined).astype(jnp.bfloat16)
     return layer_out[None]

time: 569 us -> 596 us (1.047)
  blocking collectives: 127 us -> 0 us
  starting transfers between devices: 62.4 us -> 134 us
  waiting for transfers between devices: 234 us -> 295 us
  local copies, waits for them, and re-layouts: 52.7 us -> 65.4 us
  other arithmetic: 28.7 us -> 35.3 us
    all_to_all x2 -> x0, blocking collectives: 127 us -> none  [the longest x1 70.6 us: local(): lax.all_to_all(expert_out, EXP, split_axis=0, concat_axis=0, tiled=True)]
    ppermute x30 -> x42, starting transfers between devices: 49.5 us -> 121 us  [_pp(): return lax.ppermute(v, axis, [(i, (i + shift) % n) for i in range(n)])]
    ppermute x30 -> x42, waiting for transfers between devices: 220 us -> 280 us  [_pp(): return lax.ppermute(v, axis, [(i, (i + shift) % n) for i in range(n)])]
    another operation x5 -> x9, other arithmetic: 19.4 us -> 23.8 us
    unnamed x37 -> x42, local copies, waits for them, and re-layouts: 20.6 us -> 20.6 us
  transfers between devices with their start and end apart: 32 -> 44, of which waited for: 20 -> 28; matrix products, arithmetic and copies ran while one was open for 7% -> 7% of each run, Pallas kernels for 0% -> 0%
where the time goes in v2:
time: 596 us; the launch traced here: 590 us
  waiting for transfers between devices  295 us (49%)
  starting transfers between devices  134 us (22%)
  local copies, waits for them, and re-layouts  65.4 us (11%)
  matrix products  46.1 us (8%)
  other arithmetic  35.3 us (6%)
  between operations  14.4 us (2%)
    ppermute x42, waiting for transfers between devices, _pp(): return lax.ppermute(v, axis, [(i, (i + shift) % n) for i in range(n)])  280 us
    ppermute x42, starting transfers between devices, _pp(): return lax.ppermute(v, axis, [(i, (i + shift) % n) for i in range(n)])  121 us
    unnamed x42, local copies, waits for them, and re-layouts  20.6 us
    dot_general x1, matrix products, local(): jnp.dot(inner, down_local, preferred_element_type=jnp.float32)  20.5 us
    another operation x5, other arithmetic  19.4 us
    all_to_all x1, waiting for transfers between devices, local(): lax.all_to_all(attended.reshape(tok_rows, n_ctx, qwidth // n_ctx), CTX, s...  14.7 us
    all_to_all x1, starting transfers between devices, local(): lax.all_to_all(attended.reshape(tok_rows, n_ctx, qwidth // n_ctx), CTX, s...  12.9 us
  transfers between devices with their start and end apart: 44, of which 28 were waited for; matrix products, arithmetic and copies ran while one was open for 7% of the time, Pallas kernels for 0%

profile of v2, /device:TPU:1, one launch (start us, length us, event | category | flops | bytes accessed | tf_op | source)
XLA Modules:
  0.0 589.9 jit_solution(824425921193542151)
XLA Ops:
  8.7 7.8 %collective-permute-start = (bf16[64,1024]{0,1:T(8,128)(2,1)S(1)}, bf16[64,1024]{0,1:T(8,128)(2,1)S(1)}, u32[]{:S(2)}, u32[]{:S(2)}) collective-permute-start(bf16[64,1024]{0,1:T(8,128)(2,1)S(1)} %pad_maximum_fusion.9), channel_id=1, source_target_pairs={{0,32},{32,0},{1,33},{33,1},{2,34},{34,2},{3,35},{35,3},{4,36},{36... | collective-permute-start | bytes 393224 | tf_op jit(solution)/shard_map/ppermute | solution.py:19
  19.9 3.1 collective-permute-done
  23.1 2.9 collective-permute-start.4
  26.1 4.2 collective-permute-done.4
  33.5 3.8 concatenate.81
  42.9 6.1 %collective-permute-done.5 = bf16[64,1024]{0,1:T(8,128)(2,1)} collective-permute-done((bf16[64,1024]{0,1:T(8,128)(2,1)S(1)}, bf16[64,1024]{0,1:T(8,128)(2,1)}, u32[]{:S(2)}, u32[]{:S(2)}) %collective-permute-start.5) | collective-permute-done | bytes 131104 | tf_op jit(solution)/shard_map/ppermute | solution.py:19
  54.4 5.6 concatenate.83
  60.0 3.1 fusion.100
  63.1 4.9 fusion.104
  68.0 2.9 fusion.29
  74.5 12.9 %all-to-all-start = ((bf16[64,16,160]{2,0,1:T(8,128)(2,1)}), bf16[64,16,160]{2,0,1:T(8,128)(2,1)S(1)}, u32[]{:S(2)}, u32[]{:S(2)}) async-start(bf16[64,16,160]{2,0,1:T(8,128)(2,1)} %copy.137), calls=%async_computation | async-start | bytes 1048576 | tf_op jit(solution)/shard_map/all_to_all | solution.py:140
  87.7 14.7 %all-to-all-done = bf16[64,16,160]{2,0,1:T(8,128)(2,1)S(1)} async-done(((bf16[64,16,160]{2,0,1:T(8,128)(2,1)}), bf16[64,16,160]{2,0,1:T(8,128)(2,1)S(1)}, u32[]{:S(2)}, u32[]{:S(2)}) %all-to-all-start) | async-done | bytes 327712 | tf_op jit(solution)/shard_map/all_to_all | solution.py:140
  105.1 4.1 reshape.478
  109.2 4.5 convolution_convert_fusion.1
  114.0 3.5 copy-done.1
  118.5 8.4 %collective-permute-done.9 = bf16[512,5120]{1,0:T(8,128)(2,1)} collective-permute-done((bf16[512,5120]{1,0:T(8,128)(2,1)S(1)}, bf16[512,5120]{1,0:T(8,128)(2,1)}, u32[]{:S(2)}, u32[]{:S(2)}) %collective-permute-start.9) | collective-permute-done | bytes 5242912 | tf_op jit(solution)/shard_map/ppermute | solution.py:19
  127.0 11.8 %fusion.94 = (bf16[512,5120]{1,0:T(8,128)(2,1)}, f32[512,5120]{1,0:T(8,128)}) fusion(bf16[512,5120]{1,0:T(8,128)(2,1)} %collective-permute-done.9, bf16[1024,5120]{1,0:T(8,128)(2,1)} %copy-done.1), kind=kLoop, calls=%fused_computation.191 | loop fusion | flops 10485760 | bytes 26214400 | tf_op jit(solution)/shard_map/convert.18
  142.6 14.1 %collective-permute-done.10 = bf16[64,5120]{1,0:T(8,128)(2,1)S(1)} collective-permute-done((bf16[64,5120]{1,0:T(8,128)(2,1)S(1)}, bf16[64,5120]{1,0:T(8,128)(2,1)S(1)}, u32[]{:S(2)}, u32[]{:S(2)}) %collective-permute-start.10) | collective-permute-done | bytes 655392 | tf_op jit(solution)/shard_map/ppermute | solution.py:19
  164.7 26.2 %collective-permute-done.11 = bf16[128,5120]{1,0:T(8,128)(2,1)} collective-permute-done((bf16[128,5120]{1,0:T(8,128)(2,1)}, bf16[128,5120]{1,0:T(8,128)(2,1)}, u32[]{:S(2)}, u32[]{:S(2)}) %collective-permute-start.11) | collective-permute-done | bytes 1310752 | tf_op jit(solution)/shard_map/ppermute | solution.py:19
  193.3 3.0 fusion.6
  198.9 15.5 %collective-permute-done.14 = bf16[64,5120]{1,0:T(8,128)(2,1)S(1)} collective-permute-done((bf16[64,5120]{1,0:T(8,128)(2,1)S(1)}, bf16[64,5120]{1,0:T(8,128)(2,1)S(1)}, u32[]{:S(2)}, u32[]{:S(2)}) %collective-permute-start.14) | collective-permute-done | bytes 655392 | tf_op jit(solution)/shard_map/ppermute | solution.py:19
  222.7 4.1 collective-permute-start.15
  226.9 7.8 %collective-permute-start.16 = (bf16[4,5,5120]{2,0,1:T(4,128)(2,1)S(1)}, bf16[4,5,5120]{2,0,1:T(4,128)(2,1)S(1)}, u32[]{:S(2)}, u32[]{:S(2)}) collective-permute-start(bf16[4,5,5120]{2,0,1:T(4,128)(2,1)S(1)} %bitcast.157), channel_id=1, source_target_pairs={{0,2},{1,3},{2,0},{3,1},{4,6},{5,7},{6,4},{7,5},{8,10},{9,11},{10,... | collective-permute-start | bytes 614408 | tf_op jit(solution)/shard_map/ppermute | solution.py:19
  236.4 3.4 collective-permute-done.16
  241.8 16.5 %collective-permute-start.18 = (bf16[4,5,5120]{2,0,1:T(4,128)(2,1)S(1)}, bf16[4,5,5120]{2,0,1:T(4,128)(2,1)S(1)}, u32[]{:S(2)}, u32[]{:S(2)}) collective-permute-start(bf16[4,5,5120]{2,0,1:T(4,128)(2,1)S(1)} %bitcast.158), channel_id=1, source_target_pairs={{0,4},{4,8},{8,12},{12,0},{1,5},{5,9},{9,13},{13,1},{2,6},{6,10},{... | collective-permute-start | bytes 614408 | tf_op jit(solution)/shard_map/ppermute | solution.py:19
  261.4 11.6 %collective-permute-done.19 = bf16[4,5,5120]{2,0,1:T(4,128)(2,1)S(1)} collective-permute-done((bf16[4,5,5120]{2,0,1:T(4,128)(2,1)S(1)}, bf16[4,5,5120]{2,0,1:T(4,128)(2,1)S(1)}, u32[]{:S(2)}, u32[]{:S(2)}) %collective-permute-start.19) | collective-permute-done | bytes 204832 | tf_op jit(solution)/shard_map/ppermute | solution.py:19
  278.7 2.7 collective-permute-start.24
  281.4 20.4 %collective-permute-done.21 = bf16[80,5120]{1,0:T(8,128)(2,1)S(1)} collective-permute-done((bf16[80,5120]{1,0:T(8,128)(2,1)S(1)}, bf16[80,5120]{1,0:T(8,128)(2,1)S(1)}, u32[]{:S(2)}, u32[]{:S(2)}) %collective-permute-start.21) | collective-permute-done | bytes 819232 | tf_op jit(solution)/shard_map/ppermute | solution.py:19
  304.7 9.8 %collective-permute-done.23 = bf16[80,5120]{1,0:T(8,128)(2,1)S(1)} collective-permute-done((bf16[80,5120]{1,0:T(8,128)(2,1)S(1)}, bf16[80,5120]{1,0:T(8,128)(2,1)S(1)}, u32[]{:S(2)}, u32[]{:S(2)}) %collective-permute-start.23) | collective-permute-done | bytes 819232 | tf_op jit(solution)/shard_map/ppermute | solution.py:19
  314.9 19.8 %collective-permute-start.28 = (bf16[480,5120]{1,0:T(8,128)(2,1)S(1)}, bf16[480,5120]{1,0:T(8,128)(2,1)S(1)}, u32[]{:S(2)}, u32[]{:S(2)}) collective-permute-start(bf16[480,5120]{1,0:T(8,128)(2,1)S(1)} %get-tuple-element.35), channel_id=1, source_target_pairs={{0,16},{16,0},{1,17},{17,1},{2,18},{18,2},{3,19},{19,3},{4,20},{20... | collective-permute-start | bytes 14745608 | tf_op jit(solution)/shard_map/ppermute | solution.py:19
  337.4 18.3 %collective-permute-done.26 = bf16[80,5120]{1,0:T(8,128)(2,1)S(1)} collective-permute-done((bf16[80,5120]{1,0:T(8,128)(2,1)S(1)}, bf16[80,5120]{1,0:T(8,128)(2,1)S(1)}, u32[]{:S(2)}, u32[]{:S(2)}) %collective-permute-start.26) | collective-permute-done | bytes 819232 | tf_op jit(solution)/shard_map/ppermute | solution.py:19
  357.1 4.7 copy-done.7
  366.7 7.7 %fusion.8 = f32[1280,256]{1,0:T(8,128)} fusion(bf16[1280,5120]{1,0:T(8,128)(2,1)} %constant_dynamic-update-slice_fusion.6, bf16[1,5120,256]{2,1,0:T(8,128)(2,1)S(1)} %copy-done.10), kind=kOutput, calls=%fused_computation.20 | convolution fusion | flops 3355443200 | bytes 17039360 | tf_op jit(solution)/shard_map/dot_general | solution.py:183
  374.4 20.5 %convolution_convert_fusion = bf16[1280,5120]{1,0:T(8,128)(2,1)} fusion(bf16[1,256,5120]{2,1,0:T(8,128)(2,1)S(1)} %copy-done, f32[1280,256]{1,0:T(8,128)} %fusion.8, bf16[1280,5120]{1,0:T(8,128)(2,1)} %constant_dynamic-update-slice_fusion.6, bf16[1,5120,256]{2,1,0:T(8,128)(2,1)} %param.23), kind=kOutput, calls=%fused_computation.3 | convolution fusion | flops 6719406080 | bytes 32768000 | tf_op jit(solution)/shard_map/dot_general | solution.py:186
  394.8 3.3 slice.200
  398.2 10.5 %collective-permute-done.30 = bf16[640,5120]{1,0:T(8,128)(2,1)S(1)} collective-permute-done((bf16[640,5120]{1,0:T(8,128)(2,1)S(1)}, bf16[640,5120]{1,0:T(8,128)(2,1)S(1)}, u32[]{:S(2)}, u32[]{:S(2)}) %collective-permute-start.30) | collective-permute-done | bytes 6553632 | tf_op jit(solution)/shard_map/ppermute | solution.py:19
  408.7 4.9 fusion.95
  413.8 2.8 collective-permute-start.31
  416.6 17.5 %collective-permute-done.31 = bf16[80,5120]{1,0:T(8,128)(2,1)S(1)} collective-permute-done((bf16[80,5120]{1,0:T(8,128)(2,1)S(1)}, bf16[80,5120]{1,0:T(8,128)(2,1)S(1)}, u32[]{:S(2)}, u32[]{:S(2)}) %collective-permute-start.31) | collective-permute-done | bytes 819232 | tf_op jit(solution)/shard_map/ppermute | solution.py:19
  434.1 3.1 collective-permute-done.33
  439.7 34.2 %collective-permute-done.32 = bf16[160,5120]{1,0:T(8,128)(2,1)S(1)} collective-permute-done((bf16[160,5120]{1,0:T(8,128)(2,1)S(1)}, bf16[160,5120]{1,0:T(8,128)(2,1)S(1)}, u32[]{:S(2)}, u32[]{:S(2)}) %collective-permute-start.32) | collective-permute-done | bytes 1638432 | tf_op jit(solution)/shard_map/ppermute | solution.py:19
  476.6 21.7 %collective-permute-done.35 = bf16[80,5120]{1,0:T(8,128)(2,1)S(1)} collective-permute-done((bf16[80,5120]{1,0:T(8,128)(2,1)S(1)}, bf16[80,5120]{1,0:T(8,128)(2,1)S(1)}, u32[]{:S(2)}, u32[]{:S(2)}) %collective-permute-start.35) | collective-permute-done | bytes 819232 | tf_op jit(solution)/shard_map/ppermute | solution.py:19
  501.1 5.3 collective-permute-start.36
  507.2 20.9 %collective-permute-start.37 = (bf16[4,5,5120]{2,1,0:T(8,128)(2,1)}, bf16[4,5,5120]{2,1,0:T(8,128)(2,1)S(1)}, u32[]{:S(2)}, u32[]{:S(2)}) collective-permute-start(bf16[4,5,5120]{2,1,0:T(8,128)(2,1)} %squeeze.65), channel_id=1, source_target_pairs={{0,8},{4,12},{8,0},{12,4},{1,9},{5,13},{9,1},{13,5},{2,10},{6,14},... | collective-permute-start | bytes 614408 | tf_op jit(solution)/shard_map/ppermute | solution.py:19
  529.0 5.0 collective-permute-done.36
  534.0 21.9 %collective-permute-done.37 = bf16[4,5,5120]{2,1,0:T(8,128)(2,1)S(1)} collective-permute-done((bf16[4,5,5120]{2,1,0:T(8,128)(2,1)}, bf16[4,5,5120]{2,1,0:T(8,128)(2,1)S(1)}, u32[]{:S(2)}, u32[]{:S(2)}) %collective-permute-start.37) | collective-permute-done | bytes 204832 | tf_op jit(solution)/shard_map/ppermute | solution.py:19
  560.8 4.7 collective-permute-done.39
  567.1 8.7 %collective-permute-done.41 = bf16[4,5,5120]{2,1,0:T(8,128)(2,1)S(1)} collective-permute-done((bf16[4,5,5120]{2,1,0:T(8,128)(2,1)S(1)}, bf16[4,5,5120]{2,1,0:T(8,128)(2,1)S(1)}, u32[]{:S(2)}, u32[]{:S(2)}) %collective-permute-start.41) | collective-permute-done | bytes 204832 | tf_op jit(solution)/shard_map/ppermute | solution.py:19
  (174 shorter events, 101.1 us)
Async XLA Ops:
  6.5 367.8 %copy-start = (bf16[1,256,5120]{2,1,0:T(8,128)(2,1)S(1)}, bf16[1,256,5120]{2,1,0:T(8,128)(2,1)}, u32[]{:S(2)}) copy-start(bf16[1,256,5120]{2,1,0:T(8,128)(2,1)} %param.25) | copy-start | bytes 7864324
  6.5 36.1 %copy-start.12 = (s32[1,4]{1,0:T(1,128)S(1)}, s32[1,4]{1,0:T(1,128)}, u32[]{:S(2)}) copy-start(s32[1,4]{1,0:T(1,128)} %param.17) | copy-start | bytes 52
  6.5 98.5 %all-gather.3.cloned.1.call-start = ((), (), s32[]{:S(2)}) async-start(), calls=%async_computation.1 | async-start | bytes 2785280 | tf_op jit(solution)/shard_map/all_gather | solution.py:139
  8.7 14.4 %collective-permute-start = (bf16[64,1024]{0,1:T(8,128)(2,1)S(1)}, bf16[64,1024]{0,1:T(8,128)(2,1)S(1)}, u32[]{:S(2)}, u32[]{:S(2)}) collective-permute-start(bf16[64,1024]{0,1:T(8,128)(2,1)S(1)} %pad_maximum_fusion.9), channel_id=1, source_target_pairs={{0,32},{32,0},{1,33},{33,1},{2,34},{34,2},{3,35},{35,3},{4,36},{36... | collective-permute-start | bytes 393224 | tf_op jit(solution)/shard_map/ppermute | solution.py:19
  16.5 9.6 %collective-permute-start.1 = (bf16[64,1024]{0,1:T(8,128)(2,1)S(1)}, bf16[64,1024]{0,1:T(8,128)(2,1)S(1)}, u32[]{:S(2)}, u32[]{:S(2)}) collective-permute-start(bf16[64,1024]{0,1:T(8,128)(2,1)S(1)} %pad_maximum_fusion.9), channel_id=1, source_target_pairs={{0,64},{64,128},{128,192},{192,0},{1,65},{65,129},{129,193},{193,1... | collective-permute-start | bytes 393224 | tf_op jit(solution)/shard_map/ppermute | solution.py:19
  17.7 8.4 %collective-permute-start.3 = (bf16[64,1024]{0,1:T(8,128)(2,1)S(1)}, bf16[64,1024]{0,1:T(8,128)(2,1)}, u32[]{:S(2)}, u32[]{:S(2)}) collective-permute-start(bf16[64,1024]{0,1:T(8,128)(2,1)S(1)} %pad_maximum_fusion.9), channel_id=1, source_target_pairs={{0,192},{64,0},{128,64},{192,128},{1,193},{65,1},{129,65},{193,129... | collective-permute-start | bytes 393224 | tf_op jit(solution)/shard_map/ppermute | solution.py:19
  23.1 7.2 %collective-permute-start.4 = (bf16[64,1024]{0,1:T(8,128)(2,1)S(1)}, bf16[64,1024]{0,1:T(8,128)(2,1)S(1)}, u32[]{:S(2)}, u32[]{:S(2)}) collective-permute-start(bf16[64,1024]{0,1:T(8,128)(2,1)S(1)} %collective-permute-done), channel_id=1, source_target_pairs={{0,192},{64,0},{128,64},{192,128},{1,193},{65,1},{129,65},{193,129... | collective-permute-start | bytes 393224 | tf_op jit(solution)/shard_map/ppermute | solution.py:19
  26.0 7.5 %collective-permute-start.2 = (bf16[64,1024]{0,1:T(8,128)(2,1)S(1)}, bf16[64,1024]{0,1:T(8,128)(2,1)}, u32[]{:S(2)}, u32[]{:S(2)}) collective-permute-start(bf16[64,1024]{0,1:T(8,128)(2,1)S(1)} %collective-permute-done), channel_id=1, source_target_pairs={{0,64},{64,128},{128,192},{192,0},{1,65},{65,129},{129,193},{193,1... | collective-permute-start | bytes 393224 | tf_op jit(solution)/shard_map/ppermute | solution.py:19
  37.3 17.1 %collective-permute-start.7 = (bf16[384,1024]{0,1:T(8,128)(2,1)}, bf16[384,1024]{0,1:T(8,128)(2,1)}, u32[]{:S(2)}, u32[]{:S(2)}) collective-permute-start(bf16[384,1024]{0,1:T(8,128)(2,1)} %concatenate.81), channel_id=1, source_target_pairs={{0,16},{16,0},{1,17},{17,1},{2,18},{18,2},{3,19},{19,3},{4,20},{20... | collective-permute-start | bytes 2359304 | tf_op jit(solution)/shard_map/ppermute | solution.py:19
  39.9 9.1 %collective-permute-start.5 = (bf16[64,1024]{0,1:T(8,128)(2,1)S(1)}, bf16[64,1024]{0,1:T(8,128)(2,1)}, u32[]{:S(2)}, u32[]{:S(2)}) collective-permute-start(bf16[64,1024]{0,1:T(8,128)(2,1)S(1)} %collective-permute-done.1), channel_id=1, source_target_pairs={{0,64},{64,128},{128,192},{192,0},{1,65},{65,129},{129,193},{193,1... | collective-permute-start | bytes 393224 | tf_op jit(solution)/shard_map/ppermute | solution.py:19
  39.9 9.1 %collective-permute-start.6 = (bf16[64,1024]{0,1:T(8,128)(2,1)}, bf16[64,1024]{0,1:T(8,128)(2,1)}, u32[]{:S(2)}, u32[]{:S(2)}) collective-permute-start(bf16[64,1024]{0,1:T(8,128)(2,1)} %copy-done.5), channel_id=1, source_target_pairs={{0,192},{64,0},{128,64},{192,128},{1,193},{65,1},{129,65},{193,129... | collective-permute-start | bytes 393224 | tf_op jit(solution)/shard_map/ppermute | solution.py:19
  50.9 3.5 collective-permute-start.8
  74.5 27.9 %all-to-all-start = ((bf16[64,16,160]{2,0,1:T(8,128)(2,1)}), bf16[64,16,160]{2,0,1:T(8,128)(2,1)S(1)}, u32[]{:S(2)}, u32[]{:S(2)}) async-start(bf16[64,16,160]{2,0,1:T(8,128)(2,1)} %copy.137), calls=%async_computation | async-start | bytes 1048576 | tf_op jit(solution)/shard_map/all_to_all | solution.py:140
  117.5 9.5 %collective-permute-start.9 = (bf16[512,5120]{1,0:T(8,128)(2,1)S(1)}, bf16[512,5120]{1,0:T(8,128)(2,1)}, u32[]{:S(2)}, u32[]{:S(2)}) collective-permute-start(bf16[512,5120]{1,0:T(8,128)(2,1)S(1)} %slice.182), channel_id=1, source_target_pairs={{0,16},{16,0},{1,17},{17,1},{2,18},{18,2},{3,19},{19,3},{4,20},{20... | collective-permute-start | bytes 15728648 | tf_op jit(solution)/shard_map/ppermute | solution.py:19
  140.7 16.0 %collective-permute-start.10 = (bf16[64,5120]{1,0:T(8,128)(2,1)S(1)}, bf16[64,5120]{1,0:T(8,128)(2,1)S(1)}, u32[]{:S(2)}, u32[]{:S(2)}) collective-permute-start(bf16[64,5120]{1,0:T(8,128)(2,1)S(1)} %get-tuple-element.21), channel_id=1, source_target_pairs={{0,192},{64,0},{128,64},{192,128},{1,193},{65,1},{129,65},{193,129... | collective-permute-start | bytes 1966088 | tf_op jit(solution)/shard_map/ppermute | solution.py:19
  141.3 17.2 %collective-permute-start.12 = (bf16[64,5120]{1,0:T(8,128)(2,1)S(1)}, bf16[64,5120]{1,0:T(8,128)(2,1)S(1)}, u32[]{:S(2)}, u32[]{:S(2)}) collective-permute-start(bf16[64,5120]{1,0:T(8,128)(2,1)S(1)} %get-tuple-element.22), channel_id=1, source_target_pairs={{0,64},{64,128},{128,192},{192,0},{1,65},{65,129},{129,193},{193,1... | collective-permute-start | bytes 1966088 | tf_op jit(solution)/shard_map/ppermute | solution.py:19
  161.8 29.1 %collective-permute-start.11 = (bf16[128,5120]{1,0:T(8,128)(2,1)}, bf16[128,5120]{1,0:T(8,128)(2,1)}, u32[]{:S(2)}, u32[]{:S(2)}) collective-permute-start(bf16[128,5120]{1,0:T(8,128)(2,1)} %pad_maximum_fusion.3), channel_id=1, source_target_pairs={{0,192},{64,0},{128,64},{192,128},{1,193},{65,1},{129,65},{193,129... | collective-permute-start | bytes 3932168 | tf_op jit(solution)/shard_map/ppermute | solution.py:19
  163.0 30.3 %collective-permute-start.13 = (bf16[128,5120]{1,0:T(8,128)(2,1)}, bf16[128,5120]{1,0:T(8,128)(2,1)}, u32[]{:S(2)}, u32[]{:S(2)}) collective-permute-start(bf16[128,5120]{1,0:T(8,128)(2,1)} %pad_maximum_fusion.4), channel_id=1, source_target_pairs={{0,64},{64,128},{128,192},{192,0},{1,65},{65,129},{129,193},{193,1... | collective-permute-start | bytes 3932168 | tf_op jit(solution)/shard_map/ppermute | solution.py:19
  164.7 49.7 %copy-start.2 = (bf16[1,64,5120]{2,1,0:T(8,128)(2,1)S(1)}, bf16[1,64,5120]{2,1,0:T(8,128)(2,1)}, u32[]{:S(2)}) copy-start(bf16[1,64,5120]{2,1,0:T(8,128)(2,1)} %param.18) | copy-start | bytes 1966084
  196.3 19.4 %copy-start.11 = (bf16[5120,16]{0,1:T(8,128)(2,1)S(1)}, bf16[5120,16]{0,1:T(8,128)(2,1)}, u32[]{:S(2)}) copy-start(bf16[5120,16]{0,1:T(8,128)(2,1)} %param.21) | copy-start | bytes 491524
  196.4 18.0 %collective-permute-start.14 = (bf16[64,5120]{1,0:T(8,128)(2,1)S(1)}, bf16[64,5120]{1,0:T(8,128)(2,1)S(1)}, u32[]{:S(2)}, u32[]{:S(2)}) collective-permute-start(bf16[64,5120]{1,0:T(8,128)(2,1)S(1)} %slice.248), channel_id=1, source_target_pairs={{0,32},{32,0},{1,33},{33,1},{2,34},{34,2},{3,35},{35,3},{4,36},{36... | collective-permute-start | bytes 1966088 | tf_op jit(solution)/shard_map/ppermute | solution.py:19
  222.7 13.7 %collective-permute-start.15 = (bf16[4,5,5120]{2,0,1:T(4,128)(2,1)S(1)}, bf16[4,5,5120]{2,0,1:T(4,128)(2,1)S(1)}, u32[]{:S(2)}, u32[]{:S(2)}) collective-permute-start(bf16[4,5,5120]{2,0,1:T(4,128)(2,1)S(1)} %bitcast.156), channel_id=1, source_target_pairs={{0,1},{1,2},{2,3},{3,0},{4,5},{5,6},{6,7},{7,4},{8,9},{9,10},{10,1... | collective-permute-start | bytes 614408 | tf_op jit(solution)/shard_map/ppermute | solution.py:19
  226.9 12.9 %collective-permute-start.16 = (bf16[4,5,5120]{2,0,1:T(4,128)(2,1)S(1)}, bf16[4,5,5120]{2,0,1:T(4,128)(2,1)S(1)}, u32[]{:S(2)}, u32[]{:S(2)}) collective-permute-start(bf16[4,5,5120]{2,0,1:T(4,128)(2,1)S(1)} %bitcast.157), channel_id=1, source_target_pairs={{0,2},{1,3},{2,0},{3,1},{4,6},{5,7},{6,4},{7,5},{8,10},{9,11},{10,... | collective-permute-start | bytes 614408 | tf_op jit(solution)/shard_map/ppermute | solution.py:19
  234.8 5.0 collective-permute-start.17
  241.8 19.2 %collective-permute-start.18 = (bf16[4,5,5120]{2,0,1:T(4,128)(2,1)S(1)}, bf16[4,5,5120]{2,0,1:T(4,128)(2,1)S(1)}, u32[]{:S(2)}, u32[]{:S(2)}) collective-permute-start(bf16[4,5,5120]{2,0,1:T(4,128)(2,1)S(1)} %bitcast.158), channel_id=1, source_target_pairs={{0,4},{4,8},{8,12},{12,0},{1,5},{5,9},{9,13},{13,1},{2,6},{6,10},{... | collective-permute-start | bytes 614408 | tf_op jit(solution)/shard_map/ppermute | solution.py:19
  258.4 14.5 %collective-permute-start.19 = (bf16[4,5,5120]{2,0,1:T(4,128)(2,1)S(1)}, bf16[4,5,5120]{2,0,1:T(4,128)(2,1)S(1)}, u32[]{:S(2)}, u32[]{:S(2)}) collective-permute-start(bf16[4,5,5120]{2,0,1:T(4,128)(2,1)S(1)} %bitcast.160), channel_id=1, source_target_pairs={{0,8},{4,12},{8,0},{12,4},{1,9},{5,13},{9,1},{13,5},{2,10},{6,14},... | collective-permute-start | bytes 614408 | tf_op jit(solution)/shard_map/ppermute | solution.py:19
  258.8 14.4 %collective-permute-start.20 = (bf16[4,5,5120]{2,0,1:T(4,128)(2,1)S(1)}, bf16[4,5,5120]{2,0,1:T(4,128)(2,1)S(1)}, u32[]{:S(2)}, u32[]{:S(2)}) collective-permute-start(bf16[4,5,5120]{2,0,1:T(4,128)(2,1)S(1)} %bitcast.162), channel_id=1, source_target_pairs={{0,12},{4,0},{8,4},{12,8},{1,13},{5,1},{9,5},{13,9},{2,14},{6,2},{... | collective-permute-start | bytes 614408 | tf_op jit(solution)/shard_map/ppermute | solution.py:19
  278.4 23.4 %collective-permute-start.21 = (bf16[80,5120]{1,0:T(8,128)(2,1)S(1)}, bf16[80,5120]{1,0:T(8,128)(2,1)S(1)}, u32[]{:S(2)}, u32[]{:S(2)}) collective-permute-start(bf16[80,5120]{1,0:T(8,128)(2,1)S(1)} %reshape_reshape.4), channel_id=1, source_target_pairs={{0,32},{32,0},{1,33},{33,1},{2,34},{34,2},{3,35},{35,3},{4,36},{36... | collective-permute-start | bytes 2457608 | tf_op jit(solution)/shard_map/ppermute | solution.py:19
  278.5 26.1 %collective-permute-start.22 = (bf16[80,5120]{1,0:T(8,128)(2,1)S(1)}, bf16[80,5120]{1,0:T(8,128)(2,1)S(1)}, u32[]{:S(2)}, u32[]{:S(2)}) collective-permute-start(bf16[80,5120]{1,0:T(8,128)(2,1)S(1)} %reshape_reshape.4), channel_id=1, source_target_pairs={{0,64},{64,128},{128,192},{192,0},{1,65},{65,129},{129,193},{193,1... | collective-permute-start | bytes 2457608 | tf_op jit(solution)/shard_map/ppermute | solution.py:19
  278.7 35.9 %collective-permute-start.24 = (bf16[80,5120]{1,0:T(8,128)(2,1)S(1)}, bf16[80,5120]{1,0:T(8,128)(2,1)S(1)}, u32[]{:S(2)}, u32[]{:S(2)}) collective-permute-start(bf16[80,5120]{1,0:T(8,128)(2,1)S(1)} %reshape_reshape.4), channel_id=1, source_target_pairs={{0,192},{64,0},{128,64},{192,128},{1,193},{65,1},{129,65},{193,129... | collective-permute-start | bytes 2457608 | tf_op jit(solution)/shard_map/ppermute | solution.py:19
  301.8 12.7 %collective-permute-start.23 = (bf16[80,5120]{1,0:T(8,128)(2,1)S(1)}, bf16[80,5120]{1,0:T(8,128)(2,1)S(1)}, u32[]{:S(2)}, u32[]{:S(2)}) collective-permute-start(bf16[80,5120]{1,0:T(8,128)(2,1)S(1)} %collective-permute-done.21), channel_id=1, source_target_pairs={{0,64},{64,128},{128,192},{192,0},{1,65},{65,129},{129,193},{193,1... | collective-permute-start | bytes 2457608 | tf_op jit(solution)/shard_map/ppermute | solution.py:19
  301.8 12.9 %collective-permute-start.25 = (bf16[80,5120]{1,0:T(8,128)(2,1)S(1)}, bf16[80,5120]{1,0:T(8,128)(2,1)S(1)}, u32[]{:S(2)}, u32[]{:S(2)}) collective-permute-start(bf16[80,5120]{1,0:T(8,128)(2,1)S(1)} %collective-permute-done.21), channel_id=1, source_target_pairs={{0,192},{64,0},{128,64},{192,128},{1,193},{65,1},{129,65},{193,129... | collective-permute-start | bytes 2457608 | tf_op jit(solution)/shard_map/ppermute | solution.py:19
  314.9 46.9 %collective-permute-start.28 = (bf16[480,5120]{1,0:T(8,128)(2,1)S(1)}, bf16[480,5120]{1,0:T(8,128)(2,1)S(1)}, u32[]{:S(2)}, u32[]{:S(2)}) collective-permute-start(bf16[480,5120]{1,0:T(8,128)(2,1)S(1)} %get-tuple-element.35), channel_id=1, source_target_pairs={{0,16},{16,0},{1,17},{17,1},{2,18},{18,2},{3,19},{19,3},{4,20},{20... | collective-permute-start | bytes 14745608 | tf_op jit(solution)/shard_map/ppermute | solution.py:19
  334.7 21.0 %collective-permute-start.26 = (bf16[80,5120]{1,0:T(8,128)(2,1)S(1)}, bf16[80,5120]{1,0:T(8,128)(2,1)S(1)}, u32[]{:S(2)}, u32[]{:S(2)}) collective-permute-start(bf16[80,5120]{1,0:T(8,128)(2,1)S(1)} %collective-permute-done.22), channel_id=1, source_target_pairs={{0,64},{64,128},{128,192},{192,0},{1,65},{65,129},{129,193},{193,1... | collective-permute-start | bytes 2457608 | tf_op jit(solution)/shard_map/ppermute | solution.py:19
  334.7 21.0 %collective-permute-start.27 = (bf16[80,5120]{1,0:T(8,128)(2,1)S(1)}, bf16[80,5120]{1,0:T(8,128)(2,1)S(1)}, u32[]{:S(2)}, u32[]{:S(2)}) collective-permute-start(bf16[80,5120]{1,0:T(8,128)(2,1)S(1)} %collective-permute-done.25), channel_id=1, source_target_pairs={{0,192},{64,0},{128,64},{192,128},{1,193},{65,1},{129,65},{193,129... | collective-permute-start | bytes 2457608 | tf_op jit(solution)/shard_map/ppermute | solution.py:19
  355.7 8.6 %collective-permute-start.29 = (bf16[160,5120]{1,0:T(8,128)(2,1)S(1)}, bf16[160,5120]{1,0:T(8,128)(2,1)S(1)}, u32[]{:S(2)}, u32[]{:S(2)}) collective-permute-start(bf16[160,5120]{1,0:T(8,128)(2,1)S(1)} %pad_maximum_fusion), channel_id=1, source_target_pairs={{0,16},{16,0},{1,17},{17,1},{2,18},{18,2},{3,19},{19,3},{4,20},{20... | collective-permute-start | bytes 4915208 | tf_op jit(solution)/shard_map/ppermute | solution.py:19
  398.1 10.6 %collective-permute-start.30 = (bf16[640,5120]{1,0:T(8,128)(2,1)S(1)}, bf16[640,5120]{1,0:T(8,128)(2,1)S(1)}, u32[]{:S(2)}, u32[]{:S(2)}) collective-permute-start(bf16[640,5120]{1,0:T(8,128)(2,1)S(1)} %slice.200), channel_id=1, source_target_pairs={{0,16},{16,0},{1,17},{17,1},{2,18},{18,2},{3,19},{19,3},{4,20},{20... | collective-permute-start | bytes 19660808 | tf_op jit(solution)/shard_map/ppermute | solution.py:19
  413.8 20.2 %collective-permute-start.31 = (bf16[80,5120]{1,0:T(8,128)(2,1)S(1)}, bf16[80,5120]{1,0:T(8,128)(2,1)S(1)}, u32[]{:S(2)}, u32[]{:S(2)}) collective-permute-start(bf16[80,5120]{1,0:T(8,128)(2,1)S(1)} %get-tuple-element.17), channel_id=1, source_target_pairs={{0,192},{64,0},{128,64},{192,128},{1,193},{65,1},{129,65},{193,129... | collective-permute-start | bytes 2457608 | tf_op jit(solution)/shard_map/ppermute | solution.py:19
  416.6 20.6 %collective-permute-start.33 = (bf16[80,5120]{1,0:T(8,128)(2,1)S(1)}, bf16[80,5120]{1,0:T(8,128)(2,1)S(1)}, u32[]{:S(2)}, u32[]{:S(2)}) collective-permute-start(bf16[80,5120]{1,0:T(8,128)(2,1)S(1)} %get-tuple-element.18), channel_id=1, source_target_pairs={{0,64},{64,128},{128,192},{192,0},{1,65},{65,129},{129,193},{193,1... | collective-permute-start | bytes 2457608 | tf_op jit(solution)/shard_map/ppermute | solution.py:19
  437.7 36.2 %collective-permute-start.32 = (bf16[160,5120]{1,0:T(8,128)(2,1)S(1)}, bf16[160,5120]{1,0:T(8,128)(2,1)S(1)}, u32[]{:S(2)}, u32[]{:S(2)}) collective-permute-start(bf16[160,5120]{1,0:T(8,128)(2,1)S(1)} %pad_maximum_fusion.1), channel_id=1, source_target_pairs={{0,192},{64,0},{128,64},{192,128},{1,193},{65,1},{129,65},{193,129... | collective-permute-start | bytes 4915208 | tf_op jit(solution)/shard_map/ppermute | solution.py:19
  438.2 37.6 %collective-permute-start.34 = (bf16[160,5120]{1,0:T(8,128)(2,1)S(1)}, bf16[160,5120]{1,0:T(8,128)(2,1)S(1)}, u32[]{:S(2)}, u32[]{:S(2)}) collective-permute-start(bf16[160,5120]{1,0:T(8,128)(2,1)S(1)} %pad_maximum_fusion.2), channel_id=1, source_target_pairs={{0,64},{64,128},{128,192},{192,0},{1,65},{65,129},{129,193},{193,1... | collective-permute-start | bytes 4915208 | tf_op jit(solution)/shard_map/ppermute | solution.py:19
  476.5 21.8 %collective-permute-start.35 = (bf16[80,5120]{1,0:T(8,128)(2,1)S(1)}, bf16[80,5120]{1,0:T(8,128)(2,1)S(1)}, u32[]{:S(2)}, u32[]{:S(2)}) collective-permute-start(bf16[80,5120]{1,0:T(8,128)(2,1)S(1)} %slice.247), channel_id=1, source_target_pairs={{0,32},{32,0},{1,33},{33,1},{2,34},{34,2},{3,35},{35,3},{4,36},{36... | collective-permute-start | bytes 2457608 | tf_op jit(solution)/shard_map/ppermute | solution.py:19
  501.1 32.9 %collective-permute-start.36 = (bf16[4,5,5120]{2,1,0:T(8,128)(2,1)}, bf16[4,5,5120]{2,1,0:T(8,128)(2,1)}, u32[]{:S(2)}, u32[]{:S(2)}) collective-permute-start(bf16[4,5,5120]{2,1,0:T(8,128)(2,1)} %squeeze.64), channel_id=1, source_target_pairs={{0,12},{4,0},{8,4},{12,8},{1,13},{5,1},{9,5},{13,9},{2,14},{6,2},{... | collective-permute-start | bytes 614408 | tf_op jit(solution)/shard_map/ppermute | solution.py:19
  507.2 48.7 %collective-permute-start.37 = (bf16[4,5,5120]{2,1,0:T(8,128)(2,1)}, bf16[4,5,5120]{2,1,0:T(8,128)(2,1)S(1)}, u32[]{:S(2)}, u32[]{:S(2)}) collective-permute-start(bf16[4,5,5120]{2,1,0:T(8,128)(2,1)} %squeeze.65), channel_id=1, source_target_pairs={{0,8},{4,12},{8,0},{12,4},{1,9},{5,13},{9,1},{13,5},{2,10},{6,14},... | collective-permute-start | bytes 614408 | tf_op jit(solution)/shard_map/ppermute | solution.py:19
  528.9 27.0 %collective-permute-start.38 = (bf16[4,5,5120]{2,1,0:T(8,128)(2,1)}, bf16[4,5,5120]{2,1,0:T(8,128)(2,1)}, u32[]{:S(2)}, u32[]{:S(2)}) collective-permute-start(bf16[4,5,5120]{2,1,0:T(8,128)(2,1)} %squeeze.66), channel_id=1, source_target_pairs={{0,4},{4,8},{8,12},{12,0},{1,5},{5,9},{9,13},{13,1},{2,6},{6,10},{... | collective-permute-start | bytes 614408 | tf_op jit(solution)/shard_map/ppermute | solution.py:19
  557.4 8.0 %collective-permute-start.39 = (bf16[4,5,5120]{2,1,0:T(8,128)(2,1)S(1)}, bf16[4,5,5120]{2,1,0:T(8,128)(2,1)S(1)}, u32[]{:S(2)}, u32[]{:S(2)}) collective-permute-start(bf16[4,5,5120]{2,1,0:T(8,128)(2,1)S(1)} %get-tuple-element.28), channel_id=1, source_target_pairs={{0,3},{1,0},{2,1},{3,2},{4,7},{5,4},{6,5},{7,6},{8,11},{9,8},{10,9... | collective-permute-start | bytes 614408 | tf_op jit(solution)/shard_map/ppermute | solution.py:19
  557.5 9.6 %collective-permute-start.40 = (bf16[4,5,5120]{2,1,0:T(8,128)(2,1)S(1)}, bf16[4,5,5120]{2,1,0:T(8,128)(2,1)S(1)}, u32[]{:S(2)}, u32[]{:S(2)}) collective-permute-start(bf16[4,5,5120]{2,1,0:T(8,128)(2,1)S(1)} %get-tuple-element.30), channel_id=1, source_target_pairs={{0,2},{1,3},{2,0},{3,1},{4,6},{5,7},{6,4},{7,5},{8,10},{9,11},{10,... | collective-permute-start | bytes 614408 | tf_op jit(solution)/shard_map/ppermute | solution.py:19
  560.0 15.8 %collective-permute-start.41 = (bf16[4,5,5120]{2,1,0:T(8,128)(2,1)S(1)}, bf16[4,5,5120]{2,1,0:T(8,128)(2,1)S(1)}, u32[]{:S(2)}, u32[]{:S(2)}) collective-permute-start(bf16[4,5,5120]{2,1,0:T(8,128)(2,1)S(1)} %get-tuple-element.29), channel_id=1, source_target_pairs={{0,1},{1,2},{2,3},{3,0},{4,5},{5,6},{6,7},{7,4},{8,9},{9,10},{10,1... | collective-permute-start | bytes 614408 | tf_op jit(solution)/shard_map/ppermute | solution.py:19
  (9 other events, 27.6 us)
Sparse Core Ops, SparseCore 0:
  19.3 71.4 all-gather.2

commit v3 on v1

--- a/solution.py
+++ b/solution.py
@@ -44,22 +44,20 @@
     return jnp.concatenate([first, last, _pp(first, "core", 2, 1), _pp(last, "core", 2, 1)], 0)
 
 
-def rs_rel(p):
-    r = p.shape[0] // 16
-    got = _pp(p[8 * r:], "core", 2, 1).astype(jnp.float32)
-    s = p[: 8 * r].astype(jnp.float32) + got
-    blk = [s[i * r:(i + 1) * r] for i in range(8)]
+def rs_rel(own, other):
+    r = own.shape[0] // 8
+    got = _pp(other, "core", 2, 1)
+    blk = [own[i * r:(i + 1) * r].astype(jnp.float32) + got[i * r:(i + 1) * r].astype(jnp.float32) for i in range(8)]
     a = _pp(blk[6].astype(jnp.bfloat16), "x", 4, -1)
     b = _pp(blk[7].astype(jnp.bfloat16), "x", 4, 1)
-    s2 = blk[2] + a.astype(jnp.float32)
-    s5 = blk[5] + b.astype(jnp.float32)
-    to_left = jnp.concatenate([s2, blk[3]], 0).astype(jnp.bfloat16)
-    to_right = jnp.concatenate([blk[4], s5], 0).astype(jnp.bfloat16)
-    from_right = _pp(to_left, "x", 4, -1).astype(jnp.float32)
-    from_left = _pp(to_right, "x", 4, 1).astype(jnp.float32)
-    t = jnp.concatenate([blk[0], blk[1]], 0) + from_right + from_left
-    z = _pp(t[r:].astype(jnp.bfloat16), "zh", 2, 1).astype(jnp.float32)
-    return t[:r] + z
+    c = _pp(blk[3].astype(jnp.bfloat16), "x", 4, -1)
+    d = _pp(blk[4].astype(jnp.bfloat16), "x", 4, 1)
+    e = _pp((blk[5] + b.astype(jnp.float32)).astype(jnp.bfloat16), "x", 4, 1)
+    f = _pp((blk[2] + a.astype(jnp.float32)).astype(jnp.bfloat16), "x", 4, -1)
+    t1 = blk[1] + c.astype(jnp.float32) + e.astype(jnp.float32)
+    z = _pp(t1.astype(jnp.bfloat16), "zh", 2, 1)
+    t0 = blk[0] + f.astype(jnp.float32) + d.astype(jnp.float32)
+    return t0 + z.astype(jnp.float32)
 
 
 def local(
@@ -131,9 +129,10 @@
     feature_rows = jnp.take(
         feature_block.reshape(n_ctx, tok_rows, -1), order, axis=0
     ).reshape(n_ctx * tok_rows, -1)
-    attn_sum = rs_rel(
-        jnp.dot(feature_rows, proj_rows, preferred_element_type=jnp.float32).astype(jnp.bfloat16)
-    )
+    half = 8 * tok_rows
+    attn_other = jnp.dot(feature_rows[half:], proj_rows, preferred_element_type=jnp.float32).astype(jnp.bfloat16)
+    attn_own = jnp.dot(feature_rows[:half], proj_rows, preferred_element_type=jnp.float32).astype(jnp.bfloat16)
+    attn_sum = rs_rel(attn_own, attn_other)
     hidden_state = resid[0].astype(jnp.float32) + attn_sum.astype(jnp.bfloat16).astype(jnp.float32)
     mean_square = jnp.mean(hidden_state * hidden_state, axis=-1, keepdims=True)
     normed = hidden_state * lax.rsqrt(mean_square + 1e-05) * norm_gain.astype(jnp.float32)
@@ -161,12 +160,17 @@
     up_local = up_weight[0]
     down_local = down_weight[0]
     piece = ag_rel(arrived_rows)
-    gate = jnp.dot(piece, gate_local, preferred_element_type=jnp.float32)
-    up = jnp.dot(piece, up_local, preferred_element_type=jnp.float32)
-    inner = (jax.nn.silu(gate) * up).astype(jnp.bfloat16)
-    summed = rs_rel(
-        jnp.dot(inner, down_local, preferred_element_type=jnp.float32).astype(jnp.bfloat16)
-    ).astype(jnp.bfloat16)
+    rows_half = piece.shape[0] // 2
+
+    def expert_rows(rows):
+        gate = jnp.dot(rows, gate_local, preferred_element_type=jnp.float32)
+        up = jnp.dot(rows, up_local, preferred_element_type=jnp.float32)
+        inner = (jax.nn.silu(gate) * up).astype(jnp.bfloat16)
+        return jnp.dot(inner, down_local, preferred_element_type=jnp.float32).astype(jnp.bfloat16)
+
+    part_own = expert_rows(piece[:rows_half])
+    part_other = expert_rows(piece[rows_half:])
+    summed = rs_rel(part_own, part_other).astype(jnp.bfloat16)
     expert_out = summed.reshape(n_exp, capacity, width)
     returned = lax.all_to_all(expert_out, EXP, split_axis=0, concat_axis=0, tiled=True)
     combined = jnp.einsum("tes,esd->td", selector_b, returned, preferred_element_type=jnp.float32)

time: 569 us -> 548 us (0.963)
  waiting for transfers between devices: 234 us -> 210 us
  starting transfers between devices: 62.4 us -> 82.6 us
  other arithmetic: 28.7 us -> 19.3 us
  blocking collectives: 127 us -> 118 us
  local copies, waits for them, and re-layouts: 52.7 us -> 44.7 us
  matrix products: 43.1 us -> 50.2 us
    ppermute x30 -> x34, waiting for transfers between devices: 220 us -> 196 us  [_pp(): return lax.ppermute(v, axis, [(i, (i + shift) % n) for i in range(n)])]
    ppermute x30 -> x34, starting transfers between devices: 49.5 us -> 69.8 us  [_pp(): return lax.ppermute(v, axis, [(i, (i + shift) % n) for i in range(n)])]
    another operation x5 -> x1, other arithmetic: 19.4 us -> 0.18 us
    convert_element_type x1 -> x9, other arithmetic: 1.04 us -> 13.9 us  [the longest x2 5.14 us: rs_rel(): f = _pp((blk[2] + a.astype(jnp.float32)).astype(jnp.bfloat16), 'x', 4, -1)]
    all_to_all x1, blocking collectives: 70.6 us -> 58.2 us  [local(): lax.all_to_all(expert_out, EXP, split_axis=0, concat_axis=0, tiled=True)]
    dot_general x3 -> x6, matrix products: 32.6 us -> 39.7 us  [the longest x2 26.8 us: expert_rows(): jnp.dot(inner, down_local, preferred_element_type=jnp.float32)]
    unnamed x37 -> x47, local copies, waits for them, and re-layouts: 20.6 us -> 16.9 us
  transfers between devices with their start and end apart: 32 -> 36, of which waited for: 20 -> 20; matrix products, arithmetic and copies ran while one was open for 7% -> 12% of each run, Pallas kernels for 0% -> 0%
where the time goes in v3:
time: 548 us; the launch traced here: 539 us
  waiting for transfers between devices  210 us (38%)
  blocking collectives  118 us (22%)
  starting transfers between devices  82.6 us (15%)
  matrix products  50.2 us (9%)
  local copies, waits for them, and re-layouts  44.7 us (8%)
  other arithmetic  19.3 us (4%)
  between operations  14 us (3%)
    ppermute x34, waiting for transfers between devices, _pp(): return lax.ppermute(v, axis, [(i, (i + shift) % n) for i in range(n)])  196 us
    ppermute x34, starting transfers between devices, _pp(): return lax.ppermute(v, axis, [(i, (i + shift) % n) for i in range(n)])  69.8 us
    all_to_all x1, blocking collectives, local(): lax.all_to_all(outgoing, EXP, split_axis=0, concat_axis=0, tiled=True)  59.7 us
    all_to_all x1, blocking collectives, local(): lax.all_to_all(expert_out, EXP, split_axis=0, concat_axis=0, tiled=True)  58.2 us
    dot_general x2, matrix products, expert_rows(): jnp.dot(inner, down_local, preferred_element_type=jnp.float32)  26.8 us
    unnamed x47, local copies, waits for them, and re-layouts  16.9 us
    all_to_all x1, waiting for transfers between devices, local(): lax.all_to_all(attended.reshape(tok_rows, n_ctx, qwidth // n_ctx), CTX, s...  14.9 us
    all_to_all x1, starting transfers between devices, local(): lax.all_to_all(attended.reshape(tok_rows, n_ctx, qwidth // n_ctx), CTX, s...  12.8 us
  transfers between devices with their start and end apart: 36, of which 20 were waited for; matrix products, arithmetic and copies ran while one was open for 12% of the time, Pallas kernels for 0%

profile of v3, /device:TPU:1, one launch (start us, length us, event | category | flops | bytes accessed | tf_op | source)
XLA Modules:
  0.0 539.3 jit_solution(17968902274986594777)
XLA Ops:
  8.7 7.8 %collective-permute-start = (bf16[64,1024]{0,1:T(8,128)(2,1)S(1)}, bf16[64,1024]{0,1:T(8,128)(2,1)S(1)}, u32[]{:S(2)}, u32[]{:S(2)}) collective-permute-start(bf16[64,1024]{0,1:T(8,128)(2,1)S(1)} %pad_maximum_fusion.1), channel_id=1, source_target_pairs={{0,32},{32,0},{1,33},{33,1},{2,34},{34,2},{3,35},{35,3},{4,36},{36... | collective-permute-start | bytes 393224 | tf_op jit(solution)/shard_map/ppermute | solution.py:19
  19.9 3.1 collective-permute-done
  23.1 2.9 collective-permute-start.4
  26.1 4.2 collective-permute-done.4
  33.5 3.8 concatenate.63
  39.9 2.7 collective-permute-start.6
  43.0 6.1 %collective-permute-done.5 = bf16[64,1024]{0,1:T(8,128)(2,1)} collective-permute-done((bf16[64,1024]{0,1:T(8,128)(2,1)S(1)}, bf16[64,1024]{0,1:T(8,128)(2,1)}, u32[]{:S(2)}, u32[]{:S(2)}) %collective-permute-start.5) | collective-permute-done | bytes 131104 | tf_op jit(solution)/shard_map/ppermute | solution.py:19
  54.8 5.6 %concatenate.65 = bf16[1024,1024]{0,1:T(8,128)(2,1)} concatenate(bf16[64,1024]{0,1:T(8,128)(2,1)S(1)} %pad_maximum_fusion.1, bf16[64,1024]{0,1:T(8,128)(2,1)S(1)} %collective-permute-done, bf16[64,1024]{0,1:T(8,128)(2,1)S(1)} %collective-permute-done.1, bf16[64,1024]{0,1:T(8,128)(2,1)} %collective-permute-done.2, bf16[64,1024]{0,1:T(8,128)(2,1)} %collective-permute-done.3, ...), dimensions={0} | concatenate | bytes 4194304 | tf_op jit(solution)/shard_map/concatenate | solution.py:44
  60.4 3.1 fusion.86
  63.5 4.9 fusion.88
  68.4 2.9 fusion.26
  75.0 12.8 %all-to-all-start = ((bf16[64,16,160]{2,0,1:T(8,128)(2,1)}), bf16[64,16,160]{2,0,1:T(8,128)(2,1)S(1)}, u32[]{:S(2)}, u32[]{:S(2)}) async-start(bf16[64,16,160]{2,0,1:T(8,128)(2,1)} %copy.41), calls=%async_computation | async-start | bytes 1048576 | tf_op jit(solution)/shard_map/all_to_all | solution.py:122
  88.0 14.9 %all-to-all-done = bf16[64,16,160]{2,0,1:T(8,128)(2,1)S(1)} async-done(((bf16[64,16,160]{2,0,1:T(8,128)(2,1)}), bf16[64,16,160]{2,0,1:T(8,128)(2,1)S(1)}, u32[]{:S(2)}, u32[]{:S(2)}) %all-to-all-start) | async-done | bytes 327712 | tf_op jit(solution)/shard_map/all_to_all | solution.py:122
  106.1 4.1 reshape.274
  110.2 3.1 convolution_convert_fusion.2
  115.9 6.8 %collective-permute-done.9 = bf16[512,5120]{1,0:T(8,128)(2,1)S(1)} collective-permute-done((bf16[512,5120]{1,0:T(8,128)(2,1)S(1)}, bf16[512,5120]{1,0:T(8,128)(2,1)S(1)}, u32[]{:S(2)}, u32[]{:S(2)}) %collective-permute-start.9) | collective-permute-done | bytes 5242912 | tf_op jit(solution)/shard_map/ppermute | solution.py:19
  123.3 15.6 %collective-permute-done.10 = bf16[64,5120]{1,0:T(8,128)(2,1)S(1)} collective-permute-done((bf16[64,5120]{1,0:T(8,128)(2,1)S(1)}, bf16[64,5120]{1,0:T(8,128)(2,1)S(1)}, u32[]{:S(2)}, u32[]{:S(2)}) %collective-permute-start.10) | collective-permute-done | bytes 655392 | tf_op jit(solution)/shard_map/ppermute | solution.py:19
  140.0 2.8 collective-permute-start.13
  142.8 13.4 %collective-permute-done.14 = bf16[64,5120]{1,0:T(8,128)(2,1)S(1)} collective-permute-done((bf16[64,5120]{1,0:T(8,128)(2,1)S(1)}, bf16[64,5120]{1,0:T(8,128)(2,1)S(1)}, u32[]{:S(2)}, u32[]{:S(2)}) %collective-permute-start.14) | collective-permute-done | bytes 655392 | tf_op jit(solution)/shard_map/ppermute | solution.py:19
  156.6 2.6 collective-permute-start.11
  159.2 12.7 %collective-permute-done.15 = bf16[64,5120]{1,0:T(8,128)(2,1)S(1)} collective-permute-done((bf16[64,5120]{1,0:T(8,128)(2,1)S(1)}, bf16[64,5120]{1,0:T(8,128)(2,1)S(1)}, u32[]{:S(2)}, u32[]{:S(2)}) %collective-permute-start.15) | collective-permute-done | bytes 655392 | tf_op jit(solution)/shard_map/ppermute | solution.py:19
  174.0 12.0 %collective-permute-done.12 = bf16[64,5120]{1,0:T(8,128)(2,1)S(1)} collective-permute-done((bf16[64,5120]{1,0:T(8,128)(2,1)S(1)}, bf16[64,5120]{1,0:T(8,128)(2,1)S(1)}, u32[]{:S(2)}, u32[]{:S(2)}) %collective-permute-start.12) | collective-permute-done | bytes 655392 | tf_op jit(solution)/shard_map/ppermute | solution.py:19
  189.4 59.7 %all_to_all.25 = bf16[16,5,5120]{2,1,0:T(8,128)(2,1)} all-to-all(bf16[16,5,5120]{2,1,0:T(8,128)(2,1)S(1)} %copy.42), channel_id=1, replica_groups=mesh['x'=4,'zh'=2,'core'=2,'zl'=4,'y'=4] {'zl','y'}, dimensions={0} | all-to-all | bytes 1638400 | tf_op jit(solution)/shard_map/all_to_all | solution.py:157
  252.7 2.7 collective-permute-start.20
  255.4 17.5 %collective-permute-done.17 = bf16[80,5120]{1,0:T(8,128)(2,1)S(1)} collective-permute-done((bf16[80,5120]{1,0:T(8,128)(2,1)}, bf16[80,5120]{1,0:T(8,128)(2,1)S(1)}, u32[]{:S(2)}, u32[]{:S(2)}) %collective-permute-start.17) | collective-permute-done | bytes 819232 | tf_op jit(solution)/shard_map/ppermute | solution.py:19
  272.9 2.7 collective-permute-start.21
  275.8 9.7 %collective-permute-done.19 = bf16[80,5120]{1,0:T(8,128)(2,1)S(1)} collective-permute-done((bf16[80,5120]{1,0:T(8,128)(2,1)S(1)}, bf16[80,5120]{1,0:T(8,128)(2,1)S(1)}, u32[]{:S(2)}, u32[]{:S(2)}) %collective-permute-start.19) | collective-permute-done | bytes 819232 | tf_op jit(solution)/shard_map/ppermute | solution.py:19
  286.0 2.6 copy-done.11
  288.6 21.6 %collective-permute-start.24 = (bf16[480,5120]{1,0:T(8,128)(2,1)S(1)}, bf16[480,5120]{1,0:T(8,128)(2,1)S(1)}, u32[]{:S(2)}, u32[]{:S(2)}) collective-permute-start(bf16[480,5120]{1,0:T(8,128)(2,1)S(1)} %get-tuple-element.20), channel_id=1, source_target_pairs={{0,16},{16,0},{1,17},{17,1},{2,18},{18,2},{3,19},{19,3},{4,20},{20... | collective-permute-start | bytes 14745608 | tf_op jit(solution)/shard_map/ppermute | solution.py:19
  310.3 2.9 collective-permute-start.23
  313.1 18.1 %collective-permute-done.22 = bf16[80,5120]{1,0:T(8,128)(2,1)S(1)} collective-permute-done((bf16[80,5120]{1,0:T(8,128)(2,1)S(1)}, bf16[80,5120]{1,0:T(8,128)(2,1)S(1)}, u32[]{:S(2)}, u32[]{:S(2)}) %collective-permute-start.22) | collective-permute-done | bytes 819232 | tf_op jit(solution)/shard_map/ppermute | solution.py:19
  332.9 2.6 collective-permute-done.25
  335.6 2.8 copy-done.5
  338.4 2.7 fusion.7
  341.1 13.4 %convolution_convert_fusion = bf16[640,5120]{1,0:T(8,128)(2,1)} fusion(bf16[1,256,5120]{2,1,0:T(8,128)(2,1)S(1)} %copy-done, f32[640,256]{1,0:T(8,128)} %fusion.7, bf16[640,5120]{1,0:T(8,128)(2,1)} %copy-done.5, bf16[1,5120,256]{2,1,0:T(8,128)(2,1)} %param.23), kind=kOutput, calls=%fused_computation.2 | convolution fusion | flops 3359703040 | bytes 19005440 | tf_op jit(solution)/shard_map/dot_general | solution.py:169
  359.5 5.6 %fusion.9 = f32[640,256]{1,0:T(8,128)} fusion(bf16[640,5120]{1,0:T(8,128)(2,1)} %constant_dynamic-update-slice_fusion, bf16[1,5120,256]{2,1,0:T(8,128)(2,1)S(1)} %copy-done.15), kind=kOutput, calls=%fused_computation.18 | convolution fusion | flops 1677721600 | bytes 9830400 | tf_op jit(solution)/shard_map/dot_general | solution.py:167
  365.1 13.4 %convolution_convert_fusion.1 = bf16[640,5120]{1,0:T(8,128)(2,1)} fusion(bf16[1,256,5120]{2,1,0:T(8,128)(2,1)S(1)} %copy-done, f32[640,256]{1,0:T(8,128)} %fusion.9, bf16[640,5120]{1,0:T(8,128)(2,1)} %constant_dynamic-update-slice_fusion, bf16[1,5120,256]{2,1,0:T(8,128)(2,1)} %param.23), kind=kOutput, calls=%fused_computation.3 | convolution fusion | flops 3359703040 | bytes 19005440 | tf_op jit(solution)/shard_map/dot_general | solution.py:169
  380.1 2.9 collective-permute-start.27
  383.1 17.2 %collective-permute-done.27 = bf16[80,5120]{1,0:T(8,128)(2,1)S(1)} collective-permute-done((bf16[80,5120]{1,0:T(8,128)(2,1)S(1)}, bf16[80,5120]{1,0:T(8,128)(2,1)S(1)}, u32[]{:S(2)}, u32[]{:S(2)}) %collective-permute-start.27) | collective-permute-done | bytes 819232 | tf_op jit(solution)/shard_map/ppermute | solution.py:19
  400.3 4.1 add_convert_fusion.6
  404.9 3.1 collective-permute-start.30
  408.0 17.3 %collective-permute-done.31 = bf16[80,5120]{1,0:T(8,128)(2,1)S(1)} collective-permute-done((bf16[80,5120]{1,0:T(8,128)(2,1)S(1)}, bf16[80,5120]{1,0:T(8,128)(2,1)S(1)}, u32[]{:S(2)}, u32[]{:S(2)}) %collective-permute-start.31) | collective-permute-done | bytes 819232 | tf_op jit(solution)/shard_map/ppermute | solution.py:19
  427.1 2.8 collective-permute-start.28
  429.9 16.4 %collective-permute-done.32 = bf16[80,5120]{1,0:T(8,128)(2,1)S(1)} collective-permute-done((bf16[80,5120]{1,0:T(8,128)(2,1)S(1)}, bf16[80,5120]{1,0:T(8,128)(2,1)S(1)}, u32[]{:S(2)}, u32[]{:S(2)}) %collective-permute-start.32) | collective-permute-done | bytes 819232 | tf_op jit(solution)/shard_map/ppermute | solution.py:19
  448.3 15.6 %collective-permute-done.29 = bf16[80,5120]{1,0:T(8,128)(2,1)S(1)} collective-permute-done((bf16[80,5120]{1,0:T(8,128)(2,1)S(1)}, bf16[80,5120]{1,0:T(8,128)(2,1)S(1)}, u32[]{:S(2)}, u32[]{:S(2)}) %collective-permute-start.29) | collective-permute-done | bytes 819232 | tf_op jit(solution)/shard_map/ppermute | solution.py:19
  463.9 3.3 collective-permute-done.33
  467.1 2.9 add_convert_fusion
  472.4 58.2 %all_to_all.26 = bf16[16,5,5120]{2,1,0:T(8,128)(2,1)S(1)} all-to-all(bf16[16,5,5120]{2,1,0:T(8,128)(2,1)} %reshape.263), channel_id=1, replica_groups=mesh['x'=4,'zh'=2,'core'=2,'zl'=4,'y'=4] {'zl','y'}, dimensions={0} | all-to-all | bytes 1638400 | tf_op jit(solution)/shard_map/all_to_all | solution.py:175
  (135 shorter events, 55.1 us)
Async XLA Ops:
  6.5 334.6 %copy-start = (bf16[1,256,5120]{2,1,0:T(8,128)(2,1)S(1)}, bf16[1,256,5120]{2,1,0:T(8,128)(2,1)}, u32[]{:S(2)}) copy-start(bf16[1,256,5120]{2,1,0:T(8,128)(2,1)} %param.25) | copy-start | bytes 7864324
  6.5 36.1 %copy-start.17 = (s32[1,4]{1,0:T(1,128)S(1)}, s32[1,4]{1,0:T(1,128)}, u32[]{:S(2)}) copy-start(s32[1,4]{1,0:T(1,128)} %param.17) | copy-start | bytes 52
  6.5 99.5 %all-gather.3.cloned.1.call-start = ((), (), s32[]{:S(2)}) async-start(), calls=%async_computation.3 | async-start | bytes 2785280 | tf_op jit(solution)/shard_map/all_gather | solution.py:121
  8.7 14.4 %collective-permute-start = (bf16[64,1024]{0,1:T(8,128)(2,1)S(1)}, bf16[64,1024]{0,1:T(8,128)(2,1)S(1)}, u32[]{:S(2)}, u32[]{:S(2)}) collective-permute-start(bf16[64,1024]{0,1:T(8,128)(2,1)S(1)} %pad_maximum_fusion.1), channel_id=1, source_target_pairs={{0,32},{32,0},{1,33},{33,1},{2,34},{34,2},{3,35},{35,3},{4,36},{36... | collective-permute-start | bytes 393224 | tf_op jit(solution)/shard_map/ppermute | solution.py:19
  16.5 9.6 %collective-permute-start.1 = (bf16[64,1024]{0,1:T(8,128)(2,1)S(1)}, bf16[64,1024]{0,1:T(8,128)(2,1)S(1)}, u32[]{:S(2)}, u32[]{:S(2)}) collective-permute-start(bf16[64,1024]{0,1:T(8,128)(2,1)S(1)} %pad_maximum_fusion.1), channel_id=1, source_target_pairs={{0,64},{64,128},{128,192},{192,0},{1,65},{65,129},{129,193},{193,1... | collective-permute-start | bytes 393224 | tf_op jit(solution)/shard_map/ppermute | solution.py:19
  17.7 8.4 %collective-permute-start.3 = (bf16[64,1024]{0,1:T(8,128)(2,1)S(1)}, bf16[64,1024]{0,1:T(8,128)(2,1)}, u32[]{:S(2)}, u32[]{:S(2)}) collective-permute-start(bf16[64,1024]{0,1:T(8,128)(2,1)S(1)} %pad_maximum_fusion.1), channel_id=1, source_target_pairs={{0,192},{64,0},{128,64},{192,128},{1,193},{65,1},{129,65},{193,129... | collective-permute-start | bytes 393224 | tf_op jit(solution)/shard_map/ppermute | solution.py:19
  23.1 7.2 %collective-permute-start.4 = (bf16[64,1024]{0,1:T(8,128)(2,1)S(1)}, bf16[64,1024]{0,1:T(8,128)(2,1)S(1)}, u32[]{:S(2)}, u32[]{:S(2)}) collective-permute-start(bf16[64,1024]{0,1:T(8,128)(2,1)S(1)} %collective-permute-done), channel_id=1, source_target_pairs={{0,192},{64,0},{128,64},{192,128},{1,193},{65,1},{129,65},{193,129... | collective-permute-start | bytes 393224 | tf_op jit(solution)/shard_map/ppermute | solution.py:19
  26.0 7.5 %collective-permute-start.2 = (bf16[64,1024]{0,1:T(8,128)(2,1)S(1)}, bf16[64,1024]{0,1:T(8,128)(2,1)}, u32[]{:S(2)}, u32[]{:S(2)}) collective-permute-start(bf16[64,1024]{0,1:T(8,128)(2,1)S(1)} %collective-permute-done), channel_id=1, source_target_pairs={{0,64},{64,128},{128,192},{192,0},{1,65},{65,129},{129,193},{193,1... | collective-permute-start | bytes 393224 | tf_op jit(solution)/shard_map/ppermute | solution.py:19
  37.3 17.4 %collective-permute-start.7 = (bf16[384,1024]{0,1:T(8,128)(2,1)}, bf16[384,1024]{0,1:T(8,128)(2,1)}, u32[]{:S(2)}, u32[]{:S(2)}) collective-permute-start(bf16[384,1024]{0,1:T(8,128)(2,1)} %concatenate.63), channel_id=1, source_target_pairs={{0,16},{16,0},{1,17},{17,1},{2,18},{18,2},{3,19},{19,3},{4,20},{20... | collective-permute-start | bytes 2359304 | tf_op jit(solution)/shard_map/ppermute | solution.py:19
  39.9 9.1 %collective-permute-start.5 = (bf16[64,1024]{0,1:T(8,128)(2,1)S(1)}, bf16[64,1024]{0,1:T(8,128)(2,1)}, u32[]{:S(2)}, u32[]{:S(2)}) collective-permute-start(bf16[64,1024]{0,1:T(8,128)(2,1)S(1)} %collective-permute-done.1), channel_id=1, source_target_pairs={{0,64},{64,128},{128,192},{192,0},{1,65},{65,129},{129,193},{193,1... | collective-permute-start | bytes 393224 | tf_op jit(solution)/shard_map/ppermute | solution.py:19
  39.9 9.1 %collective-permute-start.6 = (bf16[64,1024]{0,1:T(8,128)(2,1)}, bf16[64,1024]{0,1:T(8,128)(2,1)}, u32[]{:S(2)}, u32[]{:S(2)}) collective-permute-start(bf16[64,1024]{0,1:T(8,128)(2,1)} %copy-done.9), channel_id=1, source_target_pairs={{0,192},{64,0},{128,64},{192,128},{1,193},{65,1},{129,65},{193,129... | collective-permute-start | bytes 393224 | tf_op jit(solution)/shard_map/ppermute | solution.py:19
  51.0 3.8 collective-permute-start.8
  60.4 3.1 copy-start.10
  75.0 27.8 %all-to-all-start = ((bf16[64,16,160]{2,0,1:T(8,128)(2,1)}), bf16[64,16,160]{2,0,1:T(8,128)(2,1)S(1)}, u32[]{:S(2)}, u32[]{:S(2)}) async-start(bf16[64,16,160]{2,0,1:T(8,128)(2,1)} %copy.41), calls=%async_computation | async-start | bytes 1048576 | tf_op jit(solution)/shard_map/all_to_all | solution.py:122
  106.1 4.1 copy-start.8
  110.2 4.2 copy-start.1
  113.2 9.4 %collective-permute-start.9 = (bf16[512,5120]{1,0:T(8,128)(2,1)S(1)}, bf16[512,5120]{1,0:T(8,128)(2,1)S(1)}, u32[]{:S(2)}, u32[]{:S(2)}) collective-permute-start(bf16[512,5120]{1,0:T(8,128)(2,1)S(1)} %convolution_convert_fusion.2), channel_id=1, source_target_pairs={{0,16},{16,0},{1,17},{17,1},{2,18},{18,2},{3,19},{19,3},{4,20},{20... | collective-permute-start | bytes 15728648 | tf_op jit(solution)/shard_map/ppermute | solution.py:19
  122.8 16.0 %collective-permute-start.10 = (bf16[64,5120]{1,0:T(8,128)(2,1)S(1)}, bf16[64,5120]{1,0:T(8,128)(2,1)S(1)}, u32[]{:S(2)}, u32[]{:S(2)}) collective-permute-start(bf16[64,5120]{1,0:T(8,128)(2,1)S(1)} %add_convert_fusion.15), channel_id=1, source_target_pairs={{0,192},{64,0},{128,64},{192,128},{1,193},{65,1},{129,65},{193,129... | collective-permute-start | bytes 1966088 | tf_op jit(solution)/shard_map/ppermute | solution.py:19
  139.8 16.7 %copy-start.12 = (bf16[5120]{0:T(1024)(128)(2,1)S(1)}, bf16[5120]{0:T(1024)(128)(2,1)}, u32[]{:S(2)}) copy-start(bf16[5120]{0:T(1024)(128)(2,1)} %param.20) | copy-start | bytes 30724
  139.9 16.4 %collective-permute-start.14 = (bf16[64,5120]{1,0:T(8,128)(2,1)S(1)}, bf16[64,5120]{1,0:T(8,128)(2,1)S(1)}, u32[]{:S(2)}, u32[]{:S(2)}) collective-permute-start(bf16[64,5120]{1,0:T(8,128)(2,1)S(1)} %get-tuple-element.14), channel_id=1, source_target_pairs={{0,64},{64,128},{128,192},{192,0},{1,65},{65,129},{129,193},{193,1... | collective-permute-start | bytes 1966088 | tf_op jit(solution)/shard_map/ppermute | solution.py:19
  139.9 33.8 %copy-start.13 = (s32[1,64,1]{1,2,0:T(1,128)S(1)}, s32[1,64,1]{1,2,0:T(1,128)}, u32[]{:S(2)}) copy-start(s32[1,64,1]{1,2,0:T(1,128)} %param.22) | copy-start | bytes 772
  140.0 47.3 %copy-start.2 = (bf16[1,64,5120]{2,1,0:T(8,128)(2,1)S(1)}, bf16[1,64,5120]{2,1,0:T(8,128)(2,1)}, u32[]{:S(2)}) copy-start(bf16[1,64,5120]{2,1,0:T(8,128)(2,1)} %param.18) | copy-start | bytes 1966084
  140.0 19.2 %collective-permute-start.13 = (bf16[64,5120]{1,0:T(8,128)(2,1)S(1)}, bf16[64,5120]{1,0:T(8,128)(2,1)S(1)}, u32[]{:S(2)}, u32[]{:S(2)}) collective-permute-start(bf16[64,5120]{1,0:T(8,128)(2,1)S(1)} %get-tuple-element.15), channel_id=1, source_target_pairs={{0,192},{64,0},{128,64},{192,128},{1,193},{65,1},{129,65},{193,129... | collective-permute-start | bytes 1966088 | tf_op jit(solution)/shard_map/ppermute | solution.py:19
  156.4 15.5 %collective-permute-start.15 = (bf16[64,5120]{1,0:T(8,128)(2,1)S(1)}, bf16[64,5120]{1,0:T(8,128)(2,1)S(1)}, u32[]{:S(2)}, u32[]{:S(2)}) collective-permute-start(bf16[64,5120]{1,0:T(8,128)(2,1)S(1)} %add_convert_fusion.10), channel_id=1, source_target_pairs={{0,64},{64,128},{128,192},{192,0},{1,65},{65,129},{129,193},{193,1... | collective-permute-start | bytes 1966088 | tf_op jit(solution)/shard_map/ppermute | solution.py:19
  156.6 17.4 %collective-permute-start.11 = (bf16[64,5120]{1,0:T(8,128)(2,1)S(1)}, bf16[64,5120]{1,0:T(8,128)(2,1)S(1)}, u32[]{:S(2)}, u32[]{:S(2)}) collective-permute-start(bf16[64,5120]{1,0:T(8,128)(2,1)S(1)} %get-tuple-element.13), channel_id=1, source_target_pairs={{0,192},{64,0},{128,64},{192,128},{1,193},{65,1},{129,65},{193,129... | collective-permute-start | bytes 1966088 | tf_op jit(solution)/shard_map/ppermute | solution.py:19
  159.2 26.8 %collective-permute-start.12 = (bf16[64,5120]{1,0:T(8,128)(2,1)S(1)}, bf16[64,5120]{1,0:T(8,128)(2,1)S(1)}, u32[]{:S(2)}, u32[]{:S(2)}) collective-permute-start(bf16[64,5120]{1,0:T(8,128)(2,1)S(1)} %get-tuple-element.16), channel_id=1, source_target_pairs={{0,64},{64,128},{128,192},{192,0},{1,65},{65,129},{129,193},{193,1... | collective-permute-start | bytes 1966088 | tf_op jit(solution)/shard_map/ppermute | solution.py:19
  172.3 15.7 %copy-start.16 = (bf16[5120,16]{0,1:T(8,128)(2,1)S(1)}, bf16[5120,16]{0,1:T(8,128)(2,1)}, u32[]{:S(2)}) copy-start(bf16[5120,16]{0,1:T(8,128)(2,1)} %param.21) | copy-start | bytes 491524
  172.3 14.9 %collective-permute-start.16 = (bf16[64,5120]{1,0:T(8,128)(2,1)S(1)}, bf16[64,5120]{1,0:T(8,128)(2,1)S(1)}, u32[]{:S(2)}, u32[]{:S(2)}) collective-permute-start(bf16[64,5120]{1,0:T(8,128)(2,1)S(1)} %add_convert_fusion.9), channel_id=1, source_target_pairs={{0,32},{32,0},{1,33},{33,1},{2,34},{34,2},{3,35},{35,3},{4,36},{36... | collective-permute-start | bytes 1966088 | tf_op jit(solution)/shard_map/ppermute | solution.py:19
  251.3 21.6 %collective-permute-start.17 = (bf16[80,5120]{1,0:T(8,128)(2,1)}, bf16[80,5120]{1,0:T(8,128)(2,1)S(1)}, u32[]{:S(2)}, u32[]{:S(2)}) collective-permute-start(bf16[80,5120]{1,0:T(8,128)(2,1)} %reshape.262), channel_id=1, source_target_pairs={{0,32},{32,0},{1,33},{33,1},{2,34},{34,2},{3,35},{35,3},{4,36},{36... | collective-permute-start | bytes 2457608 | tf_op jit(solution)/shard_map/ppermute | solution.py:19
  251.3 24.4 %collective-permute-start.18 = (bf16[80,5120]{1,0:T(8,128)(2,1)}, bf16[80,5120]{1,0:T(8,128)(2,1)S(1)}, u32[]{:S(2)}, u32[]{:S(2)}) collective-permute-start(bf16[80,5120]{1,0:T(8,128)(2,1)} %reshape.262), channel_id=1, source_target_pairs={{0,64},{64,128},{128,192},{192,0},{1,65},{65,129},{129,193},{193,1... | collective-permute-start | bytes 2457608 | tf_op jit(solution)/shard_map/ppermute | solution.py:19
  252.7 33.1 %collective-permute-start.20 = (bf16[80,5120]{1,0:T(8,128)(2,1)}, bf16[80,5120]{1,0:T(8,128)(2,1)S(1)}, u32[]{:S(2)}, u32[]{:S(2)}) collective-permute-start(bf16[80,5120]{1,0:T(8,128)(2,1)} %reshape.262), channel_id=1, source_target_pairs={{0,192},{64,0},{128,64},{192,128},{1,193},{65,1},{129,65},{193,129... | collective-permute-start | bytes 2457608 | tf_op jit(solution)/shard_map/ppermute | solution.py:19
  272.9 12.7 %collective-permute-start.19 = (bf16[80,5120]{1,0:T(8,128)(2,1)S(1)}, bf16[80,5120]{1,0:T(8,128)(2,1)S(1)}, u32[]{:S(2)}, u32[]{:S(2)}) collective-permute-start(bf16[80,5120]{1,0:T(8,128)(2,1)S(1)} %collective-permute-done.17), channel_id=1, source_target_pairs={{0,64},{64,128},{128,192},{192,0},{1,65},{65,129},{129,193},{193,1... | collective-permute-start | bytes 2457608 | tf_op jit(solution)/shard_map/ppermute | solution.py:19
  272.9 13.0 %collective-permute-start.21 = (bf16[80,5120]{1,0:T(8,128)(2,1)S(1)}, bf16[80,5120]{1,0:T(8,128)(2,1)S(1)}, u32[]{:S(2)}, u32[]{:S(2)}) collective-permute-start(bf16[80,5120]{1,0:T(8,128)(2,1)S(1)} %collective-permute-done.17), channel_id=1, source_target_pairs={{0,192},{64,0},{128,64},{192,128},{1,193},{65,1},{129,65},{193,129... | collective-permute-start | bytes 2457608 | tf_op jit(solution)/shard_map/ppermute | solution.py:19
  288.6 43.9 %collective-permute-start.24 = (bf16[480,5120]{1,0:T(8,128)(2,1)S(1)}, bf16[480,5120]{1,0:T(8,128)(2,1)S(1)}, u32[]{:S(2)}, u32[]{:S(2)}) collective-permute-start(bf16[480,5120]{1,0:T(8,128)(2,1)S(1)} %get-tuple-element.20), channel_id=1, source_target_pairs={{0,16},{16,0},{1,17},{17,1},{2,18},{18,2},{3,19},{19,3},{4,20},{20... | collective-permute-start | bytes 14745608 | tf_op jit(solution)/shard_map/ppermute | solution.py:19
  310.3 21.0 %collective-permute-start.22 = (bf16[80,5120]{1,0:T(8,128)(2,1)S(1)}, bf16[80,5120]{1,0:T(8,128)(2,1)S(1)}, u32[]{:S(2)}, u32[]{:S(2)}) collective-permute-start(bf16[80,5120]{1,0:T(8,128)(2,1)S(1)} %collective-permute-done.18), channel_id=1, source_target_pairs={{0,64},{64,128},{128,192},{192,0},{1,65},{65,129},{129,193},{193,1... | collective-permute-start | bytes 2457608 | tf_op jit(solution)/shard_map/ppermute | solution.py:19
  310.3 21.0 %collective-permute-start.23 = (bf16[80,5120]{1,0:T(8,128)(2,1)S(1)}, bf16[80,5120]{1,0:T(8,128)(2,1)S(1)}, u32[]{:S(2)}, u32[]{:S(2)}) collective-permute-start(bf16[80,5120]{1,0:T(8,128)(2,1)S(1)} %collective-permute-done.21), channel_id=1, source_target_pairs={{0,192},{64,0},{128,64},{192,128},{1,193},{65,1},{129,65},{193,129... | collective-permute-start | bytes 2457608 | tf_op jit(solution)/shard_map/ppermute | solution.py:19
  331.4 4.1 collective-permute-start.25
  332.8 5.6 %copy-start.14 = (bf16[1,5120,256]{2,1,0:T(8,128)(2,1)S(1)}, bf16[1,5120,256]{2,1,0:T(8,128)(2,1)}, u32[]{:S(2)}) copy-start(bf16[1,5120,256]{2,1,0:T(8,128)(2,1)} %param.24) | copy-start | bytes 7864324
  354.5 5.0 copy-start.15
  354.5 24.0 %collective-permute-start.26 = (bf16[640,5120]{1,0:T(8,128)(2,1)}, bf16[640,5120]{1,0:T(8,128)(2,1)}, u32[]{:S(2)}, u32[]{:S(2)}) collective-permute-start(bf16[640,5120]{1,0:T(8,128)(2,1)} %convolution_convert_fusion), channel_id=1, source_target_pairs={{0,16},{16,0},{1,17},{17,1},{2,18},{18,2},{3,19},{19,3},{4,20},{20... | collective-permute-start | bytes 19660808 | tf_op jit(solution)/shard_map/ppermute | solution.py:19
  380.1 20.2 %collective-permute-start.27 = (bf16[80,5120]{1,0:T(8,128)(2,1)S(1)}, bf16[80,5120]{1,0:T(8,128)(2,1)S(1)}, u32[]{:S(2)}, u32[]{:S(2)}) collective-permute-start(bf16[80,5120]{1,0:T(8,128)(2,1)S(1)} %add_convert_fusion.7), channel_id=1, source_target_pairs={{0,192},{64,0},{128,64},{192,128},{1,193},{65,1},{129,65},{193,129... | collective-permute-start | bytes 2457608 | tf_op jit(solution)/shard_map/ppermute | solution.py:19
  404.4 20.9 %collective-permute-start.31 = (bf16[80,5120]{1,0:T(8,128)(2,1)S(1)}, bf16[80,5120]{1,0:T(8,128)(2,1)S(1)}, u32[]{:S(2)}, u32[]{:S(2)}) collective-permute-start(bf16[80,5120]{1,0:T(8,128)(2,1)S(1)} %get-tuple-element.10), channel_id=1, source_target_pairs={{0,64},{64,128},{128,192},{192,0},{1,65},{65,129},{129,193},{193,1... | collective-permute-start | bytes 2457608 | tf_op jit(solution)/shard_map/ppermute | solution.py:19
  404.9 25.0 %collective-permute-start.30 = (bf16[80,5120]{1,0:T(8,128)(2,1)S(1)}, bf16[80,5120]{1,0:T(8,128)(2,1)S(1)}, u32[]{:S(2)}, u32[]{:S(2)}) collective-permute-start(bf16[80,5120]{1,0:T(8,128)(2,1)S(1)} %get-tuple-element.11), channel_id=1, source_target_pairs={{0,192},{64,0},{128,64},{192,128},{1,193},{65,1},{129,65},{193,129... | collective-permute-start | bytes 2457608 | tf_op jit(solution)/shard_map/ppermute | solution.py:19
  427.0 19.3 %collective-permute-start.32 = (bf16[80,5120]{1,0:T(8,128)(2,1)S(1)}, bf16[80,5120]{1,0:T(8,128)(2,1)S(1)}, u32[]{:S(2)}, u32[]{:S(2)}) collective-permute-start(bf16[80,5120]{1,0:T(8,128)(2,1)S(1)} %add_convert_fusion.2), channel_id=1, source_target_pairs={{0,64},{64,128},{128,192},{192,0},{1,65},{65,129},{129,193},{193,1... | collective-permute-start | bytes 2457608 | tf_op jit(solution)/shard_map/ppermute | solution.py:19
  427.1 21.1 %collective-permute-start.28 = (bf16[80,5120]{1,0:T(8,128)(2,1)S(1)}, bf16[80,5120]{1,0:T(8,128)(2,1)S(1)}, u32[]{:S(2)}, u32[]{:S(2)}) collective-permute-start(bf16[80,5120]{1,0:T(8,128)(2,1)S(1)} %get-tuple-element.9), channel_id=1, source_target_pairs={{0,192},{64,0},{128,64},{192,128},{1,193},{65,1},{129,65},{193,129... | collective-permute-start | bytes 2457608 | tf_op jit(solution)/shard_map/ppermute | solution.py:19
  429.9 34.0 %collective-permute-start.29 = (bf16[80,5120]{1,0:T(8,128)(2,1)S(1)}, bf16[80,5120]{1,0:T(8,128)(2,1)S(1)}, u32[]{:S(2)}, u32[]{:S(2)}) collective-permute-start(bf16[80,5120]{1,0:T(8,128)(2,1)S(1)} %get-tuple-element.12), channel_id=1, source_target_pairs={{0,64},{64,128},{128,192},{192,0},{1,65},{65,129},{129,193},{193,1... | collective-permute-start | bytes 2457608 | tf_op jit(solution)/shard_map/ppermute | solution.py:19
  448.1 19.0 %collective-permute-start.33 = (bf16[80,5120]{1,0:T(8,128)(2,1)S(1)}, bf16[80,5120]{1,0:T(8,128)(2,1)S(1)}, u32[]{:S(2)}, u32[]{:S(2)}) collective-permute-start(bf16[80,5120]{1,0:T(8,128)(2,1)S(1)} %add_convert_fusion.1), channel_id=1, source_target_pairs={{0,32},{32,0},{1,33},{33,1},{2,34},{34,2},{3,35},{35,3},{4,36},{36... | collective-permute-start | bytes 2457608 | tf_op jit(solution)/shard_map/ppermute | solution.py:19
  472.4 58.2 %copy-start.4 = (bf16[64,5120]{1,0:T(8,128)(2,1)S(1)}, bf16[64,5120]{1,0:T(8,128)(2,1)}, u32[]{:S(2)}) copy-start(bf16[64,5120]{1,0:T(8,128)(2,1)} %copy-done.3) | copy-start | bytes 1966084
  (6 other events, 9.9 us)
Sparse Core Ops, SparseCore 0:
  19.3 71.4 all-gather.2

commit v4 on v3

--- a/solution.py
+++ b/solution.py
@@ -17,6 +17,14 @@
 
 def _pp(v, axis, n, shift):
     return lax.ppermute(v, axis, [(i, (i + shift) % n) for i in range(n)])
+
+
+def zswap(v):
+    h = v.shape[0] // 2
+    zz = ("zh", "zl")
+    up = _pp(_pp(v[:h], zz, 8, 2), zz, 8, 2)
+    down = _pp(_pp(v[h:], zz, 8, -2), zz, 8, -2)
+    return jnp.concatenate([up, down], 0)
 
 
 def rel_index():
@@ -32,7 +40,7 @@
 
 
 def ag_rel(b):
-    zo = _pp(b, "zh", 2, 1)
+    zo = zswap(b)
     l1 = _pp(b, "x", 4, 1)
     r1 = _pp(b, "x", 4, -1)
     l1o = _pp(zo, "x", 4, 1)
@@ -55,7 +63,7 @@
     e = _pp((blk[5] + b.astype(jnp.float32)).astype(jnp.bfloat16), "x", 4, 1)
     f = _pp((blk[2] + a.astype(jnp.float32)).astype(jnp.bfloat16), "x", 4, -1)
     t1 = blk[1] + c.astype(jnp.float32) + e.astype(jnp.float32)
-    z = _pp(t1.astype(jnp.bfloat16), "zh", 2, 1)
+    z = zswap(t1.astype(jnp.bfloat16))
     t0 = blk[0] + f.astype(jnp.float32) + d.astype(jnp.float32)
     return t0 + z.astype(jnp.float32)
 

time: 548 us -> 571 us (1.042)
  waiting for transfers between devices: 210 us -> 281 us
  blocking collectives: 118 us -> 76.1 us
  starting transfers between devices: 82.6 us -> 73.7 us
    ppermute x34 -> x46, waiting for transfers between devices: 196 us -> 266 us  [_pp(): return lax.ppermute(v, axis, [(i, (i + shift) % n) for i in range(n)])]
    all_to_all x1, blocking collectives: 59.7 us -> 35.7 us  [local(): lax.all_to_all(outgoing, EXP, split_axis=0, concat_axis=0, tiled=True)]
    all_to_all x1, blocking collectives: 58.2 us -> 40.4 us  [local(): lax.all_to_all(expert_out, EXP, split_axis=0, concat_axis=0, tiled=True)]
    all_to_all x1, starting transfers between devices: 12.8 us -> 6.19 us  [local(): lax.all_to_all(attended.reshape(tok_rows, n_ctx, qwidth // n_ctx), CTX, s...]
    ppermute x34 -> x46, starting transfers between devices: 69.8 us -> 67.5 us  [_pp(): return lax.ppermute(v, axis, [(i, (i + shift) % n) for i in range(n)])]
    unnamed x47 -> x50, local copies, waits for them, and re-layouts: 16.9 us -> 14.9 us
  transfers between devices with their start and end apart: 36 -> 48, of which waited for: 20 -> 27; matrix products, arithmetic and copies ran while one was open for 12% -> 12% of each run, Pallas kernels for 0% -> 0%
where the time goes in v4:
time: 571 us; the launch traced here: 562 us
  waiting for transfers between devices  281 us (49%)
  blocking collectives  76.1 us (13%)
  starting transfers between devices  73.7 us (13%)
  matrix products  50.1 us (9%)
  local copies, waits for them, and re-layouts  47.5 us (8%)
  other arithmetic  19.2 us (3%)
  between operations  14.4 us (3%)
    ppermute x46, waiting for transfers between devices, _pp(): return lax.ppermute(v, axis, [(i, (i + shift) % n) for i in range(n)])  266 us
    ppermute x46, starting transfers between devices, _pp(): return lax.ppermute(v, axis, [(i, (i + shift) % n) for i in range(n)])  67.5 us
    all_to_all x1, blocking collectives, local(): lax.all_to_all(expert_out, EXP, split_axis=0, concat_axis=0, tiled=True)  40.4 us
    all_to_all x1, blocking collectives, local(): lax.all_to_all(outgoing, EXP, split_axis=0, concat_axis=0, tiled=True)  35.7 us
    dot_general x2, matrix products, expert_rows(): jnp.dot(inner, down_local, preferred_element_type=jnp.float32)  26.7 us
    all_to_all x1, waiting for transfers between devices, local(): lax.all_to_all(attended.reshape(tok_rows, n_ctx, qwidth // n_ctx), CTX, s...  15.7 us
    unnamed x50, local copies, waits for them, and re-layouts  14.9 us
  transfers between devices with their start and end apart: 48, of which 27 were waited for; matrix products, arithmetic and copies ran while one was open for 12% of the time, Pallas kernels for 0%

profile of v4, /device:TPU:1, one launch (start us, length us, event | category | flops | bytes accessed | tf_op | source)
XLA Modules:
  0.0 562.3 jit_solution(5046420706631073637)
XLA Ops:
  9.5 3.8 collective-permute-start
  13.3 3.0 collective-permute-start.2
  19.2 5.0 collective-permute-done
  24.2 4.7 collective-permute-start.1
  32.6 10.1 %collective-permute-done.1 = bf16[32,1024]{0,1:T(8,128)(2,1)S(1)} collective-permute-done((bf16[32,1024]{0,1:T(8,128)(2,1)}, bf16[32,1024]{0,1:T(8,128)(2,1)S(1)}, u32[]{:S(2)}, u32[]{:S(2)}) %collective-permute-start.1) | collective-permute-done | bytes 65568 | tf_op jit(solution)/shard_map/ppermute | solution.py:19
  42.6 7.2 %collective-permute-done.3 = bf16[32,1024]{0,1:T(8,128)(2,1)S(1)} collective-permute-done((bf16[32,1024]{0,1:T(8,128)(2,1)}, bf16[32,1024]{0,1:T(8,128)(2,1)S(1)}, u32[]{:S(2)}, u32[]{:S(2)}) %collective-permute-start.3) | collective-permute-done | bytes 65568 | tf_op jit(solution)/shard_map/ppermute | solution.py:19
  52.6 4.8 collective-permute-done.7
  57.4 3.2 collective-permute-done.5
  60.6 4.0 concatenate.78
  69.6 6.3 %collective-permute-done.8 = bf16[64,1024]{0,1:T(8,128)(2,1)} collective-permute-done((bf16[64,1024]{0,1:T(8,128)(2,1)}, bf16[64,1024]{0,1:T(8,128)(2,1)}, u32[]{:S(2)}, u32[]{:S(2)}) %collective-permute-start.8) | collective-permute-done | bytes 131104 | tf_op jit(solution)/shard_map/ppermute | solution.py:19
  81.3 5.8 %concatenate.80 = bf16[1024,1024]{0,1:T(8,128)(2,1)} concatenate(bf16[64,1024]{0,1:T(8,128)(2,1)S(1)} %pad_maximum_fusion.1, bf16[32,1024]{0,1:T(8,128)(2,1)S(1)} %collective-permute-done.1, bf16[32,1024]{0,1:T(8,128)(2,1)S(1)} %collective-permute-done.3, bf16[64,1024]{0,1:T(8,128)(2,1)} %collective-permute-done.4, bf16[64,1024]{0,1:T(8,128)(2,1)} %collective-permute-done.5, ...), dimensions={0} | concatenate | bytes 4194304 | tf_op jit(solution)/shard_map/concatenate | solution.py:52
  87.1 3.1 fusion.88
  90.2 4.9 fusion.93
  95.1 2.9 fusion.26
  101.6 6.2 %all-to-all-start = ((bf16[64,16,160]{2,0,1:T(8,128)(2,1)}), bf16[64,16,160]{2,0,1:T(8,128)(2,1)S(1)}, u32[]{:S(2)}, u32[]{:S(2)}) async-start(bf16[64,16,160]{2,0,1:T(8,128)(2,1)} %copy.43), calls=%async_computation | async-start | bytes 1048576 | tf_op jit(solution)/shard_map/all_to_all | solution.py:130
  108.0 15.7 %all-to-all-done = bf16[64,16,160]{2,0,1:T(8,128)(2,1)S(1)} async-done(((bf16[64,16,160]{2,0,1:T(8,128)(2,1)}), bf16[64,16,160]{2,0,1:T(8,128)(2,1)S(1)}, u32[]{:S(2)}, u32[]{:S(2)}) %all-to-all-start) | async-done | bytes 327712 | tf_op jit(solution)/shard_map/all_to_all | solution.py:130
  126.3 4.1 reshape.276
  130.3 3.1 convolution_convert_fusion.2
  136.2 6.8 %collective-permute-done.12 = bf16[512,5120]{1,0:T(8,128)(2,1)S(1)} collective-permute-done((bf16[512,5120]{1,0:T(8,128)(2,1)S(1)}, bf16[512,5120]{1,0:T(8,128)(2,1)S(1)}, u32[]{:S(2)}, u32[]{:S(2)}) %collective-permute-start.12) | collective-permute-done | bytes 5242912 | tf_op jit(solution)/shard_map/ppermute | solution.py:19
  143.7 15.3 %collective-permute-done.13 = bf16[64,5120]{1,0:T(8,128)(2,1)S(1)} collective-permute-done((bf16[64,5120]{1,0:T(8,128)(2,1)S(1)}, bf16[64,5120]{1,0:T(8,128)(2,1)S(1)}, u32[]{:S(2)}, u32[]{:S(2)}) %collective-permute-start.13) | collective-permute-done | bytes 655392 | tf_op jit(solution)/shard_map/ppermute | solution.py:19
  160.2 3.1 collective-permute-start.16
  163.3 13.2 %collective-permute-done.17 = bf16[64,5120]{1,0:T(8,128)(2,1)S(1)} collective-permute-done((bf16[64,5120]{1,0:T(8,128)(2,1)S(1)}, bf16[64,5120]{1,0:T(8,128)(2,1)S(1)}, u32[]{:S(2)}, u32[]{:S(2)}) %collective-permute-start.17) | collective-permute-done | bytes 655392 | tf_op jit(solution)/shard_map/ppermute | solution.py:19
  176.8 15.4 %collective-permute-done.18 = bf16[64,5120]{1,0:T(8,128)(2,1)S(1)} collective-permute-done((bf16[64,5120]{1,0:T(8,128)(2,1)S(1)}, bf16[64,5120]{1,0:T(8,128)(2,1)S(1)}, u32[]{:S(2)}, u32[]{:S(2)}) %collective-permute-start.18) | collective-permute-done | bytes 655392 | tf_op jit(solution)/shard_map/ppermute | solution.py:19
  192.7 3.6 collective-permute-start.21
  198.0 10.2 %collective-permute-done.19 = bf16[32,5120]{1,0:T(8,128)(2,1)S(1)} collective-permute-done((bf16[32,5120]{1,0:T(8,128)(2,1)S(1)}, bf16[32,5120]{1,0:T(8,128)(2,1)S(1)}, u32[]{:S(2)}, u32[]{:S(2)}) %collective-permute-start.19) | collective-permute-done | bytes 327712 | tf_op jit(solution)/shard_map/ppermute | solution.py:19
  208.8 3.0 collective-permute-start.22
  211.8 14.8 %collective-permute-done.20 = bf16[32,5120]{1,0:T(8,128)(2,1)S(1)} collective-permute-done((bf16[32,5120]{1,0:T(8,128)(2,1)S(1)}, bf16[32,5120]{1,0:T(8,128)(2,1)S(1)}, u32[]{:S(2)}, u32[]{:S(2)}) %collective-permute-start.20) | collective-permute-done | bytes 327712 | tf_op jit(solution)/shard_map/ppermute | solution.py:19
  228.8 35.7 %all_to_all.25 = bf16[16,5,5120]{2,1,0:T(8,128)(2,1)S(1)} all-to-all(bf16[16,5,5120]{2,1,0:T(8,128)(2,1)S(1)} %copy.44), channel_id=1, replica_groups=mesh['x'=4,'zh'=2,'core'=2,'zl'=4,'y'=4] {'zl','y'}, dimensions={0} | all-to-all | bytes 1638400 | tf_op jit(solution)/shard_map/all_to_all | solution.py:165
  276.9 8.6 %collective-permute-done.23 = bf16[40,5120]{1,0:T(8,128)(2,1)} collective-permute-done((bf16[40,5120]{1,0:T(8,128)(2,1)}, bf16[40,5120]{1,0:T(8,128)(2,1)}, u32[]{:S(2)}, u32[]{:S(2)}) %collective-permute-start.23) | collective-permute-done | bytes 409632 | tf_op jit(solution)/shard_map/ppermute | solution.py:19
  287.0 6.2 %collective-permute-done.25 = bf16[40,5120]{1,0:T(8,128)(2,1)} collective-permute-done((bf16[40,5120]{1,0:T(8,128)(2,1)}, bf16[40,5120]{1,0:T(8,128)(2,1)}, u32[]{:S(2)}, u32[]{:S(2)}) %collective-permute-start.25) | collective-permute-done | bytes 409632 | tf_op jit(solution)/shard_map/ppermute | solution.py:19
  293.2 2.9 collective-permute-start.26
  297.7 15.6 %collective-permute-done.26 = bf16[40,5120]{1,0:T(8,128)(2,1)S(1)} collective-permute-done((bf16[40,5120]{1,0:T(8,128)(2,1)}, bf16[40,5120]{1,0:T(8,128)(2,1)S(1)}, u32[]{:S(2)}, u32[]{:S(2)}) %collective-permute-start.26) | collective-permute-done | bytes 409632 | tf_op jit(solution)/shard_map/ppermute | solution.py:19
  316.4 17.6 %collective-permute-done.28 = bf16[80,5120]{1,0:T(8,128)(2,1)S(1)} collective-permute-done((bf16[80,5120]{1,0:T(8,128)(2,1)S(1)}, bf16[80,5120]{1,0:T(8,128)(2,1)S(1)}, u32[]{:S(2)}, u32[]{:S(2)}) %collective-permute-start.28) | collective-permute-done | bytes 819232 | tf_op jit(solution)/shard_map/ppermute | solution.py:19
  334.3 16.7 %collective-permute-done.30 = bf16[80,5120]{1,0:T(8,128)(2,1)S(1)} collective-permute-done((bf16[80,5120]{1,0:T(8,128)(2,1)S(1)}, bf16[80,5120]{1,0:T(8,128)(2,1)S(1)}, u32[]{:S(2)}, u32[]{:S(2)}) %collective-permute-start.30) | collective-permute-done | bytes 819232 | tf_op jit(solution)/shard_map/ppermute | solution.py:19
  353.0 2.8 collective-permute-start.32
  355.9 18.5 %collective-permute-done.31 = bf16[80,5120]{1,0:T(8,128)(2,1)S(1)} collective-permute-done((bf16[80,5120]{1,0:T(8,128)(2,1)S(1)}, bf16[80,5120]{1,0:T(8,128)(2,1)S(1)}, u32[]{:S(2)}, u32[]{:S(2)}) %collective-permute-start.31) | collective-permute-done | bytes 819232 | tf_op jit(solution)/shard_map/ppermute | solution.py:19
  375.9 2.7 collective-permute-done.34
  378.7 2.8 copy-done.7
  384.2 13.4 %convolution_convert_fusion = bf16[640,5120]{1,0:T(8,128)(2,1)} fusion(bf16[1,256,5120]{2,1,0:T(8,128)(2,1)S(1)} %copy-done, f32[640,256]{1,0:T(8,128)} %fusion.7, bf16[640,5120]{1,0:T(8,128)(2,1)} %copy-done.7, bf16[1,5120,256]{2,1,0:T(8,128)(2,1)} %param.23), kind=kOutput, calls=%fused_computation.2 | convolution fusion | flops 3359703040 | bytes 19005440 | tf_op jit(solution)/shard_map/dot_general | solution.py:177
  402.6 5.6 fusion.9
  408.2 13.4 %convolution_convert_fusion.1 = bf16[640,5120]{1,0:T(8,128)(2,1)} fusion(bf16[1,256,5120]{2,1,0:T(8,128)(2,1)S(1)} %copy-done, f32[640,256]{1,0:T(8,128)} %fusion.9, bf16[640,5120]{1,0:T(8,128)(2,1)} %constant_dynamic-update-slice_fusion.2, bf16[1,5120,256]{2,1,0:T(8,128)(2,1)} %param.23), kind=kOutput, calls=%fused_computation.3 | convolution fusion | flops 3359703040 | bytes 19005440 | tf_op jit(solution)/shard_map/dot_general | solution.py:177
  426.9 18.1 %collective-permute-done.40 = bf16[80,5120]{1,0:T(8,128)(2,1)S(1)} collective-permute-done((bf16[80,5120]{1,0:T(8,128)(2,1)S(1)}, bf16[80,5120]{1,0:T(8,128)(2,1)S(1)}, u32[]{:S(2)}, u32[]{:S(2)}) %collective-permute-start.40) | collective-permute-done | bytes 819232 | tf_op jit(solution)/shard_map/ppermute | solution.py:19
  446.8 20.0 %collective-permute-done.41 = bf16[80,5120]{1,0:T(8,128)(2,1)S(1)} collective-permute-done((bf16[80,5120]{1,0:T(8,128)(2,1)S(1)}, bf16[80,5120]{1,0:T(8,128)(2,1)S(1)}, u32[]{:S(2)}, u32[]{:S(2)}) %collective-permute-start.41) | collective-permute-done | bytes 819232 | tf_op jit(solution)/shard_map/ppermute | solution.py:19
  469.9 3.7 collective-permute-start.42
  475.1 12.5 %collective-permute-done.36 = bf16[80,5120]{1,0:T(8,128)(2,1)S(1)} collective-permute-done((bf16[80,5120]{1,0:T(8,128)(2,1)S(1)}, bf16[80,5120]{1,0:T(8,128)(2,1)S(1)}, u32[]{:S(2)}, u32[]{:S(2)}) %collective-permute-start.36) | collective-permute-done | bytes 819232 | tf_op jit(solution)/shard_map/ppermute | solution.py:19
  490.6 3.4 collective-permute-start.43
  494.1 13.9 %collective-permute-done.43 = bf16[40,5120]{1,0:T(8,128)(2,1)S(1)} collective-permute-done((bf16[40,5120]{1,0:T(8,128)(2,1)S(1)}, bf16[40,5120]{1,0:T(8,128)(2,1)S(1)}, u32[]{:S(2)}, u32[]{:S(2)}) %collective-permute-start.43) | collective-permute-done | bytes 409632 | tf_op jit(solution)/shard_map/ppermute | solution.py:19
  513.0 40.4 %all_to_all.26 = bf16[16,5,5120]{2,1,0:T(8,128)(2,1)S(1)} all-to-all(bf16[16,5,5120]{2,1,0:T(8,128)(2,1)} %reshape.265), channel_id=1, replica_groups=mesh['x'=4,'zh'=2,'core'=2,'zl'=4,'y'=4] {'zl','y'}, dimensions={0} | all-to-all | bytes 1638400 | tf_op jit(solution)/shard_map/all_to_all | solution.py:183
  (169 shorter events, 90.4 us)
Async XLA Ops:
  6.5 119.7 %all-gather.3.cloned.1.call-start = ((), (), s32[]{:S(2)}) async-start(), calls=%async_computation.3 | async-start | bytes 2785280 | tf_op jit(solution)/shard_map/all_gather | solution.py:129
  9.5 14.7 %collective-permute-start = (bf16[32,1024]{0,1:T(8,128)(2,1)}, bf16[32,1024]{0,1:T(8,128)(2,1)}, u32[]{:S(2)}, u32[]{:S(2)}) collective-permute-start(bf16[32,1024]{0,1:T(8,128)(2,1)} %get-tuple-element.45), channel_id=1, source_target_pairs={{0,8},{4,12},{8,32},{12,36},{32,40},{36,44},{40,0},{44,4},{1,9},{5... | collective-permute-start | bytes 196616 | tf_op jit(solution)/shard_map/ppermute | solution.py:19
  13.3 16.2 %collective-permute-start.2 = (bf16[32,1024]{0,1:T(8,128)(2,1)S(1)}, bf16[32,1024]{0,1:T(8,128)(2,1)}, u32[]{:S(2)}, u32[]{:S(2)}) collective-permute-start(bf16[32,1024]{0,1:T(8,128)(2,1)S(1)} %get-tuple-element.44), channel_id=1, source_target_pairs={{0,40},{4,44},{8,0},{12,4},{32,8},{36,12},{40,32},{44,36},{1,41},{... | collective-permute-start | bytes 196616 | tf_op jit(solution)/shard_map/ppermute | solution.py:19
  16.4 36.2 %collective-permute-start.4 = (bf16[64,1024]{0,1:T(8,128)(2,1)S(1)}, bf16[64,1024]{0,1:T(8,128)(2,1)}, u32[]{:S(2)}, u32[]{:S(2)}) collective-permute-start(bf16[64,1024]{0,1:T(8,128)(2,1)S(1)} %pad_maximum_fusion.1), channel_id=1, source_target_pairs={{0,64},{64,128},{128,192},{192,0},{1,65},{65,129},{129,193},{193,1... | collective-permute-start | bytes 393224 | tf_op jit(solution)/shard_map/ppermute | solution.py:19
  17.7 34.9 %collective-permute-start.6 = (bf16[64,1024]{0,1:T(8,128)(2,1)S(1)}, bf16[64,1024]{0,1:T(8,128)(2,1)}, u32[]{:S(2)}, u32[]{:S(2)}) collective-permute-start(bf16[64,1024]{0,1:T(8,128)(2,1)S(1)} %pad_maximum_fusion.1), channel_id=1, source_target_pairs={{0,192},{64,0},{128,64},{192,128},{1,193},{65,1},{129,65},{193,129... | collective-permute-start | bytes 393224 | tf_op jit(solution)/shard_map/ppermute | solution.py:19
  24.2 18.4 %collective-permute-start.1 = (bf16[32,1024]{0,1:T(8,128)(2,1)}, bf16[32,1024]{0,1:T(8,128)(2,1)S(1)}, u32[]{:S(2)}, u32[]{:S(2)}) collective-permute-start(bf16[32,1024]{0,1:T(8,128)(2,1)} %collective-permute-done), channel_id=1, source_target_pairs={{0,8},{4,12},{8,32},{12,36},{32,40},{36,44},{40,0},{44,4},{1,9},{5... | collective-permute-start | bytes 196616 | tf_op jit(solution)/shard_map/ppermute | solution.py:19
  29.5 20.3 %collective-permute-start.3 = (bf16[32,1024]{0,1:T(8,128)(2,1)}, bf16[32,1024]{0,1:T(8,128)(2,1)S(1)}, u32[]{:S(2)}, u32[]{:S(2)}) collective-permute-start(bf16[32,1024]{0,1:T(8,128)(2,1)} %collective-permute-done.2), channel_id=1, source_target_pairs={{0,40},{4,44},{8,0},{12,4},{32,8},{36,12},{40,32},{44,36},{1,41},{... | collective-permute-start | bytes 196616 | tf_op jit(solution)/shard_map/ppermute | solution.py:19
  50.0 7.4 %collective-permute-start.7 = (bf16[64,1024]{0,1:T(8,128)(2,1)S(1)}, bf16[64,1024]{0,1:T(8,128)(2,1)}, u32[]{:S(2)}, u32[]{:S(2)}) collective-permute-start(bf16[64,1024]{0,1:T(8,128)(2,1)S(1)} %pad_maximum_fusion.2), channel_id=1, source_target_pairs={{0,192},{64,0},{128,64},{192,128},{1,193},{65,1},{129,65},{193,129... | collective-permute-start | bytes 393224 | tf_op jit(solution)/shard_map/ppermute | solution.py:19
  52.5 8.1 %collective-permute-start.5 = (bf16[64,1024]{0,1:T(8,128)(2,1)S(1)}, bf16[64,1024]{0,1:T(8,128)(2,1)}, u32[]{:S(2)}, u32[]{:S(2)}) collective-permute-start(bf16[64,1024]{0,1:T(8,128)(2,1)S(1)} %pad_maximum_fusion.2), channel_id=1, source_target_pairs={{0,64},{64,128},{128,192},{192,0},{1,65},{65,129},{129,193},{193,1... | collective-permute-start | bytes 393224 | tf_op jit(solution)/shard_map/ppermute | solution.py:19
  64.6 16.7 %collective-permute-start.10 = (bf16[384,1024]{0,1:T(8,128)(2,1)}, bf16[384,1024]{0,1:T(8,128)(2,1)}, u32[]{:S(2)}, u32[]{:S(2)}) collective-permute-start(bf16[384,1024]{0,1:T(8,128)(2,1)} %concatenate.78), channel_id=1, source_target_pairs={{0,16},{16,0},{1,17},{17,1},{2,18},{18,2},{3,19},{19,3},{4,20},{20... | collective-permute-start | bytes 2359304 | tf_op jit(solution)/shard_map/ppermute | solution.py:19
  66.6 9.4 %collective-permute-start.8 = (bf16[64,1024]{0,1:T(8,128)(2,1)}, bf16[64,1024]{0,1:T(8,128)(2,1)}, u32[]{:S(2)}, u32[]{:S(2)}) collective-permute-start(bf16[64,1024]{0,1:T(8,128)(2,1)} %collective-permute-done.4), channel_id=1, source_target_pairs={{0,64},{64,128},{128,192},{192,0},{1,65},{65,129},{129,193},{193,1... | collective-permute-start | bytes 393224 | tf_op jit(solution)/shard_map/ppermute | solution.py:19
  66.6 9.4 %collective-permute-start.9 = (bf16[64,1024]{0,1:T(8,128)(2,1)}, bf16[64,1024]{0,1:T(8,128)(2,1)}, u32[]{:S(2)}, u32[]{:S(2)}) collective-permute-start(bf16[64,1024]{0,1:T(8,128)(2,1)} %collective-permute-done.7), channel_id=1, source_target_pairs={{0,192},{64,0},{128,64},{192,128},{1,193},{65,1},{129,65},{193,129... | collective-permute-start | bytes 393224 | tf_op jit(solution)/shard_map/ppermute | solution.py:19
  77.8 3.4 collective-permute-start.11
  101.6 22.0 %all-to-all-start = ((bf16[64,16,160]{2,0,1:T(8,128)(2,1)}), bf16[64,16,160]{2,0,1:T(8,128)(2,1)S(1)}, u32[]{:S(2)}, u32[]{:S(2)}) async-start(bf16[64,16,160]{2,0,1:T(8,128)(2,1)} %copy.43), calls=%async_computation | async-start | bytes 1048576 | tf_op jit(solution)/shard_map/all_to_all | solution.py:130
  133.4 9.5 %collective-permute-start.12 = (bf16[512,5120]{1,0:T(8,128)(2,1)S(1)}, bf16[512,5120]{1,0:T(8,128)(2,1)S(1)}, u32[]{:S(2)}, u32[]{:S(2)}) collective-permute-start(bf16[512,5120]{1,0:T(8,128)(2,1)S(1)} %convolution_convert_fusion.2), channel_id=1, source_target_pairs={{0,16},{16,0},{1,17},{17,1},{2,18},{18,2},{3,19},{19,3},{4,20},{20... | collective-permute-start | bytes 15728648 | tf_op jit(solution)/shard_map/ppermute | solution.py:19
  143.1 16.0 %collective-permute-start.13 = (bf16[64,5120]{1,0:T(8,128)(2,1)S(1)}, bf16[64,5120]{1,0:T(8,128)(2,1)S(1)}, u32[]{:S(2)}, u32[]{:S(2)}) collective-permute-start(bf16[64,5120]{1,0:T(8,128)(2,1)S(1)} %add_convert_fusion.15), channel_id=1, source_target_pairs={{0,192},{64,0},{128,64},{192,128},{1,193},{65,1},{129,65},{193,129... | collective-permute-start | bytes 1966088 | tf_op jit(solution)/shard_map/ppermute | solution.py:19
  160.1 16.4 %collective-permute-start.17 = (bf16[64,5120]{1,0:T(8,128)(2,1)S(1)}, bf16[64,5120]{1,0:T(8,128)(2,1)S(1)}, u32[]{:S(2)}, u32[]{:S(2)}) collective-permute-start(bf16[64,5120]{1,0:T(8,128)(2,1)S(1)} %get-tuple-element.15), channel_id=1, source_target_pairs={{0,64},{64,128},{128,192},{192,0},{1,65},{65,129},{129,193},{193,1... | collective-permute-start | bytes 1966088 | tf_op jit(solution)/shard_map/ppermute | solution.py:19
  160.2 16.6 %collective-permute-start.16 = (bf16[64,5120]{1,0:T(8,128)(2,1)S(1)}, bf16[64,5120]{1,0:T(8,128)(2,1)S(1)}, u32[]{:S(2)}, u32[]{:S(2)}) collective-permute-start(bf16[64,5120]{1,0:T(8,128)(2,1)S(1)} %get-tuple-element.16), channel_id=1, source_target_pairs={{0,192},{64,0},{128,64},{192,128},{1,193},{65,1},{129,65},{193,129... | collective-permute-start | bytes 1966088 | tf_op jit(solution)/shard_map/ppermute | solution.py:19
  176.7 15.5 %collective-permute-start.18 = (bf16[64,5120]{1,0:T(8,128)(2,1)S(1)}, bf16[64,5120]{1,0:T(8,128)(2,1)S(1)}, u32[]{:S(2)}, u32[]{:S(2)}) collective-permute-start(bf16[64,5120]{1,0:T(8,128)(2,1)S(1)} %add_convert_fusion.10), channel_id=1, source_target_pairs={{0,64},{64,128},{128,192},{192,0},{1,65},{65,129},{129,193},{193,1... | collective-permute-start | bytes 1966088 | tf_op jit(solution)/shard_map/ppermute | solution.py:19
  192.6 15.6 %collective-permute-start.19 = (bf16[32,5120]{1,0:T(8,128)(2,1)S(1)}, bf16[32,5120]{1,0:T(8,128)(2,1)S(1)}, u32[]{:S(2)}, u32[]{:S(2)}) collective-permute-start(bf16[32,5120]{1,0:T(8,128)(2,1)S(1)} %get-tuple-element.34), channel_id=1, source_target_pairs={{0,8},{4,12},{8,32},{12,36},{32,40},{36,44},{40,0},{44,4},{1,9},{5... | collective-permute-start | bytes 983048 | tf_op jit(solution)/shard_map/ppermute | solution.py:19
  192.7 16.1 %collective-permute-start.21 = (bf16[32,5120]{1,0:T(8,128)(2,1)S(1)}, bf16[32,5120]{1,0:T(8,128)(2,1)S(1)}, u32[]{:S(2)}, u32[]{:S(2)}) collective-permute-start(bf16[32,5120]{1,0:T(8,128)(2,1)S(1)} %get-tuple-element.35), channel_id=1, source_target_pairs={{0,40},{4,44},{8,0},{12,4},{32,8},{36,12},{40,32},{44,36},{1,41},{... | collective-permute-start | bytes 983048 | tf_op jit(solution)/shard_map/ppermute | solution.py:19
  196.3 15.5 %collective-permute-start.14 = (bf16[64,5120]{1,0:T(8,128)(2,1)S(1)}, bf16[64,5120]{1,0:T(8,128)(2,1)S(1)}, u32[]{:S(2)}, u32[]{:S(2)}) collective-permute-start(bf16[64,5120]{1,0:T(8,128)(2,1)S(1)} %get-tuple-element.14), channel_id=1, source_target_pairs={{0,192},{64,0},{128,64},{192,128},{1,193},{65,1},{129,65},{193,129... | collective-permute-start | bytes 1966088 | tf_op jit(solution)/shard_map/ppermute | solution.py:19
  196.3 15.6 %collective-permute-start.15 = (bf16[64,5120]{1,0:T(8,128)(2,1)S(1)}, bf16[64,5120]{1,0:T(8,128)(2,1)S(1)}, u32[]{:S(2)}, u32[]{:S(2)}) collective-permute-start(bf16[64,5120]{1,0:T(8,128)(2,1)S(1)} %get-tuple-element.17), channel_id=1, source_target_pairs={{0,64},{64,128},{128,192},{192,0},{1,65},{65,129},{129,193},{193,1... | collective-permute-start | bytes 1966088 | tf_op jit(solution)/shard_map/ppermute | solution.py:19
  208.2 18.5 %collective-permute-start.20 = (bf16[32,5120]{1,0:T(8,128)(2,1)S(1)}, bf16[32,5120]{1,0:T(8,128)(2,1)S(1)}, u32[]{:S(2)}, u32[]{:S(2)}) collective-permute-start(bf16[32,5120]{1,0:T(8,128)(2,1)S(1)} %collective-permute-done.19), channel_id=1, source_target_pairs={{0,8},{4,12},{8,32},{12,36},{32,40},{36,44},{40,0},{44,4},{1,9},{5... | collective-permute-start | bytes 983048 | tf_op jit(solution)/shard_map/ppermute | solution.py:19
  208.8 17.9 %collective-permute-start.22 = (bf16[32,5120]{1,0:T(8,128)(2,1)S(1)}, bf16[32,5120]{1,0:T(8,128)(2,1)S(1)}, u32[]{:S(2)}, u32[]{:S(2)}) collective-permute-start(bf16[32,5120]{1,0:T(8,128)(2,1)S(1)} %collective-permute-done.21), channel_id=1, source_target_pairs={{0,40},{4,44},{8,0},{12,4},{32,8},{36,12},{40,32},{44,36},{1,41},{... | collective-permute-start | bytes 983048 | tf_op jit(solution)/shard_map/ppermute | solution.py:19
  268.8 16.7 %collective-permute-start.23 = (bf16[40,5120]{1,0:T(8,128)(2,1)}, bf16[40,5120]{1,0:T(8,128)(2,1)}, u32[]{:S(2)}, u32[]{:S(2)}) collective-permute-start(bf16[40,5120]{1,0:T(8,128)(2,1)} %slice.175), channel_id=1, source_target_pairs={{0,8},{4,12},{8,32},{12,36},{32,40},{36,44},{40,0},{44,4},{1,9},{5... | collective-permute-start | bytes 1228808 | tf_op jit(solution)/shard_map/ppermute | solution.py:19
  272.5 20.6 %collective-permute-start.25 = (bf16[40,5120]{1,0:T(8,128)(2,1)}, bf16[40,5120]{1,0:T(8,128)(2,1)}, u32[]{:S(2)}, u32[]{:S(2)}) collective-permute-start(bf16[40,5120]{1,0:T(8,128)(2,1)} %slice.177), channel_id=1, source_target_pairs={{0,40},{4,44},{8,0},{12,4},{32,8},{36,12},{40,32},{44,36},{1,41},{... | collective-permute-start | bytes 1228808 | tf_op jit(solution)/shard_map/ppermute | solution.py:19
  276.7 39.5 %collective-permute-start.27 = (bf16[80,5120]{1,0:T(8,128)(2,1)}, bf16[80,5120]{1,0:T(8,128)(2,1)S(1)}, u32[]{:S(2)}, u32[]{:S(2)}) collective-permute-start(bf16[80,5120]{1,0:T(8,128)(2,1)} %reshape.264), channel_id=1, source_target_pairs={{0,64},{64,128},{128,192},{192,0},{1,65},{65,129},{129,193},{193,1... | collective-permute-start | bytes 2457608 | tf_op jit(solution)/shard_map/ppermute | solution.py:19
  285.5 12.1 %collective-permute-start.24 = (bf16[40,5120]{1,0:T(8,128)(2,1)}, bf16[40,5120]{1,0:T(8,128)(2,1)S(1)}, u32[]{:S(2)}, u32[]{:S(2)}) collective-permute-start(bf16[40,5120]{1,0:T(8,128)(2,1)} %collective-permute-done.23), channel_id=1, source_target_pairs={{0,8},{4,12},{8,32},{12,36},{32,40},{36,44},{40,0},{44,4},{1,9},{5... | collective-permute-start | bytes 1228808 | tf_op jit(solution)/shard_map/ppermute | solution.py:19
  293.2 20.2 %collective-permute-start.26 = (bf16[40,5120]{1,0:T(8,128)(2,1)}, bf16[40,5120]{1,0:T(8,128)(2,1)S(1)}, u32[]{:S(2)}, u32[]{:S(2)}) collective-permute-start(bf16[40,5120]{1,0:T(8,128)(2,1)} %collective-permute-done.25), channel_id=1, source_target_pairs={{0,40},{4,44},{8,0},{12,4},{32,8},{36,12},{40,32},{44,36},{1,41},{... | collective-permute-start | bytes 1228808 | tf_op jit(solution)/shard_map/ppermute | solution.py:19
  313.4 20.5 %collective-permute-start.28 = (bf16[80,5120]{1,0:T(8,128)(2,1)S(1)}, bf16[80,5120]{1,0:T(8,128)(2,1)S(1)}, u32[]{:S(2)}, u32[]{:S(2)}) collective-permute-start(bf16[80,5120]{1,0:T(8,128)(2,1)S(1)} %get-tuple-element.40), channel_id=1, source_target_pairs={{0,64},{64,128},{128,192},{192,0},{1,65},{65,129},{129,193},{193,1... | collective-permute-start | bytes 2457608 | tf_op jit(solution)/shard_map/ppermute | solution.py:19
  314.5 19.7 %collective-permute-start.29 = (bf16[80,5120]{1,0:T(8,128)(2,1)S(1)}, bf16[80,5120]{1,0:T(8,128)(2,1)S(1)}, u32[]{:S(2)}, u32[]{:S(2)}) collective-permute-start(bf16[80,5120]{1,0:T(8,128)(2,1)S(1)} %copy-done.10), channel_id=1, source_target_pairs={{0,192},{64,0},{128,64},{192,128},{1,193},{65,1},{129,65},{193,129... | collective-permute-start | bytes 2457608 | tf_op jit(solution)/shard_map/ppermute | solution.py:19
  316.2 34.8 %collective-permute-start.30 = (bf16[80,5120]{1,0:T(8,128)(2,1)S(1)}, bf16[80,5120]{1,0:T(8,128)(2,1)S(1)}, u32[]{:S(2)}, u32[]{:S(2)}) collective-permute-start(bf16[80,5120]{1,0:T(8,128)(2,1)S(1)} %get-tuple-element.40), channel_id=1, source_target_pairs={{0,192},{64,0},{128,64},{192,128},{1,193},{65,1},{129,65},{193,129... | collective-permute-start | bytes 2457608 | tf_op jit(solution)/shard_map/ppermute | solution.py:19
  351.2 24.4 %collective-permute-start.33 = (bf16[480,5120]{1,0:T(8,128)(2,1)S(1)}, bf16[480,5120]{1,0:T(8,128)(2,1)S(1)}, u32[]{:S(2)}, u32[]{:S(2)}) collective-permute-start(bf16[480,5120]{1,0:T(8,128)(2,1)S(1)} %get-tuple-element.25), channel_id=1, source_target_pairs={{0,16},{16,0},{1,17},{17,1},{2,18},{18,2},{3,19},{19,3},{4,20},{20... | collective-permute-start | bytes 14745608 | tf_op jit(solution)/shard_map/ppermute | solution.py:19
  352.9 21.4 %collective-permute-start.31 = (bf16[80,5120]{1,0:T(8,128)(2,1)S(1)}, bf16[80,5120]{1,0:T(8,128)(2,1)S(1)}, u32[]{:S(2)}, u32[]{:S(2)}) collective-permute-start(bf16[80,5120]{1,0:T(8,128)(2,1)S(1)} %collective-permute-done.27), channel_id=1, source_target_pairs={{0,64},{64,128},{128,192},{192,0},{1,65},{65,129},{129,193},{193,1... | collective-permute-start | bytes 2457608 | tf_op jit(solution)/shard_map/ppermute | solution.py:19
  353.0 21.3 %collective-permute-start.32 = (bf16[80,5120]{1,0:T(8,128)(2,1)S(1)}, bf16[80,5120]{1,0:T(8,128)(2,1)S(1)}, u32[]{:S(2)}, u32[]{:S(2)}) collective-permute-start(bf16[80,5120]{1,0:T(8,128)(2,1)S(1)} %collective-permute-done.30), channel_id=1, source_target_pairs={{0,192},{64,0},{128,64},{192,128},{1,193},{65,1},{129,65},{193,129... | collective-permute-start | bytes 2457608 | tf_op jit(solution)/shard_map/ppermute | solution.py:19
  374.5 4.1 collective-permute-start.34
  397.6 23.9 %collective-permute-start.35 = (bf16[640,5120]{1,0:T(8,128)(2,1)}, bf16[640,5120]{1,0:T(8,128)(2,1)}, u32[]{:S(2)}, u32[]{:S(2)}) collective-permute-start(bf16[640,5120]{1,0:T(8,128)(2,1)} %convolution_convert_fusion), channel_id=1, source_target_pairs={{0,16},{16,0},{1,17},{17,1},{2,18},{18,2},{3,19},{19,3},{4,20},{20... | collective-permute-start | bytes 19660808 | tf_op jit(solution)/shard_map/ppermute | solution.py:19
  424.1 20.9 %collective-permute-start.40 = (bf16[80,5120]{1,0:T(8,128)(2,1)S(1)}, bf16[80,5120]{1,0:T(8,128)(2,1)S(1)}, u32[]{:S(2)}, u32[]{:S(2)}) collective-permute-start(bf16[80,5120]{1,0:T(8,128)(2,1)S(1)} %get-tuple-element.13), channel_id=1, source_target_pairs={{0,64},{64,128},{128,192},{192,0},{1,65},{65,129},{129,193},{193,1... | collective-permute-start | bytes 2457608 | tf_op jit(solution)/shard_map/ppermute | solution.py:19
  425.0 21.8 %collective-permute-start.39 = (bf16[80,5120]{1,0:T(8,128)(2,1)S(1)}, bf16[80,5120]{1,0:T(8,128)(2,1)S(1)}, u32[]{:S(2)}, u32[]{:S(2)}) collective-permute-start(bf16[80,5120]{1,0:T(8,128)(2,1)S(1)} %get-tuple-element.12), channel_id=1, source_target_pairs={{0,192},{64,0},{128,64},{192,128},{1,193},{65,1},{129,65},{193,129... | collective-permute-start | bytes 2457608 | tf_op jit(solution)/shard_map/ppermute | solution.py:19
  446.7 20.1 %collective-permute-start.41 = (bf16[80,5120]{1,0:T(8,128)(2,1)S(1)}, bf16[80,5120]{1,0:T(8,128)(2,1)S(1)}, u32[]{:S(2)}, u32[]{:S(2)}) collective-permute-start(bf16[80,5120]{1,0:T(8,128)(2,1)S(1)} %add_convert_fusion.2), channel_id=1, source_target_pairs={{0,64},{64,128},{128,192},{192,0},{1,65},{65,129},{129,193},{193,1... | collective-permute-start | bytes 2457608 | tf_op jit(solution)/shard_map/ppermute | solution.py:19
  469.6 18.0 %collective-permute-start.36 = (bf16[80,5120]{1,0:T(8,128)(2,1)S(1)}, bf16[80,5120]{1,0:T(8,128)(2,1)S(1)}, u32[]{:S(2)}, u32[]{:S(2)}) collective-permute-start(bf16[80,5120]{1,0:T(8,128)(2,1)S(1)} %get-tuple-element.11), channel_id=1, source_target_pairs={{0,192},{64,0},{128,64},{192,128},{1,193},{65,1},{129,65},{193,129... | collective-permute-start | bytes 2457608 | tf_op jit(solution)/shard_map/ppermute | solution.py:19
  469.9 20.6 %collective-permute-start.42 = (bf16[40,5120]{1,0:T(8,128)(2,1)S(1)}, bf16[40,5120]{1,0:T(8,128)(2,1)S(1)}, u32[]{:S(2)}, u32[]{:S(2)}) collective-permute-start(bf16[40,5120]{1,0:T(8,128)(2,1)S(1)} %get-tuple-element.22), channel_id=1, source_target_pairs={{0,8},{4,12},{8,32},{12,36},{32,40},{36,44},{40,0},{44,4},{1,9},{5... | collective-permute-start | bytes 1228808 | tf_op jit(solution)/shard_map/ppermute | solution.py:19
  473.7 20.3 %collective-permute-start.44 = (bf16[40,5120]{1,0:T(8,128)(2,1)S(1)}, bf16[40,5120]{1,0:T(8,128)(2,1)S(1)}, u32[]{:S(2)}, u32[]{:S(2)}) collective-permute-start(bf16[40,5120]{1,0:T(8,128)(2,1)S(1)} %get-tuple-element.23), channel_id=1, source_target_pairs={{0,40},{4,44},{8,0},{12,4},{32,8},{36,12},{40,32},{44,36},{1,41},{... | collective-permute-start | bytes 1228808 | tf_op jit(solution)/shard_map/ppermute | solution.py:19
  473.9 34.1 %collective-permute-start.38 = (bf16[80,5120]{1,0:T(8,128)(2,1)S(1)}, bf16[80,5120]{1,0:T(8,128)(2,1)S(1)}, u32[]{:S(2)}, u32[]{:S(2)}) collective-permute-start(bf16[80,5120]{1,0:T(8,128)(2,1)S(1)} %get-tuple-element.10), channel_id=1, source_target_pairs={{0,64},{64,128},{128,192},{192,0},{1,65},{65,129},{129,193},{193,1... | collective-permute-start | bytes 2457608 | tf_op jit(solution)/shard_map/ppermute | solution.py:19
  489.0 19.0 %collective-permute-start.37 = (bf16[80,5120]{1,0:T(8,128)(2,1)S(1)}, bf16[80,5120]{1,0:T(8,128)(2,1)S(1)}, u32[]{:S(2)}, u32[]{:S(2)}) collective-permute-start(bf16[80,5120]{1,0:T(8,128)(2,1)S(1)} %add_convert_fusion.6), channel_id=1, source_target_pairs={{0,192},{64,0},{128,64},{192,128},{1,193},{65,1},{129,65},{193,129... | collective-permute-start | bytes 2457608 | tf_op jit(solution)/shard_map/ppermute | solution.py:19
  490.6 17.4 %collective-permute-start.43 = (bf16[40,5120]{1,0:T(8,128)(2,1)S(1)}, bf16[40,5120]{1,0:T(8,128)(2,1)S(1)}, u32[]{:S(2)}, u32[]{:S(2)}) collective-permute-start(bf16[40,5120]{1,0:T(8,128)(2,1)S(1)} %collective-permute-done.42), channel_id=1, source_target_pairs={{0,8},{4,12},{8,32},{12,36},{32,40},{36,44},{40,0},{44,4},{1,9},{5... | collective-permute-start | bytes 1228808 | tf_op jit(solution)/shard_map/ppermute | solution.py:19
  493.9 14.1 %collective-permute-start.45 = (bf16[40,5120]{1,0:T(8,128)(2,1)S(1)}, bf16[40,5120]{1,0:T(8,128)(2,1)S(1)}, u32[]{:S(2)}, u32[]{:S(2)}) collective-permute-start(bf16[40,5120]{1,0:T(8,128)(2,1)S(1)} %collective-permute-done.44), channel_id=1, source_target_pairs={{0,40},{4,44},{8,0},{12,4},{32,8},{36,12},{40,32},{44,36},{1,41},{... | collective-permute-start | bytes 1228808 | tf_op jit(solution)/shard_map/ppermute | solution.py:19
  (19 other events, 752.6 us)
Sparse Core Ops, SparseCore 0:
  19.3 81.2 all-gather.2

commit v5 on v3

--- a/solution.py
+++ b/solution.py
@@ -48,10 +48,10 @@
     r = own.shape[0] // 8
     got = _pp(other, "core", 2, 1)
     blk = [own[i * r:(i + 1) * r].astype(jnp.float32) + got[i * r:(i + 1) * r].astype(jnp.float32) for i in range(8)]
-    a = _pp(blk[6].astype(jnp.bfloat16), "x", 4, -1)
-    b = _pp(blk[7].astype(jnp.bfloat16), "x", 4, 1)
-    c = _pp(blk[3].astype(jnp.bfloat16), "x", 4, -1)
-    d = _pp(blk[4].astype(jnp.bfloat16), "x", 4, 1)
+    ac = _pp(jnp.concatenate([blk[6], blk[3]], 0).astype(jnp.bfloat16), "x", 4, -1)
+    bd = _pp(jnp.concatenate([blk[7], blk[4]], 0).astype(jnp.bfloat16), "x", 4, 1)
+    a, c = ac[:r], ac[r:]
+    b, d = bd[:r], bd[r:]
     e = _pp((blk[5] + b.astype(jnp.float32)).astype(jnp.bfloat16), "x", 4, 1)
     f = _pp((blk[2] + a.astype(jnp.float32)).astype(jnp.bfloat16), "x", 4, -1)
     t1 = blk[1] + c.astype(jnp.float32) + e.astype(jnp.float32)

time: 548 us -> 576 us (1.051)
  waiting for transfers between devices: 210 us -> 256 us
  starting transfers between devices: 82.6 us -> 74.8 us
  blocking collectives: 118 us -> 112 us
    ppermute x34 -> x30, waiting for transfers between devices: 196 us -> 241 us  [_pp(): return lax.ppermute(v, axis, [(i, (i + shift) % n) for i in range(n)])]
    ppermute x34 -> x30, starting transfers between devices: 69.8 us -> 61.9 us  [_pp(): return lax.ppermute(v, axis, [(i, (i + shift) % n) for i in range(n)])]
    another operation x1 -> x5, other arithmetic: 0.18 us -> 6.33 us
    convert_element_type x6 -> x0, other arithmetic: 5.78 us -> none  [the longest x2 2.12 us: rs_rel(): z = _pp(t1.astype(jnp.bfloat16), 'zh', 2, 1)]
    unnamed x47 -> x51, local copies, waits for them, and re-layouts: 16.9 us -> 16.8 us
  transfers between devices with their start and end apart: 36 -> 32, of which waited for: 20 -> 20; matrix products, arithmetic and copies ran while one was open for 12% -> 10% of each run, Pallas kernels for 0% -> 0%
where the time goes in v5:
time: 576 us; the launch traced here: 569 us
  waiting for transfers between devices  256 us (44%)
  blocking collectives  112 us (19%)
  starting transfers between devices  74.8 us (13%)
  matrix products  51 us (9%)
  local copies, waits for them, and re-layouts  43.4 us (8%)
  other arithmetic  17.7 us (3%)
  between operations  14.3 us (2%)
    ppermute x30, waiting for transfers between devices, _pp(): return lax.ppermute(v, axis, [(i, (i + shift) % n) for i in range(n)])  241 us
    ppermute x30, starting transfers between devices, _pp(): return lax.ppermute(v, axis, [(i, (i + shift) % n) for i in range(n)])  61.9 us
    all_to_all x1, blocking collectives, local(): lax.all_to_all(outgoing, EXP, split_axis=0, concat_axis=0, tiled=True)  56.8 us
    all_to_all x1, blocking collectives, local(): lax.all_to_all(expert_out, EXP, split_axis=0, concat_axis=0, tiled=True)  55.3 us
    dot_general x2, matrix products, expert_rows(): jnp.dot(inner, down_local, preferred_element_type=jnp.float32)  26.8 us
    unnamed x51, local copies, waits for them, and re-layouts  16.8 us
    all_to_all x1, waiting for transfers between devices, local(): lax.all_to_all(attended.reshape(tok_rows, n_ctx, qwidth // n_ctx), CTX, s...  15.2 us
    all_to_all x1, starting transfers between devices, local(): lax.all_to_all(attended.reshape(tok_rows, n_ctx, qwidth // n_ctx), CTX, s...  12.8 us
  transfers between devices with their start and end apart: 32, of which 20 were waited for; matrix products, arithmetic and copies ran while one was open for 10% of the time, Pallas kernels for 0%

profile of v5, /device:TPU:1, one launch (start us, length us, event | category | flops | bytes accessed | tf_op | source)
XLA Modules:
  0.0 569.4 jit_solution(294683239235703034)
XLA Ops:
  8.7 7.8 %collective-permute-start = (bf16[64,1024]{0,1:T(8,128)(2,1)S(1)}, bf16[64,1024]{0,1:T(8,128)(2,1)S(1)}, u32[]{:S(2)}, u32[]{:S(2)}) collective-permute-start(bf16[64,1024]{0,1:T(8,128)(2,1)S(1)} %pad_maximum_fusion.5), channel_id=1, source_target_pairs={{0,32},{32,0},{1,33},{33,1},{2,34},{34,2},{3,35},{35,3},{4,36},{36... | collective-permute-start | bytes 393224 | tf_op jit(solution)/shard_map/ppermute | solution.py:19
  19.9 3.1 collective-permute-done
  23.1 2.9 collective-permute-start.4
  26.1 4.2 collective-permute-done.4
  31.0 2.5 collective-permute-done.2
  33.5 3.8 concatenate.79
  37.3 2.5 collective-permute-start.7
  39.9 2.7 collective-permute-start.6
  42.9 6.1 %collective-permute-done.5 = bf16[64,1024]{0,1:T(8,128)(2,1)} collective-permute-done((bf16[64,1024]{0,1:T(8,128)(2,1)S(1)}, bf16[64,1024]{0,1:T(8,128)(2,1)}, u32[]{:S(2)}, u32[]{:S(2)}) %collective-permute-start.5) | collective-permute-done | bytes 131104 | tf_op jit(solution)/shard_map/ppermute | solution.py:19
  54.7 5.6 concatenate.81
  60.4 3.1 fusion.86
  63.5 4.9 fusion.88
  68.4 2.9 fusion.26
  74.9 12.8 %all-to-all-start = ((bf16[64,16,160]{2,0,1:T(8,128)(2,1)}), bf16[64,16,160]{2,0,1:T(8,128)(2,1)S(1)}, u32[]{:S(2)}, u32[]{:S(2)}) async-start(bf16[64,16,160]{2,0,1:T(8,128)(2,1)} %copy.41), calls=%async_computation | async-start | bytes 1048576 | tf_op jit(solution)/shard_map/all_to_all | solution.py:122
  87.9 15.2 %all-to-all-done = bf16[64,16,160]{2,0,1:T(8,128)(2,1)S(1)} async-done(((bf16[64,16,160]{2,0,1:T(8,128)(2,1)}), bf16[64,16,160]{2,0,1:T(8,128)(2,1)S(1)}, u32[]{:S(2)}, u32[]{:S(2)}) %all-to-all-start) | async-done | bytes 327712 | tf_op jit(solution)/shard_map/all_to_all | solution.py:122
  106.4 4.1 reshape.274
  110.5 3.1 convolution_convert_fusion.2
  115.9 6.8 %collective-permute-done.9 = bf16[512,5120]{1,0:T(8,128)(2,1)S(1)} collective-permute-done((bf16[512,5120]{1,0:T(8,128)(2,1)S(1)}, bf16[512,5120]{1,0:T(8,128)(2,1)S(1)}, u32[]{:S(2)}, u32[]{:S(2)}) %collective-permute-start.9) | collective-permute-done | bytes 5242912 | tf_op jit(solution)/shard_map/ppermute | solution.py:19
  123.2 31.2 %collective-permute-done.12 = bf16[128,5120]{1,0:T(8,128)(2,1)S(1)} collective-permute-done((bf16[128,5120]{1,0:T(8,128)(2,1)S(1)}, bf16[128,5120]{1,0:T(8,128)(2,1)S(1)}, u32[]{:S(2)}, u32[]{:S(2)}) %collective-permute-start.12) | collective-permute-done | bytes 1310752 | tf_op jit(solution)/shard_map/ppermute | solution.py:19
  156.9 14.9 %collective-permute-done.13 = bf16[64,5120]{1,0:T(8,128)(2,1)S(1)} collective-permute-done((bf16[64,5120]{1,0:T(8,128)(2,1)S(1)}, bf16[64,5120]{1,0:T(8,128)(2,1)S(1)}, u32[]{:S(2)}, u32[]{:S(2)}) %collective-permute-start.13) | collective-permute-done | bytes 655392 | tf_op jit(solution)/shard_map/ppermute | solution.py:19
  171.8 12.6 %collective-permute-done.10 = bf16[128,5120]{1,0:T(8,128)(2,1)S(1)} collective-permute-done((bf16[128,5120]{1,0:T(8,128)(2,1)S(1)}, bf16[128,5120]{1,0:T(8,128)(2,1)S(1)}, u32[]{:S(2)}, u32[]{:S(2)}) %collective-permute-start.10) | collective-permute-done | bytes 1310752 | tf_op jit(solution)/shard_map/ppermute | solution.py:19
  187.8 11.5 %collective-permute-done.11 = bf16[64,5120]{1,0:T(8,128)(2,1)S(1)} collective-permute-done((bf16[64,5120]{1,0:T(8,128)(2,1)S(1)}, bf16[64,5120]{1,0:T(8,128)(2,1)S(1)}, u32[]{:S(2)}, u32[]{:S(2)}) %collective-permute-start.11) | collective-permute-done | bytes 655392 | tf_op jit(solution)/shard_map/ppermute | solution.py:19
  199.3 5.6 collective-permute-done.14
  207.0 56.8 %all_to_all.25 = bf16[16,5,5120]{2,1,0:T(8,128)(2,1)} all-to-all(bf16[16,5,5120]{2,1,0:T(8,128)(2,1)S(1)} %copy.42), channel_id=1, replica_groups=mesh['x'=4,'zh'=2,'core'=2,'zl'=4,'y'=4] {'zl','y'}, dimensions={0} | all-to-all | bytes 1638400 | tf_op jit(solution)/shard_map/all_to_all | solution.py:157
  267.5 2.6 collective-permute-start.18
  270.1 17.5 %collective-permute-done.15 = bf16[80,5120]{1,0:T(8,128)(2,1)S(1)} collective-permute-done((bf16[80,5120]{1,0:T(8,128)(2,1)}, bf16[80,5120]{1,0:T(8,128)(2,1)S(1)}, u32[]{:S(2)}, u32[]{:S(2)}) %collective-permute-start.15) | collective-permute-done | bytes 819232 | tf_op jit(solution)/shard_map/ppermute | solution.py:19
  287.7 2.7 collective-permute-start.19
  290.6 9.7 %collective-permute-done.17 = bf16[80,5120]{1,0:T(8,128)(2,1)S(1)} collective-permute-done((bf16[80,5120]{1,0:T(8,128)(2,1)S(1)}, bf16[80,5120]{1,0:T(8,128)(2,1)S(1)}, u32[]{:S(2)}, u32[]{:S(2)}) %collective-permute-start.17) | collective-permute-done | bytes 819232 | tf_op jit(solution)/shard_map/ppermute | solution.py:19
  300.8 2.6 copy-done.14
  303.4 21.5 %collective-permute-start.22 = (bf16[480,5120]{1,0:T(8,128)(2,1)S(1)}, bf16[480,5120]{1,0:T(8,128)(2,1)S(1)}, u32[]{:S(2)}, u32[]{:S(2)}) collective-permute-start(bf16[480,5120]{1,0:T(8,128)(2,1)S(1)} %get-tuple-element.26), channel_id=1, source_target_pairs={{0,16},{16,0},{1,17},{17,1},{2,18},{18,2},{3,19},{19,3},{4,20},{20... | collective-permute-start | bytes 14745608 | tf_op jit(solution)/shard_map/ppermute | solution.py:19
  324.9 2.7 collective-permute-start.21
  327.6 18.3 %collective-permute-done.20 = bf16[80,5120]{1,0:T(8,128)(2,1)S(1)} collective-permute-done((bf16[80,5120]{1,0:T(8,128)(2,1)S(1)}, bf16[80,5120]{1,0:T(8,128)(2,1)S(1)}, u32[]{:S(2)}, u32[]{:S(2)}) %collective-permute-start.20) | collective-permute-done | bytes 819232 | tf_op jit(solution)/shard_map/ppermute | solution.py:19
  347.6 2.8 collective-permute-done.23
  350.5 2.8 copy-done.6
  353.3 2.7 fusion.7
  356.0 13.4 %convolution_convert_fusion = bf16[640,5120]{1,0:T(8,128)(2,1)} fusion(bf16[1,256,5120]{2,1,0:T(8,128)(2,1)S(1)} %copy-done, f32[640,256]{1,0:T(8,128)} %fusion.7, bf16[640,5120]{1,0:T(8,128)(2,1)} %copy-done.6, bf16[1,5120,256]{2,1,0:T(8,128)(2,1)} %param.23), kind=kOutput, calls=%fused_computation.2 | convolution fusion | flops 3359703040 | bytes 19005440 | tf_op jit(solution)/shard_map/dot_general | solution.py:169
  373.0 6.3 %fusion.9 = f32[640,256]{1,0:T(8,128)} fusion(bf16[640,5120]{1,0:T(8,128)(2,1)} %constant_dynamic-update-slice_fusion, bf16[1,5120,256]{2,1,0:T(8,128)(2,1)} %param.24), kind=kOutput, calls=%fused_computation.18 | convolution fusion | flops 1677721600 | bytes 9830400 | tf_op jit(solution)/shard_map/dot_general | solution.py:167
  379.4 13.4 %convolution_convert_fusion.1 = bf16[640,5120]{1,0:T(8,128)(2,1)} fusion(bf16[1,256,5120]{2,1,0:T(8,128)(2,1)S(1)} %copy-done, f32[640,256]{1,0:T(8,128)} %fusion.9, bf16[640,5120]{1,0:T(8,128)(2,1)} %constant_dynamic-update-slice_fusion, bf16[1,5120,256]{2,1,0:T(8,128)(2,1)} %param.23), kind=kOutput, calls=%fused_computation.3 | convolution fusion | flops 3359703040 | bytes 19005440 | tf_op jit(solution)/shard_map/dot_general | solution.py:169
  392.8 2.5 add_convert_fusion.4
  396.3 37.6 %collective-permute-done.27 = bf16[160,5120]{1,0:T(8,128)(2,1)S(1)} collective-permute-done((bf16[160,5120]{1,0:T(8,128)(2,1)S(1)}, bf16[160,5120]{1,0:T(8,128)(2,1)S(1)}, u32[]{:S(2)}, u32[]{:S(2)}) %collective-permute-start.27) | collective-permute-done | bytes 1638432 | tf_op jit(solution)/shard_map/ppermute | solution.py:19
  433.9 2.6 add_convert_fusion.7
  438.2 19.7 %collective-permute-done.28 = bf16[80,5120]{1,0:T(8,128)(2,1)S(1)} collective-permute-done((bf16[80,5120]{1,0:T(8,128)(2,1)S(1)}, bf16[80,5120]{1,0:T(8,128)(2,1)S(1)}, u32[]{:S(2)}, u32[]{:S(2)}) %collective-permute-start.28) | collective-permute-done | bytes 819232 | tf_op jit(solution)/shard_map/ppermute | solution.py:19
  457.9 15.2 %collective-permute-done.25 = bf16[160,5120]{1,0:T(8,128)(2,1)S(1)} collective-permute-done((bf16[160,5120]{1,0:T(8,128)(2,1)S(1)}, bf16[160,5120]{1,0:T(8,128)(2,1)S(1)}, u32[]{:S(2)}, u32[]{:S(2)}) %collective-permute-start.25) | collective-permute-done | bytes 1638432 | tf_op jit(solution)/shard_map/ppermute | solution.py:19
  475.4 3.1 collective-permute-start.26
  478.5 15.8 %collective-permute-done.26 = bf16[80,5120]{1,0:T(8,128)(2,1)S(1)} collective-permute-done((bf16[80,5120]{1,0:T(8,128)(2,1)S(1)}, bf16[80,5120]{1,0:T(8,128)(2,1)S(1)}, u32[]{:S(2)}, u32[]{:S(2)}) %collective-permute-start.26) | collective-permute-done | bytes 819232 | tf_op jit(solution)/shard_map/ppermute | solution.py:19
  494.2 6.0 %collective-permute-done.29 = bf16[80,5120]{1,0:T(8,128)(2,1)S(1)} collective-permute-done((bf16[80,5120]{1,0:T(8,128)(2,1)S(1)}, bf16[80,5120]{1,0:T(8,128)(2,1)S(1)}, u32[]{:S(2)}, u32[]{:S(2)}) %collective-permute-start.29) | collective-permute-done | bytes 819232 | tf_op jit(solution)/shard_map/ppermute | solution.py:19
  500.2 2.7 add_convert_fusion
  505.2 55.3 %all_to_all.26 = bf16[16,5,5120]{2,1,0:T(8,128)(2,1)S(1)} all-to-all(bf16[16,5,5120]{2,1,0:T(8,128)(2,1)} %reshape.263), channel_id=1, replica_groups=mesh['x'=4,'zh'=2,'core'=2,'zl'=4,'y'=4] {'zl','y'}, dimensions={0} | all-to-all | bytes 1638400 | tf_op jit(solution)/shard_map/all_to_all | solution.py:175
  (133 shorter events, 48.9 us)
Async XLA Ops:
  6.5 349.5 %copy-start = (bf16[1,256,5120]{2,1,0:T(8,128)(2,1)S(1)}, bf16[1,256,5120]{2,1,0:T(8,128)(2,1)}, u32[]{:S(2)}) copy-start(bf16[1,256,5120]{2,1,0:T(8,128)(2,1)} %param.25) | copy-start | bytes 7864324
  6.5 36.1 %copy-start.19 = (s32[1,4]{1,0:T(1,128)S(1)}, s32[1,4]{1,0:T(1,128)}, u32[]{:S(2)}) copy-start(s32[1,4]{1,0:T(1,128)} %param.17) | copy-start | bytes 52
  6.5 99.8 %all-gather.3.cloned.1.call-start = ((), (), s32[]{:S(2)}) async-start(), calls=%async_computation.3 | async-start | bytes 2785280 | tf_op jit(solution)/shard_map/all_gather | solution.py:121
  8.7 14.4 %collective-permute-start = (bf16[64,1024]{0,1:T(8,128)(2,1)S(1)}, bf16[64,1024]{0,1:T(8,128)(2,1)S(1)}, u32[]{:S(2)}, u32[]{:S(2)}) collective-permute-start(bf16[64,1024]{0,1:T(8,128)(2,1)S(1)} %pad_maximum_fusion.5), channel_id=1, source_target_pairs={{0,32},{32,0},{1,33},{33,1},{2,34},{34,2},{3,35},{35,3},{4,36},{36... | collective-permute-start | bytes 393224 | tf_op jit(solution)/shard_map/ppermute | solution.py:19
  16.5 9.6 %collective-permute-start.1 = (bf16[64,1024]{0,1:T(8,128)(2,1)S(1)}, bf16[64,1024]{0,1:T(8,128)(2,1)S(1)}, u32[]{:S(2)}, u32[]{:S(2)}) collective-permute-start(bf16[64,1024]{0,1:T(8,128)(2,1)S(1)} %pad_maximum_fusion.5), channel_id=1, source_target_pairs={{0,64},{64,128},{128,192},{192,0},{1,65},{65,129},{129,193},{193,1... | collective-permute-start | bytes 393224 | tf_op jit(solution)/shard_map/ppermute | solution.py:19
  17.7 8.4 %collective-permute-start.3 = (bf16[64,1024]{0,1:T(8,128)(2,1)S(1)}, bf16[64,1024]{0,1:T(8,128)(2,1)}, u32[]{:S(2)}, u32[]{:S(2)}) collective-permute-start(bf16[64,1024]{0,1:T(8,128)(2,1)S(1)} %pad_maximum_fusion.5), channel_id=1, source_target_pairs={{0,192},{64,0},{128,64},{192,128},{1,193},{65,1},{129,65},{193,129... | collective-permute-start | bytes 393224 | tf_op jit(solution)/shard_map/ppermute | solution.py:19
  23.1 7.2 %collective-permute-start.4 = (bf16[64,1024]{0,1:T(8,128)(2,1)S(1)}, bf16[64,1024]{0,1:T(8,128)(2,1)S(1)}, u32[]{:S(2)}, u32[]{:S(2)}) collective-permute-start(bf16[64,1024]{0,1:T(8,128)(2,1)S(1)} %collective-permute-done), channel_id=1, source_target_pairs={{0,192},{64,0},{128,64},{192,128},{1,193},{65,1},{129,65},{193,129... | collective-permute-start | bytes 393224 | tf_op jit(solution)/shard_map/ppermute | solution.py:19
  26.0 7.5 %collective-permute-start.2 = (bf16[64,1024]{0,1:T(8,128)(2,1)S(1)}, bf16[64,1024]{0,1:T(8,128)(2,1)}, u32[]{:S(2)}, u32[]{:S(2)}) collective-permute-start(bf16[64,1024]{0,1:T(8,128)(2,1)S(1)} %collective-permute-done), channel_id=1, source_target_pairs={{0,64},{64,128},{128,192},{192,0},{1,65},{65,129},{129,193},{193,1... | collective-permute-start | bytes 393224 | tf_op jit(solution)/shard_map/ppermute | solution.py:19
  37.3 17.4 %collective-permute-start.7 = (bf16[384,1024]{0,1:T(8,128)(2,1)}, bf16[384,1024]{0,1:T(8,128)(2,1)}, u32[]{:S(2)}, u32[]{:S(2)}) collective-permute-start(bf16[384,1024]{0,1:T(8,128)(2,1)} %concatenate.79), channel_id=1, source_target_pairs={{0,16},{16,0},{1,17},{17,1},{2,18},{18,2},{3,19},{19,3},{4,20},{20... | collective-permute-start | bytes 2359304 | tf_op jit(solution)/shard_map/ppermute | solution.py:19
  39.9 9.1 %collective-permute-start.5 = (bf16[64,1024]{0,1:T(8,128)(2,1)S(1)}, bf16[64,1024]{0,1:T(8,128)(2,1)}, u32[]{:S(2)}, u32[]{:S(2)}) collective-permute-start(bf16[64,1024]{0,1:T(8,128)(2,1)S(1)} %collective-permute-done.1), channel_id=1, source_target_pairs={{0,64},{64,128},{128,192},{192,0},{1,65},{65,129},{129,193},{193,1... | collective-permute-start | bytes 393224 | tf_op jit(solution)/shard_map/ppermute | solution.py:19
  39.9 9.1 %collective-permute-start.6 = (bf16[64,1024]{0,1:T(8,128)(2,1)}, bf16[64,1024]{0,1:T(8,128)(2,1)}, u32[]{:S(2)}, u32[]{:S(2)}) collective-permute-start(bf16[64,1024]{0,1:T(8,128)(2,1)} %copy-done.12), channel_id=1, source_target_pairs={{0,192},{64,0},{128,64},{192,128},{1,193},{65,1},{129,65},{193,129... | collective-permute-start | bytes 393224 | tf_op jit(solution)/shard_map/ppermute | solution.py:19
  50.9 3.8 collective-permute-start.8
  60.4 3.1 copy-start.13
  74.9 28.2 %all-to-all-start = ((bf16[64,16,160]{2,0,1:T(8,128)(2,1)}), bf16[64,16,160]{2,0,1:T(8,128)(2,1)S(1)}, u32[]{:S(2)}, u32[]{:S(2)}) async-start(bf16[64,16,160]{2,0,1:T(8,128)(2,1)} %copy.41), calls=%async_computation | async-start | bytes 1048576 | tf_op jit(solution)/shard_map/all_to_all | solution.py:122
  106.4 4.1 copy-start.11
  110.5 3.9 copy-start.1
  113.6 9.1 %collective-permute-start.9 = (bf16[512,5120]{1,0:T(8,128)(2,1)S(1)}, bf16[512,5120]{1,0:T(8,128)(2,1)S(1)}, u32[]{:S(2)}, u32[]{:S(2)}) collective-permute-start(bf16[512,5120]{1,0:T(8,128)(2,1)S(1)} %convolution_convert_fusion.2), channel_id=1, source_target_pairs={{0,16},{16,0},{1,17},{17,1},{2,18},{18,2},{3,19},{19,3},{4,20},{20... | collective-permute-start | bytes 15728648 | tf_op jit(solution)/shard_map/ppermute | solution.py:19
  123.1 31.3 %collective-permute-start.12 = (bf16[128,5120]{1,0:T(8,128)(2,1)S(1)}, bf16[128,5120]{1,0:T(8,128)(2,1)S(1)}, u32[]{:S(2)}, u32[]{:S(2)}) collective-permute-start(bf16[128,5120]{1,0:T(8,128)(2,1)S(1)} %pad_maximum_fusion.4), channel_id=1, source_target_pairs={{0,64},{64,128},{128,192},{192,0},{1,65},{65,129},{129,193},{193,1... | collective-permute-start | bytes 3932168 | tf_op jit(solution)/shard_map/ppermute | solution.py:19
  155.0 1.8 copy-start.15
  155.1 29.2 %collective-permute-start.10 = (bf16[128,5120]{1,0:T(8,128)(2,1)S(1)}, bf16[128,5120]{1,0:T(8,128)(2,1)S(1)}, u32[]{:S(2)}, u32[]{:S(2)}) collective-permute-start(bf16[128,5120]{1,0:T(8,128)(2,1)S(1)} %pad_maximum_fusion.3), channel_id=1, source_target_pairs={{0,192},{64,0},{128,64},{192,128},{1,193},{65,1},{129,65},{193,129... | collective-permute-start | bytes 3932168 | tf_op jit(solution)/shard_map/ppermute | solution.py:19
  155.2 16.5 %collective-permute-start.13 = (bf16[64,5120]{1,0:T(8,128)(2,1)S(1)}, bf16[64,5120]{1,0:T(8,128)(2,1)S(1)}, u32[]{:S(2)}, u32[]{:S(2)}) collective-permute-start(bf16[64,5120]{1,0:T(8,128)(2,1)S(1)} %get-tuple-element.19), channel_id=1, source_target_pairs={{0,64},{64,128},{128,192},{192,0},{1,65},{65,129},{129,193},{193,1... | collective-permute-start | bytes 1966088 | tf_op jit(solution)/shard_map/ppermute | solution.py:19
  156.8 30.7 %copy-start.16 = (s32[1,64,1]{1,2,0:T(1,128)S(1)}, s32[1,64,1]{1,2,0:T(1,128)}, u32[]{:S(2)}) copy-start(s32[1,64,1]{1,2,0:T(1,128)} %param.22) | copy-start | bytes 772
  156.8 48.0 %copy-start.3 = (bf16[1,64,5120]{2,1,0:T(8,128)(2,1)S(1)}, bf16[1,64,5120]{2,1,0:T(8,128)(2,1)}, u32[]{:S(2)}) copy-start(bf16[1,64,5120]{2,1,0:T(8,128)(2,1)} %param.18) | copy-start | bytes 1966084
  185.0 14.3 %collective-permute-start.11 = (bf16[64,5120]{1,0:T(8,128)(2,1)S(1)}, bf16[64,5120]{1,0:T(8,128)(2,1)S(1)}, u32[]{:S(2)}, u32[]{:S(2)}) collective-permute-start(bf16[64,5120]{1,0:T(8,128)(2,1)S(1)} %get-tuple-element.16), channel_id=1, source_target_pairs={{0,192},{64,0},{128,64},{192,128},{1,193},{65,1},{129,65},{193,129... | collective-permute-start | bytes 1966088 | tf_op jit(solution)/shard_map/ppermute | solution.py:19
  186.6 18.3 %collective-permute-start.14 = (bf16[64,5120]{1,0:T(8,128)(2,1)S(1)}, bf16[64,5120]{1,0:T(8,128)(2,1)S(1)}, u32[]{:S(2)}, u32[]{:S(2)}) collective-permute-start(bf16[64,5120]{1,0:T(8,128)(2,1)S(1)} %get-tuple-element.17), channel_id=1, source_target_pairs={{0,32},{32,0},{1,33},{33,1},{2,34},{34,2},{3,35},{35,3},{4,36},{36... | collective-permute-start | bytes 1966088 | tf_op jit(solution)/shard_map/ppermute | solution.py:19
  187.7 17.8 %copy-start.18 = (bf16[5120,16]{0,1:T(8,128)(2,1)S(1)}, bf16[5120,16]{0,1:T(8,128)(2,1)}, u32[]{:S(2)}) copy-start(bf16[5120,16]{0,1:T(8,128)(2,1)} %param.21) | copy-start | bytes 491524
  266.0 1.4 copy-start.10
  266.0 21.6 %collective-permute-start.15 = (bf16[80,5120]{1,0:T(8,128)(2,1)}, bf16[80,5120]{1,0:T(8,128)(2,1)S(1)}, u32[]{:S(2)}, u32[]{:S(2)}) collective-permute-start(bf16[80,5120]{1,0:T(8,128)(2,1)} %reshape.262), channel_id=1, source_target_pairs={{0,32},{32,0},{1,33},{33,1},{2,34},{34,2},{3,35},{35,3},{4,36},{36... | collective-permute-start | bytes 2457608 | tf_op jit(solution)/shard_map/ppermute | solution.py:19
  266.1 24.4 %collective-permute-start.16 = (bf16[80,5120]{1,0:T(8,128)(2,1)}, bf16[80,5120]{1,0:T(8,128)(2,1)S(1)}, u32[]{:S(2)}, u32[]{:S(2)}) collective-permute-start(bf16[80,5120]{1,0:T(8,128)(2,1)} %reshape.262), channel_id=1, source_target_pairs={{0,64},{64,128},{128,192},{192,0},{1,65},{65,129},{129,193},{193,1... | collective-permute-start | bytes 2457608 | tf_op jit(solution)/shard_map/ppermute | solution.py:19
  267.5 33.0 %collective-permute-start.18 = (bf16[80,5120]{1,0:T(8,128)(2,1)S(1)}, bf16[80,5120]{1,0:T(8,128)(2,1)S(1)}, u32[]{:S(2)}, u32[]{:S(2)}) collective-permute-start(bf16[80,5120]{1,0:T(8,128)(2,1)S(1)} %copy-done.10), channel_id=1, source_target_pairs={{0,192},{64,0},{128,64},{192,128},{1,193},{65,1},{129,65},{193,129... | collective-permute-start | bytes 2457608 | tf_op jit(solution)/shard_map/ppermute | solution.py:19
  287.7 12.7 %collective-permute-start.17 = (bf16[80,5120]{1,0:T(8,128)(2,1)S(1)}, bf16[80,5120]{1,0:T(8,128)(2,1)S(1)}, u32[]{:S(2)}, u32[]{:S(2)}) collective-permute-start(bf16[80,5120]{1,0:T(8,128)(2,1)S(1)} %collective-permute-done.15), channel_id=1, source_target_pairs={{0,64},{64,128},{128,192},{192,0},{1,65},{65,129},{129,193},{193,1... | collective-permute-start | bytes 2457608 | tf_op jit(solution)/shard_map/ppermute | solution.py:19
  287.7 13.0 %collective-permute-start.19 = (bf16[80,5120]{1,0:T(8,128)(2,1)S(1)}, bf16[80,5120]{1,0:T(8,128)(2,1)S(1)}, u32[]{:S(2)}, u32[]{:S(2)}) collective-permute-start(bf16[80,5120]{1,0:T(8,128)(2,1)S(1)} %collective-permute-done.15), channel_id=1, source_target_pairs={{0,192},{64,0},{128,64},{192,128},{1,193},{65,1},{129,65},{193,129... | collective-permute-start | bytes 2457608 | tf_op jit(solution)/shard_map/ppermute | solution.py:19
  300.8 2.6 copy-start.14
  303.4 43.8 %collective-permute-start.22 = (bf16[480,5120]{1,0:T(8,128)(2,1)S(1)}, bf16[480,5120]{1,0:T(8,128)(2,1)S(1)}, u32[]{:S(2)}, u32[]{:S(2)}) collective-permute-start(bf16[480,5120]{1,0:T(8,128)(2,1)S(1)} %get-tuple-element.26), channel_id=1, source_target_pairs={{0,16},{16,0},{1,17},{17,1},{2,18},{18,2},{3,19},{19,3},{4,20},{20... | collective-permute-start | bytes 14745608 | tf_op jit(solution)/shard_map/ppermute | solution.py:19
  324.9 21.0 %collective-permute-start.20 = (bf16[80,5120]{1,0:T(8,128)(2,1)S(1)}, bf16[80,5120]{1,0:T(8,128)(2,1)S(1)}, u32[]{:S(2)}, u32[]{:S(2)}) collective-permute-start(bf16[80,5120]{1,0:T(8,128)(2,1)S(1)} %collective-permute-done.16), channel_id=1, source_target_pairs={{0,64},{64,128},{128,192},{192,0},{1,65},{65,129},{129,193},{193,1... | collective-permute-start | bytes 2457608 | tf_op jit(solution)/shard_map/ppermute | solution.py:19
  324.9 21.0 %collective-permute-start.21 = (bf16[80,5120]{1,0:T(8,128)(2,1)S(1)}, bf16[80,5120]{1,0:T(8,128)(2,1)S(1)}, u32[]{:S(2)}, u32[]{:S(2)}) collective-permute-start(bf16[80,5120]{1,0:T(8,128)(2,1)S(1)} %collective-permute-done.19), channel_id=1, source_target_pairs={{0,192},{64,0},{128,64},{192,128},{1,193},{65,1},{129,65},{193,129... | collective-permute-start | bytes 2457608 | tf_op jit(solution)/shard_map/ppermute | solution.py:19
  346.0 4.3 collective-permute-start.23
  347.5 5.7 %copy-start.17 = (bf16[1,5120,256]{2,1,0:T(8,128)(2,1)S(1)}, bf16[1,5120,256]{2,1,0:T(8,128)(2,1)}, u32[]{:S(2)}) copy-start(bf16[1,5120,256]{2,1,0:T(8,128)(2,1)} %param.24) | copy-start | bytes 7864324
  350.5 2.8 copy-start.6
  369.4 2.7 copy-start.9
  369.4 23.4 %collective-permute-start.24 = (bf16[640,5120]{1,0:T(8,128)(2,1)}, bf16[640,5120]{1,0:T(8,128)(2,1)}, u32[]{:S(2)}, u32[]{:S(2)}) collective-permute-start(bf16[640,5120]{1,0:T(8,128)(2,1)} %convolution_convert_fusion), channel_id=1, source_target_pairs={{0,16},{16,0},{1,17},{17,1},{2,18},{18,2},{3,19},{19,3},{4,20},{20... | collective-permute-start | bytes 19660808 | tf_op jit(solution)/shard_map/ppermute | solution.py:19
  392.8 41.2 %copy-start.2 = (bf16[640,5120]{1,0:T(8,128)(2,1)S(1)}, bf16[640,5120]{1,0:T(8,128)(2,1)}, u32[]{:S(2)}) copy-start(bf16[640,5120]{1,0:T(8,128)(2,1)} %convolution_convert_fusion.1) | copy-start | bytes 19660804
  395.4 38.5 %collective-permute-start.27 = (bf16[160,5120]{1,0:T(8,128)(2,1)S(1)}, bf16[160,5120]{1,0:T(8,128)(2,1)S(1)}, u32[]{:S(2)}, u32[]{:S(2)}) collective-permute-start(bf16[160,5120]{1,0:T(8,128)(2,1)S(1)} %pad_maximum_fusion.2), channel_id=1, source_target_pairs={{0,64},{64,128},{128,192},{192,0},{1,65},{65,129},{129,193},{193,1... | collective-permute-start | bytes 4915208 | tf_op jit(solution)/shard_map/ppermute | solution.py:19
  436.7 36.4 %collective-permute-start.25 = (bf16[160,5120]{1,0:T(8,128)(2,1)S(1)}, bf16[160,5120]{1,0:T(8,128)(2,1)S(1)}, u32[]{:S(2)}, u32[]{:S(2)}) collective-permute-start(bf16[160,5120]{1,0:T(8,128)(2,1)S(1)} %pad_maximum_fusion.1), channel_id=1, source_target_pairs={{0,192},{64,0},{128,64},{192,128},{1,193},{65,1},{129,65},{193,129... | collective-permute-start | bytes 4915208 | tf_op jit(solution)/shard_map/ppermute | solution.py:19
  438.2 19.7 %collective-permute-start.28 = (bf16[80,5120]{1,0:T(8,128)(2,1)S(1)}, bf16[80,5120]{1,0:T(8,128)(2,1)S(1)}, u32[]{:S(2)}, u32[]{:S(2)}) collective-permute-start(bf16[80,5120]{1,0:T(8,128)(2,1)S(1)} %get-tuple-element.12), channel_id=1, source_target_pairs={{0,64},{64,128},{128,192},{192,0},{1,65},{65,129},{129,193},{193,1... | collective-permute-start | bytes 2457608 | tf_op jit(solution)/shard_map/ppermute | solution.py:19
  475.4 18.8 %collective-permute-start.26 = (bf16[80,5120]{1,0:T(8,128)(2,1)S(1)}, bf16[80,5120]{1,0:T(8,128)(2,1)S(1)}, u32[]{:S(2)}, u32[]{:S(2)}) collective-permute-start(bf16[80,5120]{1,0:T(8,128)(2,1)S(1)} %get-tuple-element.9), channel_id=1, source_target_pairs={{0,192},{64,0},{128,64},{192,128},{1,193},{65,1},{129,65},{193,129... | collective-permute-start | bytes 2457608 | tf_op jit(solution)/shard_map/ppermute | solution.py:19
  478.5 21.7 %collective-permute-start.29 = (bf16[80,5120]{1,0:T(8,128)(2,1)S(1)}, bf16[80,5120]{1,0:T(8,128)(2,1)S(1)}, u32[]{:S(2)}, u32[]{:S(2)}) collective-permute-start(bf16[80,5120]{1,0:T(8,128)(2,1)S(1)} %get-tuple-element.10), channel_id=1, source_target_pairs={{0,32},{32,0},{1,33},{33,1},{2,34},{34,2},{3,35},{35,3},{4,36},{36... | collective-permute-start | bytes 2457608 | tf_op jit(solution)/shard_map/ppermute | solution.py:19
  505.2 55.3 %copy-start.5 = (bf16[64,5120]{1,0:T(8,128)(2,1)S(1)}, bf16[64,5120]{1,0:T(8,128)(2,1)}, u32[]{:S(2)}) copy-start(bf16[64,5120]{1,0:T(8,128)(2,1)} %copy-done.4) | copy-start | bytes 1966084
  (4 other events, 4.7 us)
Sparse Core Ops, SparseCore 0:
  19.3 71.4 all-gather.2

commit v6 on v3

--- a/solution.py
+++ b/solution.py
@@ -48,14 +48,16 @@
     r = own.shape[0] // 8
     got = _pp(other, "core", 2, 1)
     blk = [own[i * r:(i + 1) * r].astype(jnp.float32) + got[i * r:(i + 1) * r].astype(jnp.float32) for i in range(8)]
-    a = _pp(blk[6].astype(jnp.bfloat16), "x", 4, -1)
     b = _pp(blk[7].astype(jnp.bfloat16), "x", 4, 1)
     c = _pp(blk[3].astype(jnp.bfloat16), "x", 4, -1)
-    d = _pp(blk[4].astype(jnp.bfloat16), "x", 4, 1)
     e = _pp((blk[5] + b.astype(jnp.float32)).astype(jnp.bfloat16), "x", 4, 1)
-    f = _pp((blk[2] + a.astype(jnp.float32)).astype(jnp.bfloat16), "x", 4, -1)
+    a_src, _ = lax.optimization_barrier((blk[6].astype(jnp.bfloat16), c))
+    a = _pp(a_src, "x", 4, -1)
     t1 = blk[1] + c.astype(jnp.float32) + e.astype(jnp.float32)
     z = _pp(t1.astype(jnp.bfloat16), "zh", 2, 1)
+    d_src, _ = lax.optimization_barrier((blk[4].astype(jnp.bfloat16), e))
+    d = _pp(d_src, "x", 4, 1)
+    f = _pp((blk[2] + a.astype(jnp.float32)).astype(jnp.bfloat16), "x", 4, -1)
     t0 = blk[0] + f.astype(jnp.float32) + d.astype(jnp.float32)
     return t0 + z.astype(jnp.float32)
 

time: 548 us -> 516 us (0.942)
  waiting for transfers between devices: 210 us -> 188 us
    ppermute x34, waiting for transfers between devices: 196 us -> 173 us  [_pp(): return lax.ppermute(v, axis, [(i, (i + shift) % n) for i in range(n)])]
    unnamed x47 -> x49, local copies, waits for them, and re-layouts: 16.9 us -> 16.9 us
  transfers between devices with their start and end apart: 36 -> 36, of which waited for: 20 -> 18; matrix products, arithmetic and copies ran while one was open for 12% -> 12% of each run, Pallas kernels for 0% -> 0%
where the time goes in v6:
time: 516 us; the launch traced here: 510 us
  waiting for transfers between devices  188 us (36%)
  blocking collectives  113 us (22%)
  starting transfers between devices  82.4 us (16%)
  matrix products  50.2 us (10%)
  local copies, waits for them, and re-layouts  44.6 us (9%)
  other arithmetic  17.5 us (3%)
  between operations  14 us (3%)
    ppermute x34, waiting for transfers between devices, _pp(): return lax.ppermute(v, axis, [(i, (i + shift) % n) for i in range(n)])  173 us
    ppermute x34, starting transfers between devices, _pp(): return lax.ppermute(v, axis, [(i, (i + shift) % n) for i in range(n)])  69.5 us
    all_to_all x1, blocking collectives, local(): lax.all_to_all(outgoing, EXP, split_axis=0, concat_axis=0, tiled=True)  57.3 us
    all_to_all x1, blocking collectives, local(): lax.all_to_all(expert_out, EXP, split_axis=0, concat_axis=0, tiled=True)  55.6 us
    dot_general x2, matrix products, expert_rows(): jnp.dot(inner, down_local, preferred_element_type=jnp.float32)  26.7 us
    unnamed x49, local copies, waits for them, and re-layouts  16.9 us
    all_to_all x1, waiting for transfers between devices, local(): lax.all_to_all(attended.reshape(tok_rows, n_ctx, qwidth // n_ctx), CTX, s...  15.2 us
    all_to_all x1, starting transfers between devices, local(): lax.all_to_all(attended.reshape(tok_rows, n_ctx, qwidth // n_ctx), CTX, s...  12.8 us
  transfers between devices with their start and end apart: 36, of which 18 were waited for; matrix products, arithmetic and copies ran while one was open for 12% of the time, Pallas kernels for 0%

profile of v6, /device:TPU:1, one launch (start us, length us, event | category | flops | bytes accessed | tf_op | source)
XLA Modules:
  0.0 509.7 jit_solution(14023714147858080183)
XLA Ops:
  8.7 7.8 %collective-permute-start = (bf16[64,1024]{0,1:T(8,128)(2,1)S(1)}, bf16[64,1024]{0,1:T(8,128)(2,1)S(1)}, u32[]{:S(2)}, u32[]{:S(2)}) collective-permute-start(bf16[64,1024]{0,1:T(8,128)(2,1)S(1)} %pad_maximum_fusion.1), channel_id=1, source_target_pairs={{0,32},{32,0},{1,33},{33,1},{2,34},{34,2},{3,35},{35,3},{4,36},{36... | collective-permute-start | bytes 393224 | tf_op jit(solution)/shard_map/ppermute | solution.py:19
  19.9 3.1 collective-permute-done
  23.1 2.9 collective-permute-start.4
  26.1 4.2 collective-permute-done.4
  33.5 3.8 concatenate.63
  39.9 2.7 collective-permute-start.6
  42.9 6.1 %collective-permute-done.5 = bf16[64,1024]{0,1:T(8,128)(2,1)} collective-permute-done((bf16[64,1024]{0,1:T(8,128)(2,1)S(1)}, bf16[64,1024]{0,1:T(8,128)(2,1)}, u32[]{:S(2)}, u32[]{:S(2)}) %collective-permute-start.5) | collective-permute-done | bytes 131104 | tf_op jit(solution)/shard_map/ppermute | solution.py:19
  54.7 5.6 %concatenate.65 = bf16[1024,1024]{0,1:T(8,128)(2,1)} concatenate(bf16[64,1024]{0,1:T(8,128)(2,1)S(1)} %pad_maximum_fusion.1, bf16[64,1024]{0,1:T(8,128)(2,1)S(1)} %collective-permute-done, bf16[64,1024]{0,1:T(8,128)(2,1)S(1)} %collective-permute-done.1, bf16[64,1024]{0,1:T(8,128)(2,1)} %collective-permute-done.2, bf16[64,1024]{0,1:T(8,128)(2,1)} %collective-permute-done.3, ...), dimensions={0} | concatenate | bytes 4194304 | tf_op jit(solution)/shard_map/concatenate | solution.py:44
  60.3 3.1 fusion.86
  63.4 4.9 fusion.88
  68.4 2.9 fusion.26
  74.9 12.8 %all-to-all-start = ((bf16[64,16,160]{2,0,1:T(8,128)(2,1)}), bf16[64,16,160]{2,0,1:T(8,128)(2,1)S(1)}, u32[]{:S(2)}, u32[]{:S(2)}) async-start(bf16[64,16,160]{2,0,1:T(8,128)(2,1)} %copy.41), calls=%async_computation | async-start | bytes 1048576 | tf_op jit(solution)/shard_map/all_to_all | solution.py:124
  87.9 15.2 %all-to-all-done = bf16[64,16,160]{2,0,1:T(8,128)(2,1)S(1)} async-done(((bf16[64,16,160]{2,0,1:T(8,128)(2,1)}), bf16[64,16,160]{2,0,1:T(8,128)(2,1)S(1)}, u32[]{:S(2)}, u32[]{:S(2)}) %all-to-all-start) | async-done | bytes 327712 | tf_op jit(solution)/shard_map/all_to_all | solution.py:124
  106.4 4.1 reshape.274
  110.5 3.1 convolution_convert_fusion.2
  115.9 6.8 %collective-permute-done.9 = bf16[512,5120]{1,0:T(8,128)(2,1)S(1)} collective-permute-done((bf16[512,5120]{1,0:T(8,128)(2,1)S(1)}, bf16[512,5120]{1,0:T(8,128)(2,1)S(1)}, u32[]{:S(2)}, u32[]{:S(2)}) %collective-permute-start.9) | collective-permute-done | bytes 5242912 | tf_op jit(solution)/shard_map/ppermute | solution.py:19
  123.4 2.7 collective-permute-start.10
  126.1 14.5 %collective-permute-done.13 = bf16[64,5120]{1,0:T(8,128)(2,1)S(1)} collective-permute-done((bf16[64,5120]{1,0:T(8,128)(2,1)S(1)}, bf16[64,5120]{1,0:T(8,128)(2,1)S(1)}, u32[]{:S(2)}, u32[]{:S(2)}) %collective-permute-start.13) | collective-permute-done | bytes 655392 | tf_op jit(solution)/shard_map/ppermute | solution.py:19
  141.0 2.7 collective-permute-start.11
  143.7 13.6 %collective-permute-done.14 = bf16[64,5120]{1,0:T(8,128)(2,1)S(1)} collective-permute-done((bf16[64,5120]{1,0:T(8,128)(2,1)S(1)}, bf16[64,5120]{1,0:T(8,128)(2,1)S(1)}, u32[]{:S(2)}, u32[]{:S(2)}) %collective-permute-start.14) | collective-permute-done | bytes 655392 | tf_op jit(solution)/shard_map/ppermute | solution.py:19
  158.3 2.7 collective-permute-start.12
  161.3 12.4 %collective-permute-done.15 = bf16[64,5120]{1,0:T(8,128)(2,1)S(1)} collective-permute-done((bf16[64,5120]{1,0:T(8,128)(2,1)S(1)}, bf16[64,5120]{1,0:T(8,128)(2,1)S(1)}, u32[]{:S(2)}, u32[]{:S(2)}) %collective-permute-start.15) | collective-permute-done | bytes 655392 | tf_op jit(solution)/shard_map/ppermute | solution.py:19
  173.7 5.0 collective-permute-done.16
  180.8 57.3 %all_to_all.25 = bf16[16,5,5120]{2,1,0:T(8,128)(2,1)} all-to-all(bf16[16,5,5120]{2,1,0:T(8,128)(2,1)S(1)} %copy.42), channel_id=1, replica_groups=mesh['x'=4,'zh'=2,'core'=2,'zl'=4,'y'=4] {'zl','y'}, dimensions={0} | all-to-all | bytes 1638400 | tf_op jit(solution)/shard_map/all_to_all | solution.py:159
  241.7 2.7 collective-permute-start.20
  244.5 17.6 %collective-permute-done.17 = bf16[80,5120]{1,0:T(8,128)(2,1)S(1)} collective-permute-done((bf16[80,5120]{1,0:T(8,128)(2,1)}, bf16[80,5120]{1,0:T(8,128)(2,1)S(1)}, u32[]{:S(2)}, u32[]{:S(2)}) %collective-permute-start.17) | collective-permute-done | bytes 819232 | tf_op jit(solution)/shard_map/ppermute | solution.py:19
  262.0 2.7 collective-permute-start.21
  265.0 9.7 %collective-permute-done.19 = bf16[80,5120]{1,0:T(8,128)(2,1)S(1)} collective-permute-done((bf16[80,5120]{1,0:T(8,128)(2,1)S(1)}, bf16[80,5120]{1,0:T(8,128)(2,1)S(1)}, u32[]{:S(2)}, u32[]{:S(2)}) %collective-permute-start.19) | collective-permute-done | bytes 819232 | tf_op jit(solution)/shard_map/ppermute | solution.py:19
  275.1 2.6 copy-done.12
  277.8 21.5 %collective-permute-start.24 = (bf16[480,5120]{1,0:T(8,128)(2,1)S(1)}, bf16[480,5120]{1,0:T(8,128)(2,1)S(1)}, u32[]{:S(2)}, u32[]{:S(2)}) collective-permute-start(bf16[480,5120]{1,0:T(8,128)(2,1)S(1)} %get-tuple-element.32), channel_id=1, source_target_pairs={{0,16},{16,0},{1,17},{17,1},{2,18},{18,2},{3,19},{19,3},{4,20},{20... | collective-permute-start | bytes 14745608 | tf_op jit(solution)/shard_map/ppermute | solution.py:19
  299.3 2.9 collective-permute-start.23
  302.2 18.1 %collective-permute-done.22 = bf16[80,5120]{1,0:T(8,128)(2,1)S(1)} collective-permute-done((bf16[80,5120]{1,0:T(8,128)(2,1)S(1)}, bf16[80,5120]{1,0:T(8,128)(2,1)S(1)}, u32[]{:S(2)}, u32[]{:S(2)}) %collective-permute-start.22) | collective-permute-done | bytes 819232 | tf_op jit(solution)/shard_map/ppermute | solution.py:19
  321.8 2.7 collective-permute-done.25
  324.6 2.8 copy-done.6
  327.4 2.7 fusion.7
  330.2 13.4 %convolution_convert_fusion = bf16[640,5120]{1,0:T(8,128)(2,1)} fusion(bf16[1,256,5120]{2,1,0:T(8,128)(2,1)S(1)} %copy-done, f32[640,256]{1,0:T(8,128)} %fusion.7, bf16[640,5120]{1,0:T(8,128)(2,1)} %copy-done.6, bf16[1,5120,256]{2,1,0:T(8,128)(2,1)} %param.23), kind=kOutput, calls=%fused_computation.2 | convolution fusion | flops 3359703040 | bytes 19005440 | tf_op jit(solution)/shard_map/dot_general | solution.py:171
  348.5 5.6 %fusion.9 = f32[640,256]{1,0:T(8,128)} fusion(bf16[640,5120]{1,0:T(8,128)(2,1)} %constant_dynamic-update-slice_fusion, bf16[1,5120,256]{2,1,0:T(8,128)(2,1)S(1)} %copy-done.16), kind=kOutput, calls=%fused_computation.18 | convolution fusion | flops 1677721600 | bytes 9830400 | tf_op jit(solution)/shard_map/dot_general | solution.py:169
  354.1 13.4 %convolution_convert_fusion.1 = bf16[640,5120]{1,0:T(8,128)(2,1)} fusion(bf16[1,256,5120]{2,1,0:T(8,128)(2,1)S(1)} %copy-done, f32[640,256]{1,0:T(8,128)} %fusion.9, bf16[640,5120]{1,0:T(8,128)(2,1)} %constant_dynamic-update-slice_fusion, bf16[1,5120,256]{2,1,0:T(8,128)(2,1)} %param.23), kind=kOutput, calls=%fused_computation.3 | convolution fusion | flops 3359703040 | bytes 19005440 | tf_op jit(solution)/shard_map/dot_general | solution.py:171
  367.5 3.3 add_convert_fusion.7
  373.9 18.1 %collective-permute-done.30 = bf16[80,5120]{1,0:T(8,128)(2,1)S(1)} collective-permute-done((bf16[80,5120]{1,0:T(8,128)(2,1)S(1)}, bf16[80,5120]{1,0:T(8,128)(2,1)S(1)}, u32[]{:S(2)}, u32[]{:S(2)}) %collective-permute-start.30) | collective-permute-done | bytes 819232 | tf_op jit(solution)/shard_map/ppermute | solution.py:19
  393.5 2.8 collective-permute-start.28
  396.3 17.2 %collective-permute-done.31 = bf16[80,5120]{1,0:T(8,128)(2,1)S(1)} collective-permute-done((bf16[80,5120]{1,0:T(8,128)(2,1)S(1)}, bf16[80,5120]{1,0:T(8,128)(2,1)S(1)}, u32[]{:S(2)}, u32[]{:S(2)}) %collective-permute-start.31) | collective-permute-done | bytes 819232 | tf_op jit(solution)/shard_map/ppermute | solution.py:19
  413.5 2.9 add_convert_fusion.5
  416.4 2.7 collective-permute-start.29
  419.1 16.5 %collective-permute-done.32 = bf16[80,5120]{1,0:T(8,128)(2,1)S(1)} collective-permute-done((bf16[80,5120]{1,0:T(8,128)(2,1)S(1)}, bf16[80,5120]{1,0:T(8,128)(2,1)S(1)}, u32[]{:S(2)}, u32[]{:S(2)}) %collective-permute-start.32) | collective-permute-done | bytes 819232 | tf_op jit(solution)/shard_map/ppermute | solution.py:19
  435.6 5.0 collective-permute-done.33
  440.5 2.7 add_convert_fusion
  445.5 55.6 %all_to_all.26 = bf16[16,5,5120]{2,1,0:T(8,128)(2,1)S(1)} all-to-all(bf16[16,5,5120]{2,1,0:T(8,128)(2,1)} %reshape.263), channel_id=1, replica_groups=mesh['x'=4,'zh'=2,'core'=2,'zl'=4,'y'=4] {'zl','y'}, dimensions={0} | all-to-all | bytes 1638400 | tf_op jit(solution)/shard_map/all_to_all | solution.py:177
  (135 shorter events, 50.9 us)
Async XLA Ops:
  6.5 323.6 %copy-start = (bf16[1,256,5120]{2,1,0:T(8,128)(2,1)S(1)}, bf16[1,256,5120]{2,1,0:T(8,128)(2,1)}, u32[]{:S(2)}) copy-start(bf16[1,256,5120]{2,1,0:T(8,128)(2,1)} %param.25) | copy-start | bytes 7864324
  6.5 36.1 %copy-start.18 = (s32[1,4]{1,0:T(1,128)S(1)}, s32[1,4]{1,0:T(1,128)}, u32[]{:S(2)}) copy-start(s32[1,4]{1,0:T(1,128)} %param.17) | copy-start | bytes 52
  6.5 99.8 %all-gather.3.cloned.1.call-start = ((), (), s32[]{:S(2)}) async-start(), calls=%async_computation.3 | async-start | bytes 2785280 | tf_op jit(solution)/shard_map/all_gather | solution.py:123
  8.7 14.4 %collective-permute-start = (bf16[64,1024]{0,1:T(8,128)(2,1)S(1)}, bf16[64,1024]{0,1:T(8,128)(2,1)S(1)}, u32[]{:S(2)}, u32[]{:S(2)}) collective-permute-start(bf16[64,1024]{0,1:T(8,128)(2,1)S(1)} %pad_maximum_fusion.1), channel_id=1, source_target_pairs={{0,32},{32,0},{1,33},{33,1},{2,34},{34,2},{3,35},{35,3},{4,36},{36... | collective-permute-start | bytes 393224 | tf_op jit(solution)/shard_map/ppermute | solution.py:19
  16.5 9.6 %collective-permute-start.1 = (bf16[64,1024]{0,1:T(8,128)(2,1)S(1)}, bf16[64,1024]{0,1:T(8,128)(2,1)S(1)}, u32[]{:S(2)}, u32[]{:S(2)}) collective-permute-start(bf16[64,1024]{0,1:T(8,128)(2,1)S(1)} %pad_maximum_fusion.1), channel_id=1, source_target_pairs={{0,64},{64,128},{128,192},{192,0},{1,65},{65,129},{129,193},{193,1... | collective-permute-start | bytes 393224 | tf_op jit(solution)/shard_map/ppermute | solution.py:19
  17.7 8.4 %collective-permute-start.3 = (bf16[64,1024]{0,1:T(8,128)(2,1)S(1)}, bf16[64,1024]{0,1:T(8,128)(2,1)}, u32[]{:S(2)}, u32[]{:S(2)}) collective-permute-start(bf16[64,1024]{0,1:T(8,128)(2,1)S(1)} %pad_maximum_fusion.1), channel_id=1, source_target_pairs={{0,192},{64,0},{128,64},{192,128},{1,193},{65,1},{129,65},{193,129... | collective-permute-start | bytes 393224 | tf_op jit(solution)/shard_map/ppermute | solution.py:19
  23.1 7.2 %collective-permute-start.4 = (bf16[64,1024]{0,1:T(8,128)(2,1)S(1)}, bf16[64,1024]{0,1:T(8,128)(2,1)S(1)}, u32[]{:S(2)}, u32[]{:S(2)}) collective-permute-start(bf16[64,1024]{0,1:T(8,128)(2,1)S(1)} %collective-permute-done), channel_id=1, source_target_pairs={{0,192},{64,0},{128,64},{192,128},{1,193},{65,1},{129,65},{193,129... | collective-permute-start | bytes 393224 | tf_op jit(solution)/shard_map/ppermute | solution.py:19
  26.0 7.5 %collective-permute-start.2 = (bf16[64,1024]{0,1:T(8,128)(2,1)S(1)}, bf16[64,1024]{0,1:T(8,128)(2,1)}, u32[]{:S(2)}, u32[]{:S(2)}) collective-permute-start(bf16[64,1024]{0,1:T(8,128)(2,1)S(1)} %collective-permute-done), channel_id=1, source_target_pairs={{0,64},{64,128},{128,192},{192,0},{1,65},{65,129},{129,193},{193,1... | collective-permute-start | bytes 393224 | tf_op jit(solution)/shard_map/ppermute | solution.py:19
  37.3 17.4 %collective-permute-start.7 = (bf16[384,1024]{0,1:T(8,128)(2,1)}, bf16[384,1024]{0,1:T(8,128)(2,1)}, u32[]{:S(2)}, u32[]{:S(2)}) collective-permute-start(bf16[384,1024]{0,1:T(8,128)(2,1)} %concatenate.63), channel_id=1, source_target_pairs={{0,16},{16,0},{1,17},{17,1},{2,18},{18,2},{3,19},{19,3},{4,20},{20... | collective-permute-start | bytes 2359304 | tf_op jit(solution)/shard_map/ppermute | solution.py:19
  39.9 9.1 %collective-permute-start.5 = (bf16[64,1024]{0,1:T(8,128)(2,1)S(1)}, bf16[64,1024]{0,1:T(8,128)(2,1)}, u32[]{:S(2)}, u32[]{:S(2)}) collective-permute-start(bf16[64,1024]{0,1:T(8,128)(2,1)S(1)} %collective-permute-done.1), channel_id=1, source_target_pairs={{0,64},{64,128},{128,192},{192,0},{1,65},{65,129},{129,193},{193,1... | collective-permute-start | bytes 393224 | tf_op jit(solution)/shard_map/ppermute | solution.py:19
  39.9 9.1 %collective-permute-start.6 = (bf16[64,1024]{0,1:T(8,128)(2,1)}, bf16[64,1024]{0,1:T(8,128)(2,1)}, u32[]{:S(2)}, u32[]{:S(2)}) collective-permute-start(bf16[64,1024]{0,1:T(8,128)(2,1)} %copy-done.10), channel_id=1, source_target_pairs={{0,192},{64,0},{128,64},{192,128},{1,193},{65,1},{129,65},{193,129... | collective-permute-start | bytes 393224 | tf_op jit(solution)/shard_map/ppermute | solution.py:19
  50.9 3.8 collective-permute-start.8
  74.9 28.2 %all-to-all-start = ((bf16[64,16,160]{2,0,1:T(8,128)(2,1)}), bf16[64,16,160]{2,0,1:T(8,128)(2,1)S(1)}, u32[]{:S(2)}, u32[]{:S(2)}) async-start(bf16[64,16,160]{2,0,1:T(8,128)(2,1)} %copy.41), calls=%async_computation | async-start | bytes 1048576 | tf_op jit(solution)/shard_map/all_to_all | solution.py:124
  106.4 4.1 copy-start.9
  110.5 3.9 copy-start.1
  113.6 9.1 %collective-permute-start.9 = (bf16[512,5120]{1,0:T(8,128)(2,1)S(1)}, bf16[512,5120]{1,0:T(8,128)(2,1)S(1)}, u32[]{:S(2)}, u32[]{:S(2)}) collective-permute-start(bf16[512,5120]{1,0:T(8,128)(2,1)S(1)} %convolution_convert_fusion.2), channel_id=1, source_target_pairs={{0,16},{16,0},{1,17},{17,1},{2,18},{18,2},{3,19},{19,3},{4,20},{20... | collective-permute-start | bytes 15728648 | tf_op jit(solution)/shard_map/ppermute | solution.py:19
  123.3 20.4 %copy-start.13 = (bf16[5120]{0:T(1024)(128)(2,1)S(1)}, bf16[5120]{0:T(1024)(128)(2,1)}, u32[]{:S(2)}) copy-start(bf16[5120]{0:T(1024)(128)(2,1)} %param.20) | copy-start | bytes 30724
  123.3 17.2 %collective-permute-start.13 = (bf16[64,5120]{1,0:T(8,128)(2,1)S(1)}, bf16[64,5120]{1,0:T(8,128)(2,1)S(1)}, u32[]{:S(2)}, u32[]{:S(2)}) collective-permute-start(bf16[64,5120]{1,0:T(8,128)(2,1)S(1)} %get-tuple-element.27), channel_id=1, source_target_pairs={{0,64},{64,128},{128,192},{192,0},{1,65},{65,129},{129,193},{193,1... | collective-permute-start | bytes 1966088 | tf_op jit(solution)/shard_map/ppermute | solution.py:19
  123.4 17.6 %collective-permute-start.10 = (bf16[64,5120]{1,0:T(8,128)(2,1)S(1)}, bf16[64,5120]{1,0:T(8,128)(2,1)S(1)}, u32[]{:S(2)}, u32[]{:S(2)}) collective-permute-start(bf16[64,5120]{1,0:T(8,128)(2,1)S(1)} %get-tuple-element.28), channel_id=1, source_target_pairs={{0,192},{64,0},{128,64},{192,128},{1,193},{65,1},{129,65},{193,129... | collective-permute-start | bytes 1966088 | tf_op jit(solution)/shard_map/ppermute | solution.py:19
  140.7 16.5 %collective-permute-start.14 = (bf16[64,5120]{1,0:T(8,128)(2,1)S(1)}, bf16[64,5120]{1,0:T(8,128)(2,1)S(1)}, u32[]{:S(2)}, u32[]{:S(2)}) collective-permute-start(bf16[64,5120]{1,0:T(8,128)(2,1)S(1)} %add_convert_fusion.10), channel_id=1, source_target_pairs={{0,64},{64,128},{128,192},{192,0},{1,65},{65,129},{129,193},{193,1... | collective-permute-start | bytes 1966088 | tf_op jit(solution)/shard_map/ppermute | solution.py:19
  141.0 16.3 %collective-permute-start.11 = (bf16[64,5120]{1,0:T(8,128)(2,1)S(1)}, bf16[64,5120]{1,0:T(8,128)(2,1)S(1)}, u32[]{:S(2)}, u32[]{:S(2)}) collective-permute-start(bf16[64,5120]{1,0:T(8,128)(2,1)S(1)} %get-tuple-element.9), channel_id=1, source_target_pairs={{0,192},{64,0},{128,64},{192,128},{1,193},{65,1},{129,65},{193,129... | collective-permute-start | bytes 1966088 | tf_op jit(solution)/shard_map/ppermute | solution.py:19
  143.7 17.4 %copy-start.14 = (s32[1,64,1]{1,2,0:T(1,128)S(1)}, s32[1,64,1]{1,2,0:T(1,128)}, u32[]{:S(2)}) copy-start(s32[1,64,1]{1,2,0:T(1,128)} %param.22) | copy-start | bytes 772
  143.7 35.0 %copy-start.3 = (bf16[1,64,5120]{2,1,0:T(8,128)(2,1)S(1)}, bf16[1,64,5120]{2,1,0:T(8,128)(2,1)}, u32[]{:S(2)}) copy-start(bf16[1,64,5120]{2,1,0:T(8,128)(2,1)} %param.18) | copy-start | bytes 1966084
  158.2 21.2 %copy-start.17 = (bf16[5120,16]{0,1:T(8,128)(2,1)S(1)}, bf16[5120,16]{0,1:T(8,128)(2,1)}, u32[]{:S(2)}) copy-start(bf16[5120,16]{0,1:T(8,128)(2,1)} %param.21) | copy-start | bytes 491524
  158.2 15.5 %collective-permute-start.15 = (bf16[64,5120]{1,0:T(8,128)(2,1)S(1)}, bf16[64,5120]{1,0:T(8,128)(2,1)S(1)}, u32[]{:S(2)}, u32[]{:S(2)}) collective-permute-start(bf16[64,5120]{1,0:T(8,128)(2,1)S(1)} %get-tuple-element.10), channel_id=1, source_target_pairs={{0,64},{64,128},{128,192},{192,0},{1,65},{65,129},{129,193},{193,1... | collective-permute-start | bytes 1966088 | tf_op jit(solution)/shard_map/ppermute | solution.py:19
  158.3 15.4 %collective-permute-start.12 = (bf16[64,5120]{1,0:T(8,128)(2,1)S(1)}, bf16[64,5120]{1,0:T(8,128)(2,1)S(1)}, u32[]{:S(2)}, u32[]{:S(2)}) collective-permute-start(bf16[64,5120]{1,0:T(8,128)(2,1)S(1)} %get-tuple-element.23), channel_id=1, source_target_pairs={{0,192},{64,0},{128,64},{192,128},{1,193},{65,1},{129,65},{193,129... | collective-permute-start | bytes 1966088 | tf_op jit(solution)/shard_map/ppermute | solution.py:19
  161.0 17.7 %collective-permute-start.16 = (bf16[64,5120]{1,0:T(8,128)(2,1)S(1)}, bf16[64,5120]{1,0:T(8,128)(2,1)S(1)}, u32[]{:S(2)}, u32[]{:S(2)}) collective-permute-start(bf16[64,5120]{1,0:T(8,128)(2,1)S(1)} %get-tuple-element.24), channel_id=1, source_target_pairs={{0,32},{32,0},{1,33},{33,1},{2,34},{34,2},{3,35},{35,3},{4,36},{36... | collective-permute-start | bytes 1966088 | tf_op jit(solution)/shard_map/ppermute | solution.py:19
  240.4 21.6 %collective-permute-start.17 = (bf16[80,5120]{1,0:T(8,128)(2,1)}, bf16[80,5120]{1,0:T(8,128)(2,1)S(1)}, u32[]{:S(2)}, u32[]{:S(2)}) collective-permute-start(bf16[80,5120]{1,0:T(8,128)(2,1)} %reshape.262), channel_id=1, source_target_pairs={{0,32},{32,0},{1,33},{33,1},{2,34},{34,2},{3,35},{35,3},{4,36},{36... | collective-permute-start | bytes 2457608 | tf_op jit(solution)/shard_map/ppermute | solution.py:19
  240.4 24.4 %collective-permute-start.18 = (bf16[80,5120]{1,0:T(8,128)(2,1)}, bf16[80,5120]{1,0:T(8,128)(2,1)S(1)}, u32[]{:S(2)}, u32[]{:S(2)}) collective-permute-start(bf16[80,5120]{1,0:T(8,128)(2,1)} %reshape.262), channel_id=1, source_target_pairs={{0,64},{64,128},{128,192},{192,0},{1,65},{65,129},{129,193},{193,1... | collective-permute-start | bytes 2457608 | tf_op jit(solution)/shard_map/ppermute | solution.py:19
  241.7 33.1 %collective-permute-start.20 = (bf16[80,5120]{1,0:T(8,128)(2,1)}, bf16[80,5120]{1,0:T(8,128)(2,1)S(1)}, u32[]{:S(2)}, u32[]{:S(2)}) collective-permute-start(bf16[80,5120]{1,0:T(8,128)(2,1)} %reshape.262), channel_id=1, source_target_pairs={{0,192},{64,0},{128,64},{192,128},{1,193},{65,1},{129,65},{193,129... | collective-permute-start | bytes 2457608 | tf_op jit(solution)/shard_map/ppermute | solution.py:19
  262.0 12.7 %collective-permute-start.19 = (bf16[80,5120]{1,0:T(8,128)(2,1)S(1)}, bf16[80,5120]{1,0:T(8,128)(2,1)S(1)}, u32[]{:S(2)}, u32[]{:S(2)}) collective-permute-start(bf16[80,5120]{1,0:T(8,128)(2,1)S(1)} %collective-permute-done.17), channel_id=1, source_target_pairs={{0,64},{64,128},{128,192},{192,0},{1,65},{65,129},{129,193},{193,1... | collective-permute-start | bytes 2457608 | tf_op jit(solution)/shard_map/ppermute | solution.py:19
  262.0 13.0 %collective-permute-start.21 = (bf16[80,5120]{1,0:T(8,128)(2,1)S(1)}, bf16[80,5120]{1,0:T(8,128)(2,1)S(1)}, u32[]{:S(2)}, u32[]{:S(2)}) collective-permute-start(bf16[80,5120]{1,0:T(8,128)(2,1)S(1)} %collective-permute-done.17), channel_id=1, source_target_pairs={{0,192},{64,0},{128,64},{192,128},{1,193},{65,1},{129,65},{193,129... | collective-permute-start | bytes 2457608 | tf_op jit(solution)/shard_map/ppermute | solution.py:19
  277.8 43.7 %collective-permute-start.24 = (bf16[480,5120]{1,0:T(8,128)(2,1)S(1)}, bf16[480,5120]{1,0:T(8,128)(2,1)S(1)}, u32[]{:S(2)}, u32[]{:S(2)}) collective-permute-start(bf16[480,5120]{1,0:T(8,128)(2,1)S(1)} %get-tuple-element.32), channel_id=1, source_target_pairs={{0,16},{16,0},{1,17},{17,1},{2,18},{18,2},{3,19},{19,3},{4,20},{20... | collective-permute-start | bytes 14745608 | tf_op jit(solution)/shard_map/ppermute | solution.py:19
  299.3 21.0 %collective-permute-start.22 = (bf16[80,5120]{1,0:T(8,128)(2,1)S(1)}, bf16[80,5120]{1,0:T(8,128)(2,1)S(1)}, u32[]{:S(2)}, u32[]{:S(2)}) collective-permute-start(bf16[80,5120]{1,0:T(8,128)(2,1)S(1)} %collective-permute-done.18), channel_id=1, source_target_pairs={{0,64},{64,128},{128,192},{192,0},{1,65},{65,129},{129,193},{193,1... | collective-permute-start | bytes 2457608 | tf_op jit(solution)/shard_map/ppermute | solution.py:19
  299.3 21.0 %collective-permute-start.23 = (bf16[80,5120]{1,0:T(8,128)(2,1)S(1)}, bf16[80,5120]{1,0:T(8,128)(2,1)S(1)}, u32[]{:S(2)}, u32[]{:S(2)}) collective-permute-start(bf16[80,5120]{1,0:T(8,128)(2,1)S(1)} %collective-permute-done.21), channel_id=1, source_target_pairs={{0,192},{64,0},{128,64},{192,128},{1,193},{65,1},{129,65},{193,129... | collective-permute-start | bytes 2457608 | tf_op jit(solution)/shard_map/ppermute | solution.py:19
  320.4 4.1 collective-permute-start.25
  321.8 5.6 %copy-start.15 = (bf16[1,5120,256]{2,1,0:T(8,128)(2,1)S(1)}, bf16[1,5120,256]{2,1,0:T(8,128)(2,1)}, u32[]{:S(2)}) copy-start(bf16[1,5120,256]{2,1,0:T(8,128)(2,1)} %param.24) | copy-start | bytes 7864324
  343.5 5.0 copy-start.16
  343.5 24.0 %collective-permute-start.26 = (bf16[640,5120]{1,0:T(8,128)(2,1)}, bf16[640,5120]{1,0:T(8,128)(2,1)}, u32[]{:S(2)}, u32[]{:S(2)}) collective-permute-start(bf16[640,5120]{1,0:T(8,128)(2,1)} %convolution_convert_fusion), channel_id=1, source_target_pairs={{0,16},{16,0},{1,17},{17,1},{2,18},{18,2},{3,19},{19,3},{4,20},{20... | collective-permute-start | bytes 19660808 | tf_op jit(solution)/shard_map/ppermute | solution.py:19
  367.5 24.5 %copy-start.2 = (bf16[640,5120]{1,0:T(8,128)(2,1)S(1)}, bf16[640,5120]{1,0:T(8,128)(2,1)}, u32[]{:S(2)}) copy-start(bf16[640,5120]{1,0:T(8,128)(2,1)} %convolution_convert_fusion.1) | copy-start | bytes 19660804
  370.9 21.1 %collective-permute-start.30 = (bf16[80,5120]{1,0:T(8,128)(2,1)S(1)}, bf16[80,5120]{1,0:T(8,128)(2,1)S(1)}, u32[]{:S(2)}, u32[]{:S(2)}) collective-permute-start(bf16[80,5120]{1,0:T(8,128)(2,1)S(1)} %get-tuple-element.21), channel_id=1, source_target_pairs={{0,64},{64,128},{128,192},{192,0},{1,65},{65,129},{129,193},{193,1... | collective-permute-start | bytes 2457608 | tf_op jit(solution)/shard_map/ppermute | solution.py:19
  372.0 21.5 %collective-permute-start.27 = (bf16[80,5120]{1,0:T(8,128)(2,1)S(1)}, bf16[80,5120]{1,0:T(8,128)(2,1)S(1)}, u32[]{:S(2)}, u32[]{:S(2)}) collective-permute-start(bf16[80,5120]{1,0:T(8,128)(2,1)S(1)} %get-tuple-element.22), channel_id=1, source_target_pairs={{0,192},{64,0},{128,64},{192,128},{1,193},{65,1},{129,65},{193,129... | collective-permute-start | bytes 2457608 | tf_op jit(solution)/shard_map/ppermute | solution.py:19
  393.4 20.1 %collective-permute-start.31 = (bf16[80,5120]{1,0:T(8,128)(2,1)S(1)}, bf16[80,5120]{1,0:T(8,128)(2,1)S(1)}, u32[]{:S(2)}, u32[]{:S(2)}) collective-permute-start(bf16[80,5120]{1,0:T(8,128)(2,1)S(1)} %add_convert_fusion.2), channel_id=1, source_target_pairs={{0,64},{64,128},{128,192},{192,0},{1,65},{65,129},{129,193},{193,1... | collective-permute-start | bytes 2457608 | tf_op jit(solution)/shard_map/ppermute | solution.py:19
  393.5 20.0 %collective-permute-start.28 = (bf16[80,5120]{1,0:T(8,128)(2,1)S(1)}, bf16[80,5120]{1,0:T(8,128)(2,1)S(1)}, u32[]{:S(2)}, u32[]{:S(2)}) collective-permute-start(bf16[80,5120]{1,0:T(8,128)(2,1)S(1)} %get-tuple-element.11), channel_id=1, source_target_pairs={{0,192},{64,0},{128,64},{192,128},{1,193},{65,1},{129,65},{193,129... | collective-permute-start | bytes 2457608 | tf_op jit(solution)/shard_map/ppermute | solution.py:19
  416.3 19.2 %collective-permute-start.32 = (bf16[80,5120]{1,0:T(8,128)(2,1)S(1)}, bf16[80,5120]{1,0:T(8,128)(2,1)S(1)}, u32[]{:S(2)}, u32[]{:S(2)}) collective-permute-start(bf16[80,5120]{1,0:T(8,128)(2,1)S(1)} %get-tuple-element.12), channel_id=1, source_target_pairs={{0,64},{64,128},{128,192},{192,0},{1,65},{65,129},{129,193},{193,1... | collective-permute-start | bytes 2457608 | tf_op jit(solution)/shard_map/ppermute | solution.py:19
  416.4 19.1 %collective-permute-start.29 = (bf16[80,5120]{1,0:T(8,128)(2,1)S(1)}, bf16[80,5120]{1,0:T(8,128)(2,1)S(1)}, u32[]{:S(2)}, u32[]{:S(2)}) collective-permute-start(bf16[80,5120]{1,0:T(8,128)(2,1)S(1)} %get-tuple-element.17), channel_id=1, source_target_pairs={{0,192},{64,0},{128,64},{192,128},{1,193},{65,1},{129,65},{193,129... | collective-permute-start | bytes 2457608 | tf_op jit(solution)/shard_map/ppermute | solution.py:19
  419.1 21.4 %collective-permute-start.33 = (bf16[80,5120]{1,0:T(8,128)(2,1)S(1)}, bf16[80,5120]{1,0:T(8,128)(2,1)S(1)}, u32[]{:S(2)}, u32[]{:S(2)}) collective-permute-start(bf16[80,5120]{1,0:T(8,128)(2,1)S(1)} %get-tuple-element.18), channel_id=1, source_target_pairs={{0,32},{32,0},{1,33},{33,1},{2,34},{34,2},{3,35},{35,3},{4,36},{36... | collective-permute-start | bytes 2457608 | tf_op jit(solution)/shard_map/ppermute | solution.py:19
  445.5 55.6 %copy-start.5 = (bf16[64,5120]{1,0:T(8,128)(2,1)S(1)}, bf16[64,5120]{1,0:T(8,128)(2,1)}, u32[]{:S(2)}) copy-start(bf16[64,5120]{1,0:T(8,128)(2,1)} %copy-done.4) | copy-start | bytes 1966084
  (7 other events, 12.9 us)
Sparse Core Ops, SparseCore 0:
  19.3 71.4 all-gather.2

commit v7 on v6

--- a/solution.py
+++ b/solution.py
@@ -32,13 +32,14 @@
 
 
 def ag_rel(b):
+    h = b.shape[0] // 2
     zo = _pp(b, "zh", 2, 1)
     l1 = _pp(b, "x", 4, 1)
     r1 = _pp(b, "x", 4, -1)
+    l2 = jnp.concatenate([_pp(l1[:h], "x", 4, 1), _pp(r1[h:], "x", 4, -1)], 0)
     l1o = _pp(zo, "x", 4, 1)
     r1o = _pp(zo, "x", 4, -1)
-    l2 = _pp(l1, "x", 4, 1)
-    r2o = _pp(r1o, "x", 4, -1)
+    r2o = jnp.concatenate([_pp(l1o[:h], "x", 4, 1), _pp(r1o[h:], "x", 4, -1)], 0)
     first = jnp.concatenate([b, zo, l1, l1o, r1, r1o], 0)
     last = jnp.concatenate([l2, r2o], 0)
     return jnp.concatenate([first, last, _pp(first, "core", 2, 1), _pp(last, "core", 2, 1)], 0)

time: 516 us -> 519 us (level)
    ppermute x34 -> x38, starting transfers between devices: 69.5 us -> 74.8 us  [_pp(): return lax.ppermute(v, axis, [(i, (i + shift) % n) for i in range(n)])]
    ppermute x34 -> x38, waiting for transfers between devices: 173 us -> 175 us  [_pp(): return lax.ppermute(v, axis, [(i, (i + shift) % n) for i in range(n)])]
    unnamed x49 -> x61, local copies, waits for them, and re-layouts: 16.9 us -> 16.9 us
  transfers between devices with their start and end apart: 36 -> 40, of which waited for: 18 -> 22; matrix products, arithmetic and copies ran while one was open for 12% -> 12% of each run, Pallas kernels for 0% -> 0%
where the time goes in v7:
time: 519 us; the launch traced here: 511 us
  waiting for transfers between devices  190 us (37%)
  blocking collectives  112 us (22%)
  starting transfers between devices  85.2 us (16%)
  matrix products  50.1 us (10%)
  local copies, waits for them, and re-layouts  42.7 us (8%)
  other arithmetic  16.6 us (3%)
  between operations  14.1 us (3%)
    ppermute x38, waiting for transfers between devices, _pp(): return lax.ppermute(v, axis, [(i, (i + shift) % n) for i in range(n)])  175 us
    ppermute x38, starting transfers between devices, _pp(): return lax.ppermute(v, axis, [(i, (i + shift) % n) for i in range(n)])  74.8 us
    all_to_all x1, blocking collectives, local(): lax.all_to_all(expert_out, EXP, split_axis=0, concat_axis=0, tiled=True)  58.2 us
    all_to_all x1, blocking collectives, local(): lax.all_to_all(outgoing, EXP, split_axis=0, concat_axis=0, tiled=True)  53.7 us
    dot_general x2, matrix products, expert_rows(): jnp.dot(inner, down_local, preferred_element_type=jnp.float32)  26.7 us
    unnamed x61, local copies, waits for them, and re-layouts  16.9 us
    all_to_all x1, waiting for transfers between devices, local(): lax.all_to_all(attended.reshape(tok_rows, n_ctx, qwidth // n_ctx), CTX, s...  15.3 us
    all_to_all x1, starting transfers between devices, local(): lax.all_to_all(attended.reshape(tok_rows, n_ctx, qwidth // n_ctx), CTX, s...  10.4 us
  transfers between devices with their start and end apart: 40, of which 22 were waited for; matrix products, arithmetic and copies ran while one was open for 12% of the time, Pallas kernels for 0%

profile of v7, /device:TPU:1, one launch (start us, length us, event | category | flops | bytes accessed | tf_op | source)
XLA Modules:
  0.0 511.1 jit_solution(12172294787714064478)
XLA Ops:
  8.7 7.8 %collective-permute-start = (bf16[64,1024]{0,1:T(8,128)(2,1)S(1)}, bf16[64,1024]{0,1:T(8,128)(2,1)}, u32[]{:S(2)}, u32[]{:S(2)}) collective-permute-start(bf16[64,1024]{0,1:T(8,128)(2,1)S(1)} %pad_maximum_fusion.1), channel_id=1, source_target_pairs={{0,32},{32,0},{1,33},{33,1},{2,34},{34,2},{3,35},{35,3},{4,36},{36... | collective-permute-start | bytes 393224 | tf_op jit(solution)/shard_map/ppermute | solution.py:19
  19.9 3.3 collective-permute-done
  26.2 5.0 collective-permute-done.2
  31.3 3.2 concatenate.63
  40.3 2.8 collective-permute-start.8
  43.0 2.8 collective-permute-done.6
  45.8 3.4 collective-permute-done.5
  51.4 3.4 collective-permute-done.7
  59.5 5.8 %concatenate.65 = bf16[1024,1024]{0,1:T(8,128)(2,1)} concatenate(bf16[64,1024]{0,1:T(8,128)(2,1)S(1)} %pad_maximum_fusion.1, bf16[64,1024]{0,1:T(8,128)(2,1)} %collective-permute-done, bf16[64,1024]{0,1:T(8,128)(2,1)} %collective-permute-done.1, bf16[64,1024]{0,1:T(8,128)(2,1)} %collective-permute-done.2, bf16[64,1024]{0,1:T(8,128)(2,1)S(1)} %collective-permute-done.3, ...), dimensions={0} | concatenate | bytes 4194304 | tf_op jit(solution)/shard_map/concatenate | solution.py:45
  65.3 3.1 fusion.86
  68.4 4.9 fusion.88
  73.3 2.9 fusion.26
  79.9 10.4 %all-to-all-start = ((bf16[64,16,160]{2,0,1:T(8,128)(2,1)}), bf16[64,16,160]{2,0,1:T(8,128)(2,1)S(1)}, u32[]{:S(2)}, u32[]{:S(2)}) async-start(bf16[64,16,160]{2,0,1:T(8,128)(2,1)} %copy.41), calls=%async_computation | async-start | bytes 1048576 | tf_op jit(solution)/shard_map/all_to_all | solution.py:125
  90.5 15.3 %all-to-all-done = bf16[64,16,160]{2,0,1:T(8,128)(2,1)S(1)} async-done(((bf16[64,16,160]{2,0,1:T(8,128)(2,1)}), bf16[64,16,160]{2,0,1:T(8,128)(2,1)S(1)}, u32[]{:S(2)}, u32[]{:S(2)}) %all-to-all-start) | async-done | bytes 327712 | tf_op jit(solution)/shard_map/all_to_all | solution.py:125
  108.4 4.1 reshape.274
  112.4 3.1 convolution_convert_fusion.2
  119.0 6.8 %collective-permute-done.11 = bf16[512,5120]{1,0:T(8,128)(2,1)S(1)} collective-permute-done((bf16[512,5120]{1,0:T(8,128)(2,1)S(1)}, bf16[512,5120]{1,0:T(8,128)(2,1)S(1)}, u32[]{:S(2)}, u32[]{:S(2)}) %collective-permute-start.11) | collective-permute-done | bytes 5242912 | tf_op jit(solution)/shard_map/ppermute | solution.py:19
  126.5 2.7 collective-permute-start.12
  129.1 14.5 %collective-permute-done.15 = bf16[64,5120]{1,0:T(8,128)(2,1)S(1)} collective-permute-done((bf16[64,5120]{1,0:T(8,128)(2,1)S(1)}, bf16[64,5120]{1,0:T(8,128)(2,1)S(1)}, u32[]{:S(2)}, u32[]{:S(2)}) %collective-permute-start.15) | collective-permute-done | bytes 655392 | tf_op jit(solution)/shard_map/ppermute | solution.py:19
  144.1 2.7 collective-permute-start.13
  146.8 13.6 %collective-permute-done.16 = bf16[64,5120]{1,0:T(8,128)(2,1)S(1)} collective-permute-done((bf16[64,5120]{1,0:T(8,128)(2,1)S(1)}, bf16[64,5120]{1,0:T(8,128)(2,1)S(1)}, u32[]{:S(2)}, u32[]{:S(2)}) %collective-permute-start.16) | collective-permute-done | bytes 655392 | tf_op jit(solution)/shard_map/ppermute | solution.py:19
  161.4 2.7 collective-permute-start.14
  164.4 12.5 %collective-permute-done.17 = bf16[64,5120]{1,0:T(8,128)(2,1)S(1)} collective-permute-done((bf16[64,5120]{1,0:T(8,128)(2,1)S(1)}, bf16[64,5120]{1,0:T(8,128)(2,1)S(1)}, u32[]{:S(2)}, u32[]{:S(2)}) %collective-permute-start.17) | collective-permute-done | bytes 655392 | tf_op jit(solution)/shard_map/ppermute | solution.py:19
  176.9 5.0 collective-permute-done.18
  184.0 53.7 %all_to_all.25 = bf16[16,5,5120]{2,1,0:T(8,128)(2,1)} all-to-all(bf16[16,5,5120]{2,1,0:T(8,128)(2,1)S(1)} %copy.42), channel_id=1, replica_groups=mesh['x'=4,'zh'=2,'core'=2,'zl'=4,'y'=4] {'zl','y'}, dimensions={0} | all-to-all | bytes 1638400 | tf_op jit(solution)/shard_map/all_to_all | solution.py:160
  241.4 2.7 collective-permute-start.22
  244.2 17.7 %collective-permute-done.19 = bf16[80,5120]{1,0:T(8,128)(2,1)S(1)} collective-permute-done((bf16[80,5120]{1,0:T(8,128)(2,1)}, bf16[80,5120]{1,0:T(8,128)(2,1)S(1)}, u32[]{:S(2)}, u32[]{:S(2)}) %collective-permute-start.19) | collective-permute-done | bytes 819232 | tf_op jit(solution)/shard_map/ppermute | solution.py:19
  261.8 2.7 collective-permute-start.23
  264.8 9.4 %collective-permute-done.21 = bf16[80,5120]{1,0:T(8,128)(2,1)S(1)} collective-permute-done((bf16[80,5120]{1,0:T(8,128)(2,1)S(1)}, bf16[80,5120]{1,0:T(8,128)(2,1)S(1)}, u32[]{:S(2)}, u32[]{:S(2)}) %collective-permute-start.21) | collective-permute-done | bytes 819232 | tf_op jit(solution)/shard_map/ppermute | solution.py:19
  274.7 19.8 %collective-permute-start.28 = (bf16[480,5120]{1,0:T(8,128)(2,1)S(1)}, bf16[480,5120]{1,0:T(8,128)(2,1)S(1)}, u32[]{:S(2)}, u32[]{:S(2)}) collective-permute-start(bf16[480,5120]{1,0:T(8,128)(2,1)S(1)} %get-tuple-element.32), channel_id=1, source_target_pairs={{0,16},{16,0},{1,17},{17,1},{2,18},{18,2},{3,19},{19,3},{4,20},{20... | collective-permute-start | bytes 14745608 | tf_op jit(solution)/shard_map/ppermute | solution.py:19
  298.0 2.7 collective-permute-start.27
  300.7 6.1 %collective-permute-done.24 = bf16[40,5120]{1,0:T(8,128)(2,1)S(1)} collective-permute-done((bf16[40,5120]{1,0:T(8,128)(2,1)S(1)}, bf16[40,5120]{1,0:T(8,128)(2,1)S(1)}, u32[]{:S(2)}, u32[]{:S(2)}) %collective-permute-start.24) | collective-permute-done | bytes 409632 | tf_op jit(solution)/shard_map/ppermute | solution.py:19
  306.8 8.8 %collective-permute-done.26 = bf16[40,5120]{1,0:T(8,128)(2,1)S(1)} collective-permute-done((bf16[40,5120]{1,0:T(8,128)(2,1)S(1)}, bf16[40,5120]{1,0:T(8,128)(2,1)S(1)}, u32[]{:S(2)}, u32[]{:S(2)}) %collective-permute-start.26) | collective-permute-done | bytes 409632 | tf_op jit(solution)/shard_map/ppermute | solution.py:19
  317.3 2.8 collective-permute-done.29
  320.2 2.8 copy-done.6
  323.0 2.7 fusion.7
  325.7 13.3 %convolution_convert_fusion = bf16[640,5120]{1,0:T(8,128)(2,1)} fusion(bf16[1,256,5120]{2,1,0:T(8,128)(2,1)S(1)} %copy-done, f32[640,256]{1,0:T(8,128)} %fusion.7, bf16[640,5120]{1,0:T(8,128)(2,1)} %copy-done.6, bf16[1,5120,256]{2,1,0:T(8,128)(2,1)} %param.23), kind=kOutput, calls=%fused_computation.2 | convolution fusion | flops 3359703040 | bytes 19005440 | tf_op jit(solution)/shard_map/dot_general | solution.py:172
  346.0 5.6 %fusion.9 = f32[640,256]{1,0:T(8,128)} fusion(bf16[640,5120]{1,0:T(8,128)(2,1)} %constant_dynamic-update-slice_fusion, bf16[1,5120,256]{2,1,0:T(8,128)(2,1)S(1)} %copy-done.21), kind=kOutput, calls=%fused_computation.18 | convolution fusion | flops 1677721600 | bytes 9830400 | tf_op jit(solution)/shard_map/dot_general | solution.py:170
  351.6 13.4 %convolution_convert_fusion.1 = bf16[640,5120]{1,0:T(8,128)(2,1)} fusion(bf16[1,256,5120]{2,1,0:T(8,128)(2,1)S(1)} %copy-done, f32[640,256]{1,0:T(8,128)} %fusion.9, bf16[640,5120]{1,0:T(8,128)(2,1)} %constant_dynamic-update-slice_fusion, bf16[1,5120,256]{2,1,0:T(8,128)(2,1)} %param.23), kind=kOutput, calls=%fused_computation.3 | convolution fusion | flops 3359703040 | bytes 19005440 | tf_op jit(solution)/shard_map/dot_general | solution.py:172
  365.0 3.3 add_convert_fusion.7
  371.4 18.5 %collective-permute-done.34 = bf16[80,5120]{1,0:T(8,128)(2,1)S(1)} collective-permute-done((bf16[80,5120]{1,0:T(8,128)(2,1)S(1)}, bf16[80,5120]{1,0:T(8,128)(2,1)S(1)}, u32[]{:S(2)}, u32[]{:S(2)}) %collective-permute-start.34) | collective-permute-done | bytes 819232 | tf_op jit(solution)/shard_map/ppermute | solution.py:19
  391.5 2.8 collective-permute-start.32
  394.3 17.5 %collective-permute-done.35 = bf16[80,5120]{1,0:T(8,128)(2,1)S(1)} collective-permute-done((bf16[80,5120]{1,0:T(8,128)(2,1)S(1)}, bf16[80,5120]{1,0:T(8,128)(2,1)S(1)}, u32[]{:S(2)}, u32[]{:S(2)}) %collective-permute-start.35) | collective-permute-done | bytes 819232 | tf_op jit(solution)/shard_map/ppermute | solution.py:19
  411.8 2.9 add_convert_fusion.5
  414.8 2.7 collective-permute-start.33
  417.5 16.9 %collective-permute-done.36 = bf16[80,5120]{1,0:T(8,128)(2,1)S(1)} collective-permute-done((bf16[80,5120]{1,0:T(8,128)(2,1)S(1)}, bf16[80,5120]{1,0:T(8,128)(2,1)S(1)}, u32[]{:S(2)}, u32[]{:S(2)}) %collective-permute-start.36) | collective-permute-done | bytes 819232 | tf_op jit(solution)/shard_map/ppermute | solution.py:19
  434.3 4.9 collective-permute-done.37
  444.2 58.2 %all_to_all.26 = bf16[16,5,5120]{2,1,0:T(8,128)(2,1)S(1)} all-to-all(bf16[16,5,5120]{2,1,0:T(8,128)(2,1)} %reshape.263), channel_id=1, replica_groups=mesh['x'=4,'zh'=2,'core'=2,'zl'=4,'y'=4] {'zl','y'}, dimensions={0} | all-to-all | bytes 1638400 | tf_op jit(solution)/shard_map/all_to_all | solution.py:178
  (161 shorter events, 63.5 us)
Async XLA Ops:
  6.5 319.1 %copy-start = (bf16[1,256,5120]{2,1,0:T(8,128)(2,1)S(1)}, bf16[1,256,5120]{2,1,0:T(8,128)(2,1)}, u32[]{:S(2)}) copy-start(bf16[1,256,5120]{2,1,0:T(8,128)(2,1)} %param.25) | copy-start | bytes 7864324
  6.5 30.6 %copy-start.23 = (s32[1,4]{1,0:T(1,128)S(1)}, s32[1,4]{1,0:T(1,128)}, u32[]{:S(2)}) copy-start(s32[1,4]{1,0:T(1,128)} %param.17) | copy-start | bytes 52
  6.5 101.8 %all-gather.3.cloned.1.call-start = ((), (), s32[]{:S(2)}) async-start(), calls=%async_computation.3 | async-start | bytes 2785280 | tf_op jit(solution)/shard_map/all_gather | solution.py:124
  8.7 14.5 %collective-permute-start = (bf16[64,1024]{0,1:T(8,128)(2,1)S(1)}, bf16[64,1024]{0,1:T(8,128)(2,1)}, u32[]{:S(2)}, u32[]{:S(2)}) collective-permute-start(bf16[64,1024]{0,1:T(8,128)(2,1)S(1)} %pad_maximum_fusion.1), channel_id=1, source_target_pairs={{0,32},{32,0},{1,33},{33,1},{2,34},{34,2},{3,35},{35,3},{4,36},{36... | collective-permute-start | bytes 393224 | tf_op jit(solution)/shard_map/ppermute | solution.py:19
  16.5 9.7 %collective-permute-start.1 = (bf16[64,1024]{0,1:T(8,128)(2,1)S(1)}, bf16[64,1024]{0,1:T(8,128)(2,1)}, u32[]{:S(2)}, u32[]{:S(2)}) collective-permute-start(bf16[64,1024]{0,1:T(8,128)(2,1)S(1)} %pad_maximum_fusion.1), channel_id=1, source_target_pairs={{0,64},{64,128},{128,192},{192,0},{1,65},{65,129},{129,193},{193,1... | collective-permute-start | bytes 393224 | tf_op jit(solution)/shard_map/ppermute | solution.py:19
  17.7 8.5 %collective-permute-start.3 = (bf16[64,1024]{0,1:T(8,128)(2,1)S(1)}, bf16[64,1024]{0,1:T(8,128)(2,1)S(1)}, u32[]{:S(2)}, u32[]{:S(2)}) collective-permute-start(bf16[64,1024]{0,1:T(8,128)(2,1)S(1)} %pad_maximum_fusion.1), channel_id=1, source_target_pairs={{0,192},{64,0},{128,64},{192,128},{1,193},{65,1},{129,65},{193,129... | collective-permute-start | bytes 393224 | tf_op jit(solution)/shard_map/ppermute | solution.py:19
  23.2 8.1 %collective-permute-start.2 = (bf16[64,1024]{0,1:T(8,128)(2,1)}, bf16[64,1024]{0,1:T(8,128)(2,1)}, u32[]{:S(2)}, u32[]{:S(2)}) collective-permute-start(bf16[64,1024]{0,1:T(8,128)(2,1)} %collective-permute-done), channel_id=1, source_target_pairs={{0,64},{64,128},{128,192},{192,0},{1,65},{65,129},{129,193},{193,1... | collective-permute-start | bytes 393224 | tf_op jit(solution)/shard_map/ppermute | solution.py:19
  24.8 6.5 %collective-permute-start.4 = (bf16[64,1024]{0,1:T(8,128)(2,1)}, bf16[64,1024]{0,1:T(8,128)(2,1)S(1)}, u32[]{:S(2)}, u32[]{:S(2)}) collective-permute-start(bf16[64,1024]{0,1:T(8,128)(2,1)} %collective-permute-done), channel_id=1, source_target_pairs={{0,192},{64,0},{128,64},{192,128},{1,193},{65,1},{129,65},{193,129... | collective-permute-start | bytes 393224 | tf_op jit(solution)/shard_map/ppermute | solution.py:19
  34.6 24.9 %collective-permute-start.9 = (bf16[384,1024]{0,1:T(8,128)(2,1)}, bf16[384,1024]{0,1:T(8,128)(2,1)}, u32[]{:S(2)}, u32[]{:S(2)}) collective-permute-start(bf16[384,1024]{0,1:T(8,128)(2,1)} %concatenate.63), channel_id=1, source_target_pairs={{0,16},{16,0},{1,17},{17,1},{2,18},{18,2},{3,19},{19,3},{4,20},{20... | collective-permute-start | bytes 2359304 | tf_op jit(solution)/shard_map/ppermute | solution.py:19
  37.6 8.2 %collective-permute-start.6 = (bf16[32,1024]{0,1:T(8,128)(2,1)S(1)}, bf16[32,1024]{0,1:T(8,128)(2,1)S(1)}, u32[]{:S(2)}, u32[]{:S(2)}) collective-permute-start(bf16[32,1024]{0,1:T(8,128)(2,1)S(1)} %slice.191), channel_id=1, source_target_pairs={{0,192},{64,0},{128,64},{192,128},{1,193},{65,1},{129,65},{193,129... | collective-permute-start | bytes 196616 | tf_op jit(solution)/shard_map/ppermute | solution.py:19
  40.1 9.1 %collective-permute-start.5 = (bf16[32,1024]{0,1:T(8,128)(2,1)}, bf16[32,1024]{0,1:T(8,128)(2,1)S(1)}, u32[]{:S(2)}, u32[]{:S(2)}) collective-permute-start(bf16[32,1024]{0,1:T(8,128)(2,1)} %bitcast.107), channel_id=1, source_target_pairs={{0,64},{64,128},{128,192},{192,0},{1,65},{65,129},{129,193},{193,1... | collective-permute-start | bytes 196616 | tf_op jit(solution)/shard_map/ppermute | solution.py:19
  40.3 11.1 %collective-permute-start.8 = (bf16[32,1024]{0,1:T(8,128)(2,1)S(1)}, bf16[32,1024]{0,1:T(8,128)(2,1)S(1)}, u32[]{:S(2)}, u32[]{:S(2)}) collective-permute-start(bf16[32,1024]{0,1:T(8,128)(2,1)S(1)} %slice.193), channel_id=1, source_target_pairs={{0,192},{64,0},{128,64},{192,128},{1,193},{65,1},{129,65},{193,129... | collective-permute-start | bytes 196616 | tf_op jit(solution)/shard_map/ppermute | solution.py:19
  43.0 11.8 %collective-permute-start.7 = (bf16[32,1024]{0,1:T(8,128)(2,1)}, bf16[32,1024]{0,1:T(8,128)(2,1)S(1)}, u32[]{:S(2)}, u32[]{:S(2)}) collective-permute-start(bf16[32,1024]{0,1:T(8,128)(2,1)} %bitcast.108), channel_id=1, source_target_pairs={{0,64},{64,128},{128,192},{192,0},{1,65},{65,129},{129,193},{193,1... | collective-permute-start | bytes 196616 | tf_op jit(solution)/shard_map/ppermute | solution.py:19
  55.9 3.6 collective-permute-start.10
  79.9 25.9 %all-to-all-start = ((bf16[64,16,160]{2,0,1:T(8,128)(2,1)}), bf16[64,16,160]{2,0,1:T(8,128)(2,1)S(1)}, u32[]{:S(2)}, u32[]{:S(2)}) async-start(bf16[64,16,160]{2,0,1:T(8,128)(2,1)} %copy.41), calls=%async_computation | async-start | bytes 1048576 | tf_op jit(solution)/shard_map/all_to_all | solution.py:125
  115.5 10.3 %collective-permute-start.11 = (bf16[512,5120]{1,0:T(8,128)(2,1)S(1)}, bf16[512,5120]{1,0:T(8,128)(2,1)S(1)}, u32[]{:S(2)}, u32[]{:S(2)}) collective-permute-start(bf16[512,5120]{1,0:T(8,128)(2,1)S(1)} %convolution_convert_fusion.2), channel_id=1, source_target_pairs={{0,16},{16,0},{1,17},{17,1},{2,18},{18,2},{3,19},{19,3},{4,20},{20... | collective-permute-start | bytes 15728648 | tf_op jit(solution)/shard_map/ppermute | solution.py:19
  126.4 20.4 %copy-start.18 = (bf16[5120]{0:T(1024)(128)(2,1)S(1)}, bf16[5120]{0:T(1024)(128)(2,1)}, u32[]{:S(2)}) copy-start(bf16[5120]{0:T(1024)(128)(2,1)} %param.20) | copy-start | bytes 30724
  126.4 17.2 %collective-permute-start.15 = (bf16[64,5120]{1,0:T(8,128)(2,1)S(1)}, bf16[64,5120]{1,0:T(8,128)(2,1)S(1)}, u32[]{:S(2)}, u32[]{:S(2)}) collective-permute-start(bf16[64,5120]{1,0:T(8,128)(2,1)S(1)} %get-tuple-element.27), channel_id=1, source_target_pairs={{0,64},{64,128},{128,192},{192,0},{1,65},{65,129},{129,193},{193,1... | collective-permute-start | bytes 1966088 | tf_op jit(solution)/shard_map/ppermute | solution.py:19
  126.5 17.7 %collective-permute-start.12 = (bf16[64,5120]{1,0:T(8,128)(2,1)S(1)}, bf16[64,5120]{1,0:T(8,128)(2,1)S(1)}, u32[]{:S(2)}, u32[]{:S(2)}) collective-permute-start(bf16[64,5120]{1,0:T(8,128)(2,1)S(1)} %get-tuple-element.28), channel_id=1, source_target_pairs={{0,192},{64,0},{128,64},{192,128},{1,193},{65,1},{129,65},{193,129... | collective-permute-start | bytes 1966088 | tf_op jit(solution)/shard_map/ppermute | solution.py:19
  143.8 16.6 %collective-permute-start.16 = (bf16[64,5120]{1,0:T(8,128)(2,1)S(1)}, bf16[64,5120]{1,0:T(8,128)(2,1)S(1)}, u32[]{:S(2)}, u32[]{:S(2)}) collective-permute-start(bf16[64,5120]{1,0:T(8,128)(2,1)S(1)} %add_convert_fusion.10), channel_id=1, source_target_pairs={{0,64},{64,128},{128,192},{192,0},{1,65},{65,129},{129,193},{193,1... | collective-permute-start | bytes 1966088 | tf_op jit(solution)/shard_map/ppermute | solution.py:19
  144.1 16.3 %collective-permute-start.13 = (bf16[64,5120]{1,0:T(8,128)(2,1)S(1)}, bf16[64,5120]{1,0:T(8,128)(2,1)S(1)}, u32[]{:S(2)}, u32[]{:S(2)}) collective-permute-start(bf16[64,5120]{1,0:T(8,128)(2,1)S(1)} %get-tuple-element.9), channel_id=1, source_target_pairs={{0,192},{64,0},{128,64},{192,128},{1,193},{65,1},{129,65},{193,129... | collective-permute-start | bytes 1966088 | tf_op jit(solution)/shard_map/ppermute | solution.py:19
  146.8 35.0 %copy-start.3 = (bf16[1,64,5120]{2,1,0:T(8,128)(2,1)S(1)}, bf16[1,64,5120]{2,1,0:T(8,128)(2,1)}, u32[]{:S(2)}) copy-start(bf16[1,64,5120]{2,1,0:T(8,128)(2,1)} %param.18) | copy-start | bytes 1966084
  161.3 21.2 %copy-start.22 = (bf16[5120,16]{0,1:T(8,128)(2,1)S(1)}, bf16[5120,16]{0,1:T(8,128)(2,1)}, u32[]{:S(2)}) copy-start(bf16[5120,16]{0,1:T(8,128)(2,1)} %param.21) | copy-start | bytes 491524
  161.4 15.5 %collective-permute-start.17 = (bf16[64,5120]{1,0:T(8,128)(2,1)S(1)}, bf16[64,5120]{1,0:T(8,128)(2,1)S(1)}, u32[]{:S(2)}, u32[]{:S(2)}) collective-permute-start(bf16[64,5120]{1,0:T(8,128)(2,1)S(1)} %get-tuple-element.10), channel_id=1, source_target_pairs={{0,64},{64,128},{128,192},{192,0},{1,65},{65,129},{129,193},{193,1... | collective-permute-start | bytes 1966088 | tf_op jit(solution)/shard_map/ppermute | solution.py:19
  161.4 15.4 %collective-permute-start.14 = (bf16[64,5120]{1,0:T(8,128)(2,1)S(1)}, bf16[64,5120]{1,0:T(8,128)(2,1)S(1)}, u32[]{:S(2)}, u32[]{:S(2)}) collective-permute-start(bf16[64,5120]{1,0:T(8,128)(2,1)S(1)} %get-tuple-element.23), channel_id=1, source_target_pairs={{0,192},{64,0},{128,64},{192,128},{1,193},{65,1},{129,65},{193,129... | collective-permute-start | bytes 1966088 | tf_op jit(solution)/shard_map/ppermute | solution.py:19
  164.1 17.7 %collective-permute-start.18 = (bf16[64,5120]{1,0:T(8,128)(2,1)S(1)}, bf16[64,5120]{1,0:T(8,128)(2,1)S(1)}, u32[]{:S(2)}, u32[]{:S(2)}) collective-permute-start(bf16[64,5120]{1,0:T(8,128)(2,1)S(1)} %get-tuple-element.24), channel_id=1, source_target_pairs={{0,32},{32,0},{1,33},{33,1},{2,34},{34,2},{3,35},{35,3},{4,36},{36... | collective-permute-start | bytes 1966088 | tf_op jit(solution)/shard_map/ppermute | solution.py:19
  239.9 22.0 %collective-permute-start.19 = (bf16[80,5120]{1,0:T(8,128)(2,1)}, bf16[80,5120]{1,0:T(8,128)(2,1)S(1)}, u32[]{:S(2)}, u32[]{:S(2)}) collective-permute-start(bf16[80,5120]{1,0:T(8,128)(2,1)} %reshape.262), channel_id=1, source_target_pairs={{0,32},{32,0},{1,33},{33,1},{2,34},{34,2},{3,35},{35,3},{4,36},{36... | collective-permute-start | bytes 2457608 | tf_op jit(solution)/shard_map/ppermute | solution.py:19
  240.1 24.5 %collective-permute-start.20 = (bf16[80,5120]{1,0:T(8,128)(2,1)}, bf16[80,5120]{1,0:T(8,128)(2,1)S(1)}, u32[]{:S(2)}, u32[]{:S(2)}) collective-permute-start(bf16[80,5120]{1,0:T(8,128)(2,1)} %reshape.262), channel_id=1, source_target_pairs={{0,64},{64,128},{128,192},{192,0},{1,65},{65,129},{129,193},{193,1... | collective-permute-start | bytes 2457608 | tf_op jit(solution)/shard_map/ppermute | solution.py:19
  241.4 32.9 %collective-permute-start.22 = (bf16[80,5120]{1,0:T(8,128)(2,1)}, bf16[80,5120]{1,0:T(8,128)(2,1)S(1)}, u32[]{:S(2)}, u32[]{:S(2)}) collective-permute-start(bf16[80,5120]{1,0:T(8,128)(2,1)} %reshape.262), channel_id=1, source_target_pairs={{0,192},{64,0},{128,64},{192,128},{1,193},{65,1},{129,65},{193,129... | collective-permute-start | bytes 2457608 | tf_op jit(solution)/shard_map/ppermute | solution.py:19
  261.8 12.4 %collective-permute-start.21 = (bf16[80,5120]{1,0:T(8,128)(2,1)S(1)}, bf16[80,5120]{1,0:T(8,128)(2,1)S(1)}, u32[]{:S(2)}, u32[]{:S(2)}) collective-permute-start(bf16[80,5120]{1,0:T(8,128)(2,1)S(1)} %collective-permute-done.19), channel_id=1, source_target_pairs={{0,64},{64,128},{128,192},{192,0},{1,65},{65,129},{129,193},{193,1... | collective-permute-start | bytes 2457608 | tf_op jit(solution)/shard_map/ppermute | solution.py:19
  261.8 12.7 %collective-permute-start.23 = (bf16[80,5120]{1,0:T(8,128)(2,1)S(1)}, bf16[80,5120]{1,0:T(8,128)(2,1)S(1)}, u32[]{:S(2)}, u32[]{:S(2)}) collective-permute-start(bf16[80,5120]{1,0:T(8,128)(2,1)S(1)} %collective-permute-done.19), channel_id=1, source_target_pairs={{0,192},{64,0},{128,64},{192,128},{1,193},{65,1},{129,65},{193,129... | collective-permute-start | bytes 2457608 | tf_op jit(solution)/shard_map/ppermute | solution.py:19
  274.7 40.9 %copy-start.17 = (bf16[640,5120]{1,0:T(8,128)(2,1)}, bf16[640,5120]{1,0:T(8,128)(2,1)S(1)}, u32[]{:S(2)}) copy-start(bf16[640,5120]{1,0:T(8,128)(2,1)S(1)} %get-tuple-element.31) | copy-start | bytes 19660804
  274.7 42.3 %collective-permute-start.28 = (bf16[480,5120]{1,0:T(8,128)(2,1)S(1)}, bf16[480,5120]{1,0:T(8,128)(2,1)S(1)}, u32[]{:S(2)}, u32[]{:S(2)}) collective-permute-start(bf16[480,5120]{1,0:T(8,128)(2,1)S(1)} %get-tuple-element.32), channel_id=1, source_target_pairs={{0,16},{16,0},{1,17},{17,1},{2,18},{18,2},{3,19},{19,3},{4,20},{20... | collective-permute-start | bytes 14745608 | tf_op jit(solution)/shard_map/ppermute | solution.py:19
  294.5 12.3 %collective-permute-start.24 = (bf16[40,5120]{1,0:T(8,128)(2,1)S(1)}, bf16[40,5120]{1,0:T(8,128)(2,1)S(1)}, u32[]{:S(2)}, u32[]{:S(2)}) collective-permute-start(bf16[40,5120]{1,0:T(8,128)(2,1)S(1)} %slice.214), channel_id=1, source_target_pairs={{0,64},{64,128},{128,192},{192,0},{1,65},{65,129},{129,193},{193,1... | collective-permute-start | bytes 1228808 | tf_op jit(solution)/shard_map/ppermute | solution.py:19
  295.6 11.3 %collective-permute-start.25 = (bf16[40,5120]{1,0:T(8,128)(2,1)S(1)}, bf16[40,5120]{1,0:T(8,128)(2,1)S(1)}, u32[]{:S(2)}, u32[]{:S(2)}) collective-permute-start(bf16[40,5120]{1,0:T(8,128)(2,1)S(1)} %slice.215), channel_id=1, source_target_pairs={{0,192},{64,0},{128,64},{192,128},{1,193},{65,1},{129,65},{193,129... | collective-permute-start | bytes 1228808 | tf_op jit(solution)/shard_map/ppermute | solution.py:19
  297.8 17.8 %collective-permute-start.26 = (bf16[40,5120]{1,0:T(8,128)(2,1)S(1)}, bf16[40,5120]{1,0:T(8,128)(2,1)S(1)}, u32[]{:S(2)}, u32[]{:S(2)}) collective-permute-start(bf16[40,5120]{1,0:T(8,128)(2,1)S(1)} %slice.216), channel_id=1, source_target_pairs={{0,64},{64,128},{128,192},{192,0},{1,65},{65,129},{129,193},{193,1... | collective-permute-start | bytes 1228808 | tf_op jit(solution)/shard_map/ppermute | solution.py:19
  298.0 17.7 %collective-permute-start.27 = (bf16[40,5120]{1,0:T(8,128)(2,1)S(1)}, bf16[40,5120]{1,0:T(8,128)(2,1)S(1)}, u32[]{:S(2)}, u32[]{:S(2)}) collective-permute-start(bf16[40,5120]{1,0:T(8,128)(2,1)S(1)} %slice.217), channel_id=1, source_target_pairs={{0,192},{64,0},{128,64},{192,128},{1,193},{65,1},{129,65},{193,129... | collective-permute-start | bytes 1228808 | tf_op jit(solution)/shard_map/ppermute | solution.py:19
  315.7 4.3 collective-permute-start.29
  339.0 25.9 %collective-permute-start.30 = (bf16[640,5120]{1,0:T(8,128)(2,1)}, bf16[640,5120]{1,0:T(8,128)(2,1)}, u32[]{:S(2)}, u32[]{:S(2)}) collective-permute-start(bf16[640,5120]{1,0:T(8,128)(2,1)} %convolution_convert_fusion), channel_id=1, source_target_pairs={{0,16},{16,0},{1,17},{17,1},{2,18},{18,2},{3,19},{19,3},{4,20},{20... | collective-permute-start | bytes 19660808 | tf_op jit(solution)/shard_map/ppermute | solution.py:19
  365.0 25.0 %copy-start.2 = (bf16[640,5120]{1,0:T(8,128)(2,1)S(1)}, bf16[640,5120]{1,0:T(8,128)(2,1)}, u32[]{:S(2)}) copy-start(bf16[640,5120]{1,0:T(8,128)(2,1)} %convolution_convert_fusion.1) | copy-start | bytes 19660804
  368.3 21.6 %collective-permute-start.34 = (bf16[80,5120]{1,0:T(8,128)(2,1)S(1)}, bf16[80,5120]{1,0:T(8,128)(2,1)S(1)}, u32[]{:S(2)}, u32[]{:S(2)}) collective-permute-start(bf16[80,5120]{1,0:T(8,128)(2,1)S(1)} %get-tuple-element.21), channel_id=1, source_target_pairs={{0,64},{64,128},{128,192},{192,0},{1,65},{65,129},{129,193},{193,1... | collective-permute-start | bytes 2457608 | tf_op jit(solution)/shard_map/ppermute | solution.py:19
  369.8 21.6 %collective-permute-start.31 = (bf16[80,5120]{1,0:T(8,128)(2,1)S(1)}, bf16[80,5120]{1,0:T(8,128)(2,1)S(1)}, u32[]{:S(2)}, u32[]{:S(2)}) collective-permute-start(bf16[80,5120]{1,0:T(8,128)(2,1)S(1)} %get-tuple-element.22), channel_id=1, source_target_pairs={{0,192},{64,0},{128,64},{192,128},{1,193},{65,1},{129,65},{193,129... | collective-permute-start | bytes 2457608 | tf_op jit(solution)/shard_map/ppermute | solution.py:19
  391.4 20.5 %collective-permute-start.35 = (bf16[80,5120]{1,0:T(8,128)(2,1)S(1)}, bf16[80,5120]{1,0:T(8,128)(2,1)S(1)}, u32[]{:S(2)}, u32[]{:S(2)}) collective-permute-start(bf16[80,5120]{1,0:T(8,128)(2,1)S(1)} %add_convert_fusion.2), channel_id=1, source_target_pairs={{0,64},{64,128},{128,192},{192,0},{1,65},{65,129},{129,193},{193,1... | collective-permute-start | bytes 2457608 | tf_op jit(solution)/shard_map/ppermute | solution.py:19
  391.5 20.4 %collective-permute-start.32 = (bf16[80,5120]{1,0:T(8,128)(2,1)S(1)}, bf16[80,5120]{1,0:T(8,128)(2,1)S(1)}, u32[]{:S(2)}, u32[]{:S(2)}) collective-permute-start(bf16[80,5120]{1,0:T(8,128)(2,1)S(1)} %get-tuple-element.11), channel_id=1, source_target_pairs={{0,192},{64,0},{128,64},{192,128},{1,193},{65,1},{129,65},{193,129... | collective-permute-start | bytes 2457608 | tf_op jit(solution)/shard_map/ppermute | solution.py:19
  414.7 19.6 %collective-permute-start.36 = (bf16[80,5120]{1,0:T(8,128)(2,1)S(1)}, bf16[80,5120]{1,0:T(8,128)(2,1)S(1)}, u32[]{:S(2)}, u32[]{:S(2)}) collective-permute-start(bf16[80,5120]{1,0:T(8,128)(2,1)S(1)} %get-tuple-element.12), channel_id=1, source_target_pairs={{0,64},{64,128},{128,192},{192,0},{1,65},{65,129},{129,193},{193,1... | collective-permute-start | bytes 2457608 | tf_op jit(solution)/shard_map/ppermute | solution.py:19
  414.8 19.5 %collective-permute-start.33 = (bf16[80,5120]{1,0:T(8,128)(2,1)S(1)}, bf16[80,5120]{1,0:T(8,128)(2,1)S(1)}, u32[]{:S(2)}, u32[]{:S(2)}) collective-permute-start(bf16[80,5120]{1,0:T(8,128)(2,1)S(1)} %get-tuple-element.17), channel_id=1, source_target_pairs={{0,192},{64,0},{128,64},{192,128},{1,193},{65,1},{129,65},{193,129... | collective-permute-start | bytes 2457608 | tf_op jit(solution)/shard_map/ppermute | solution.py:19
  417.5 21.8 %collective-permute-start.37 = (bf16[80,5120]{1,0:T(8,128)(2,1)S(1)}, bf16[80,5120]{1,0:T(8,128)(2,1)S(1)}, u32[]{:S(2)}, u32[]{:S(2)}) collective-permute-start(bf16[80,5120]{1,0:T(8,128)(2,1)S(1)} %get-tuple-element.18), channel_id=1, source_target_pairs={{0,32},{32,0},{1,33},{33,1},{2,34},{34,2},{3,35},{35,3},{4,36},{36... | collective-permute-start | bytes 2457608 | tf_op jit(solution)/shard_map/ppermute | solution.py:19
  444.2 58.2 %copy-start.5 = (bf16[64,5120]{1,0:T(8,128)(2,1)S(1)}, bf16[64,5120]{1,0:T(8,128)(2,1)}, u32[]{:S(2)}) copy-start(bf16[64,5120]{1,0:T(8,128)(2,1)} %copy-done.4) | copy-start | bytes 1966084
  (16 other events, 95.1 us)
Sparse Core Ops, SparseCore 0:
  19.3 71.4 all-gather.2

commit v8 on v6

--- a/solution.py
+++ b/solution.py
@@ -46,8 +46,12 @@
 
 def rs_rel(own, other):
     r = own.shape[0] // 8
-    got = _pp(other, "core", 2, 1)
-    blk = [own[i * r:(i + 1) * r].astype(jnp.float32) + got[i * r:(i + 1) * r].astype(jnp.float32) for i in range(8)]
+    early, late = (7, 3, 5), (6, 4, 2, 1, 0)
+    got_early = _pp(jnp.concatenate([other[i * r:(i + 1) * r] for i in early], 0), "core", 2, 1)
+    got_late = _pp(jnp.concatenate([other[i * r:(i + 1) * r] for i in late], 0), "core", 2, 1)
+    got = {i: got_early[k * r:(k + 1) * r] for k, i in enumerate(early)}
+    got.update({i: got_late[k * r:(k + 1) * r] for k, i in enumerate(late)})
+    blk = [own[i * r:(i + 1) * r].astype(jnp.float32) + got[i].astype(jnp.float32) for i in range(8)]
     b = _pp(blk[7].astype(jnp.bfloat16), "x", 4, 1)
     c = _pp(blk[3].astype(jnp.bfloat16), "x", 4, -1)
     e = _pp((blk[5] + b.astype(jnp.float32)).astype(jnp.bfloat16), "x", 4, 1)

time: 516 us -> 522 us (1.012)
  starting transfers between devices: 82.4 us -> 67.3 us
  blocking collectives: 113 us -> 128 us
  local copies, waits for them, and re-layouts: 44.6 us -> 52.4 us
    ppermute x34 -> x36, starting transfers between devices: 69.5 us -> 54.4 us  [_pp(): return lax.ppermute(v, axis, [(i, (i + shift) % n) for i in range(n)])]
    all_to_all x1, blocking collectives: 55.6 us -> 70.3 us  [local(): lax.all_to_all(expert_out, EXP, split_axis=0, concat_axis=0, tiled=True)]
    unnamed x49 -> x65, local copies, waits for them, and re-layouts: 16.9 us -> 24 us
    ppermute x34 -> x36, waiting for transfers between devices: 173 us -> 172 us  [_pp(): return lax.ppermute(v, axis, [(i, (i + shift) % n) for i in range(n)])]
  transfers between devices with their start and end apart: 36 -> 38, of which waited for: 18 -> 20; matrix products, arithmetic and copies ran while one was open for 12% -> 11% of each run, Pallas kernels for 0% -> 0%
where the time goes in v8:
time: 522 us; the launch traced here: 516 us
  waiting for transfers between devices  187 us (36%)
  blocking collectives  128 us (25%)
  starting transfers between devices  67.3 us (13%)
  local copies, waits for them, and re-layouts  52.4 us (10%)
  matrix products  47.2 us (9%)
  other arithmetic  19.4 us (4%)
  between operations  14.1 us (3%)
    ppermute x36, waiting for transfers between devices, _pp(): return lax.ppermute(v, axis, [(i, (i + shift) % n) for i in range(n)])  172 us
    all_to_all x1, blocking collectives, local(): lax.all_to_all(expert_out, EXP, split_axis=0, concat_axis=0, tiled=True)  70.3 us
    all_to_all x1, blocking collectives, local(): lax.all_to_all(outgoing, EXP, split_axis=0, concat_axis=0, tiled=True)  57.6 us
    ppermute x36, starting transfers between devices, _pp(): return lax.ppermute(v, axis, [(i, (i + shift) % n) for i in range(n)])  54.4 us
    dot_general x2, matrix products, expert_rows(): jnp.dot(inner, down_local, preferred_element_type=jnp.float32)  26.8 us
    unnamed x65, local copies, waits for them, and re-layouts  24 us
    all_to_all x1, waiting for transfers between devices, local(): lax.all_to_all(attended.reshape(tok_rows, n_ctx, qwidth // n_ctx), CTX, s...  15.2 us
    all_to_all x1, starting transfers between devices, local(): lax.all_to_all(attended.reshape(tok_rows, n_ctx, qwidth // n_ctx), CTX, s...  12.8 us
  transfers between devices with their start and end apart: 38, of which 20 were waited for; matrix products, arithmetic and copies ran while one was open for 11% of the time, Pallas kernels for 0%

profile of v8, /device:TPU:1, one launch (start us, length us, event | category | flops | bytes accessed | tf_op | source)
XLA Modules:
  0.0 515.8 jit_solution(6627895052874948386)
XLA Ops:
  8.7 7.8 %collective-permute-start = (bf16[64,1024]{0,1:T(8,128)(2,1)S(1)}, bf16[64,1024]{0,1:T(8,128)(2,1)S(1)}, u32[]{:S(2)}, u32[]{:S(2)}) collective-permute-start(bf16[64,1024]{0,1:T(8,128)(2,1)S(1)} %pad_maximum_fusion.3), channel_id=1, source_target_pairs={{0,32},{32,0},{1,33},{33,1},{2,34},{34,2},{3,35},{35,3},{4,36},{36... | collective-permute-start | bytes 393224 | tf_op jit(solution)/shard_map/ppermute | solution.py:19
  19.9 3.1 collective-permute-done
  23.1 2.9 collective-permute-start.4
  26.1 4.2 collective-permute-done.4
  31.0 2.5 collective-permute-done.2
  33.5 3.8 concatenate.75
  37.3 2.5 collective-permute-start.7
  39.9 2.7 collective-permute-start.6
  42.9 6.1 %collective-permute-done.5 = bf16[64,1024]{0,1:T(8,128)(2,1)} collective-permute-done((bf16[64,1024]{0,1:T(8,128)(2,1)S(1)}, bf16[64,1024]{0,1:T(8,128)(2,1)}, u32[]{:S(2)}, u32[]{:S(2)}) %collective-permute-start.5) | collective-permute-done | bytes 131104 | tf_op jit(solution)/shard_map/ppermute | solution.py:19
  54.7 5.6 %concatenate.77 = bf16[1024,1024]{0,1:T(8,128)(2,1)} concatenate(bf16[64,1024]{0,1:T(8,128)(2,1)S(1)} %pad_maximum_fusion.3, bf16[64,1024]{0,1:T(8,128)(2,1)S(1)} %collective-permute-done, bf16[64,1024]{0,1:T(8,128)(2,1)S(1)} %collective-permute-done.1, bf16[64,1024]{0,1:T(8,128)(2,1)} %collective-permute-done.2, bf16[64,1024]{0,1:T(8,128)(2,1)} %collective-permute-done.3, ...), dimensions={0} | concatenate | bytes 4194304 | tf_op jit(solution)/shard_map/concatenate | solution.py:44
  60.3 3.1 fusion.86
  63.4 4.9 fusion.88
  68.4 2.9 fusion.26
  74.9 12.8 %all-to-all-start = ((bf16[64,16,160]{2,0,1:T(8,128)(2,1)}), bf16[64,16,160]{2,0,1:T(8,128)(2,1)S(1)}, u32[]{:S(2)}, u32[]{:S(2)}) async-start(bf16[64,16,160]{2,0,1:T(8,128)(2,1)} %copy.41), calls=%async_computation | async-start | bytes 1048576 | tf_op jit(solution)/shard_map/all_to_all | solution.py:128
  87.9 15.2 %all-to-all-done = bf16[64,16,160]{2,0,1:T(8,128)(2,1)S(1)} async-done(((bf16[64,16,160]{2,0,1:T(8,128)(2,1)}), bf16[64,16,160]{2,0,1:T(8,128)(2,1)S(1)}, u32[]{:S(2)}, u32[]{:S(2)}) %all-to-all-start) | async-done | bytes 327712 | tf_op jit(solution)/shard_map/all_to_all | solution.py:128
  105.7 4.1 reshape.274
  109.7 2.9 convolution_convert_fusion.2
  118.1 2.8 collective-permute-start.11
  120.9 14.3 %collective-permute-done.14 = bf16[64,5120]{1,0:T(8,128)(2,1)S(1)} collective-permute-done((bf16[64,5120]{1,0:T(8,128)(2,1)S(1)}, bf16[64,5120]{1,0:T(8,128)(2,1)S(1)}, u32[]{:S(2)}, u32[]{:S(2)}) %collective-permute-start.14) | collective-permute-done | bytes 655392 | tf_op jit(solution)/shard_map/ppermute | solution.py:19
  137.8 13.0 %collective-permute-done.12 = bf16[64,5120]{1,0:T(8,128)(2,1)S(1)} collective-permute-done((bf16[64,5120]{1,0:T(8,128)(2,1)S(1)}, bf16[64,5120]{1,0:T(8,128)(2,1)S(1)}, u32[]{:S(2)}, u32[]{:S(2)}) %collective-permute-start.12) | collective-permute-done | bytes 655392 | tf_op jit(solution)/shard_map/ppermute | solution.py:19
  150.8 2.7 collective-permute-done.15
  154.5 2.7 collective-permute-start.13
  158.2 11.1 %collective-permute-done.16 = bf16[64,5120]{1,0:T(8,128)(2,1)S(1)} collective-permute-done((bf16[64,5120]{1,0:T(8,128)(2,1)S(1)}, bf16[64,5120]{1,0:T(8,128)(2,1)S(1)}, u32[]{:S(2)}, u32[]{:S(2)}) %collective-permute-start.16) | collective-permute-done | bytes 655392 | tf_op jit(solution)/shard_map/ppermute | solution.py:19
  169.3 4.9 collective-permute-done.17
  176.4 57.6 %all_to_all.25 = bf16[16,5,5120]{2,1,0:T(8,128)(2,1)} all-to-all(bf16[16,5,5120]{2,1,0:T(8,128)(2,1)S(1)} %copy.42), channel_id=1, replica_groups=mesh['x'=4,'zh'=2,'core'=2,'zl'=4,'y'=4] {'zl','y'}, dimensions={0} | all-to-all | bytes 1638400 | tf_op jit(solution)/shard_map/all_to_all | solution.py:163
  238.4 2.7 collective-permute-start.21
  241.2 16.9 %collective-permute-done.18 = bf16[80,5120]{1,0:T(8,128)(2,1)S(1)} collective-permute-done((bf16[80,5120]{1,0:T(8,128)(2,1)}, bf16[80,5120]{1,0:T(8,128)(2,1)S(1)}, u32[]{:S(2)}, u32[]{:S(2)}) %collective-permute-start.18) | collective-permute-done | bytes 819232 | tf_op jit(solution)/shard_map/ppermute | solution.py:19
  258.1 2.7 collective-permute-start.22
  261.1 14.7 %collective-permute-done.20 = bf16[80,5120]{1,0:T(8,128)(2,1)S(1)} collective-permute-done((bf16[80,5120]{1,0:T(8,128)(2,1)S(1)}, bf16[80,5120]{1,0:T(8,128)(2,1)S(1)}, u32[]{:S(2)}, u32[]{:S(2)}) %collective-permute-start.20) | collective-permute-done | bytes 819232 | tf_op jit(solution)/shard_map/ppermute | solution.py:19
  276.4 4.4 collective-permute-start.25
  280.8 2.7 collective-permute-start.24
  283.5 18.2 %collective-permute-done.23 = bf16[80,5120]{1,0:T(8,128)(2,1)S(1)} collective-permute-done((bf16[80,5120]{1,0:T(8,128)(2,1)S(1)}, bf16[80,5120]{1,0:T(8,128)(2,1)S(1)}, u32[]{:S(2)}, u32[]{:S(2)}) %collective-permute-start.23) | collective-permute-done | bytes 819232 | tf_op jit(solution)/shard_map/ppermute | solution.py:19
  303.3 2.8 collective-permute-done.26
  306.2 2.7 copy-done.6
  308.9 2.7 fusion.7
  311.5 13.4 %convolution_convert_fusion = bf16[640,5120]{1,0:T(8,128)(2,1)} fusion(bf16[1,256,5120]{2,1,0:T(8,128)(2,1)S(1)} %copy-done, f32[640,256]{1,0:T(8,128)} %fusion.7, bf16[640,5120]{1,0:T(8,128)(2,1)} %copy-done.6, bf16[1,5120,256]{2,1,0:T(8,128)(2,1)} %param.23), kind=kOutput, calls=%fused_computation.2 | convolution fusion | flops 3359703040 | bytes 19005440 | tf_op jit(solution)/shard_map/dot_general | solution.py:175
  333.5 3.3 slice_dynamic-update-slice_fusion
  339.6 2.8 copy-done.14
  342.4 2.7 fusion.9
  345.1 13.3 %convolution_convert_fusion.1 = bf16[640,5120]{1,0:T(8,128)(2,1)} fusion(bf16[1,256,5120]{2,1,0:T(8,128)(2,1)S(1)} %copy-done, f32[640,256]{1,0:T(8,128)} %fusion.9, bf16[640,5120]{1,0:T(8,128)(2,1)} %copy-done.14, bf16[1,5120,256]{2,1,0:T(8,128)(2,1)} %param.23), kind=kOutput, calls=%fused_computation.3 | convolution fusion | flops 3359703040 | bytes 19005440 | tf_op jit(solution)/shard_map/dot_general | solution.py:175
  363.8 17.9 %collective-permute-done.32 = bf16[80,5120]{1,0:T(8,128)(2,1)S(1)} collective-permute-done((bf16[80,5120]{1,0:T(8,128)(2,1)S(1)}, bf16[80,5120]{1,0:T(8,128)(2,1)S(1)}, u32[]{:S(2)}, u32[]{:S(2)}) %collective-permute-start.32) | collective-permute-done | bytes 819232 | tf_op jit(solution)/shard_map/ppermute | solution.py:19
  385.8 17.1 %collective-permute-done.30 = bf16[80,5120]{1,0:T(8,128)(2,1)S(1)} collective-permute-done((bf16[80,5120]{1,0:T(8,128)(2,1)S(1)}, bf16[80,5120]{1,0:T(8,128)(2,1)S(1)}, u32[]{:S(2)}, u32[]{:S(2)}) %collective-permute-start.30) | collective-permute-done | bytes 819232 | tf_op jit(solution)/shard_map/ppermute | solution.py:19
  405.2 2.9 add_convert_fusion.5
  408.4 2.7 collective-permute-start.31
  413.3 13.7 %collective-permute-done.34 = bf16[80,5120]{1,0:T(8,128)(2,1)S(1)} collective-permute-done((bf16[80,5120]{1,0:T(8,128)(2,1)S(1)}, bf16[80,5120]{1,0:T(8,128)(2,1)S(1)}, u32[]{:S(2)}, u32[]{:S(2)}) %collective-permute-start.34) | collective-permute-done | bytes 819232 | tf_op jit(solution)/shard_map/ppermute | solution.py:19
  427.0 4.8 collective-permute-done.35
  431.8 2.7 add_convert_fusion
  436.7 70.3 %all_to_all.26 = bf16[16,5,5120]{2,1,0:T(8,128)(2,1)S(1)} all-to-all(bf16[16,5,5120]{2,1,0:T(8,128)(2,1)} %reshape.263), channel_id=1, replica_groups=mesh['x'=4,'zh'=2,'core'=2,'zl'=4,'y'=4] {'zl','y'}, dimensions={0} | all-to-all | bytes 1638400 | tf_op jit(solution)/shard_map/all_to_all | solution.py:181
  (160 shorter events, 67.2 us)
Async XLA Ops:
  6.5 305.0 %copy-start = (bf16[1,256,5120]{2,1,0:T(8,128)(2,1)S(1)}, bf16[1,256,5120]{2,1,0:T(8,128)(2,1)}, u32[]{:S(2)}) copy-start(bf16[1,256,5120]{2,1,0:T(8,128)(2,1)} %param.25) | copy-start | bytes 7864324
  6.5 36.1 %copy-start.20 = (s32[1,4]{1,0:T(1,128)S(1)}, s32[1,4]{1,0:T(1,128)}, u32[]{:S(2)}) copy-start(s32[1,4]{1,0:T(1,128)} %param.17) | copy-start | bytes 52
  6.5 99.1 %all-gather.3.cloned.1.call-start = ((), (), s32[]{:S(2)}) async-start(), calls=%async_computation.3 | async-start | bytes 2785280 | tf_op jit(solution)/shard_map/all_gather | solution.py:127
  8.7 14.4 %collective-permute-start = (bf16[64,1024]{0,1:T(8,128)(2,1)S(1)}, bf16[64,1024]{0,1:T(8,128)(2,1)S(1)}, u32[]{:S(2)}, u32[]{:S(2)}) collective-permute-start(bf16[64,1024]{0,1:T(8,128)(2,1)S(1)} %pad_maximum_fusion.3), channel_id=1, source_target_pairs={{0,32},{32,0},{1,33},{33,1},{2,34},{34,2},{3,35},{35,3},{4,36},{36... | collective-permute-start | bytes 393224 | tf_op jit(solution)/shard_map/ppermute | solution.py:19
  16.5 9.6 %collective-permute-start.1 = (bf16[64,1024]{0,1:T(8,128)(2,1)S(1)}, bf16[64,1024]{0,1:T(8,128)(2,1)S(1)}, u32[]{:S(2)}, u32[]{:S(2)}) collective-permute-start(bf16[64,1024]{0,1:T(8,128)(2,1)S(1)} %pad_maximum_fusion.3), channel_id=1, source_target_pairs={{0,64},{64,128},{128,192},{192,0},{1,65},{65,129},{129,193},{193,1... | collective-permute-start | bytes 393224 | tf_op jit(solution)/shard_map/ppermute | solution.py:19
  17.7 8.4 %collective-permute-start.3 = (bf16[64,1024]{0,1:T(8,128)(2,1)S(1)}, bf16[64,1024]{0,1:T(8,128)(2,1)}, u32[]{:S(2)}, u32[]{:S(2)}) collective-permute-start(bf16[64,1024]{0,1:T(8,128)(2,1)S(1)} %pad_maximum_fusion.3), channel_id=1, source_target_pairs={{0,192},{64,0},{128,64},{192,128},{1,193},{65,1},{129,65},{193,129... | collective-permute-start | bytes 393224 | tf_op jit(solution)/shard_map/ppermute | solution.py:19
  23.1 7.2 %collective-permute-start.4 = (bf16[64,1024]{0,1:T(8,128)(2,1)S(1)}, bf16[64,1024]{0,1:T(8,128)(2,1)S(1)}, u32[]{:S(2)}, u32[]{:S(2)}) collective-permute-start(bf16[64,1024]{0,1:T(8,128)(2,1)S(1)} %collective-permute-done), channel_id=1, source_target_pairs={{0,192},{64,0},{128,64},{192,128},{1,193},{65,1},{129,65},{193,129... | collective-permute-start | bytes 393224 | tf_op jit(solution)/shard_map/ppermute | solution.py:19
  26.0 7.5 %collective-permute-start.2 = (bf16[64,1024]{0,1:T(8,128)(2,1)S(1)}, bf16[64,1024]{0,1:T(8,128)(2,1)}, u32[]{:S(2)}, u32[]{:S(2)}) collective-permute-start(bf16[64,1024]{0,1:T(8,128)(2,1)S(1)} %collective-permute-done), channel_id=1, source_target_pairs={{0,64},{64,128},{128,192},{192,0},{1,65},{65,129},{129,193},{193,1... | collective-permute-start | bytes 393224 | tf_op jit(solution)/shard_map/ppermute | solution.py:19
  37.3 17.4 %collective-permute-start.7 = (bf16[384,1024]{0,1:T(8,128)(2,1)}, bf16[384,1024]{0,1:T(8,128)(2,1)}, u32[]{:S(2)}, u32[]{:S(2)}) collective-permute-start(bf16[384,1024]{0,1:T(8,128)(2,1)} %concatenate.75), channel_id=1, source_target_pairs={{0,16},{16,0},{1,17},{17,1},{2,18},{18,2},{3,19},{19,3},{4,20},{20... | collective-permute-start | bytes 2359304 | tf_op jit(solution)/shard_map/ppermute | solution.py:19
  39.9 9.1 %collective-permute-start.5 = (bf16[64,1024]{0,1:T(8,128)(2,1)S(1)}, bf16[64,1024]{0,1:T(8,128)(2,1)}, u32[]{:S(2)}, u32[]{:S(2)}) collective-permute-start(bf16[64,1024]{0,1:T(8,128)(2,1)S(1)} %collective-permute-done.1), channel_id=1, source_target_pairs={{0,64},{64,128},{128,192},{192,0},{1,65},{65,129},{129,193},{193,1... | collective-permute-start | bytes 393224 | tf_op jit(solution)/shard_map/ppermute | solution.py:19
  39.9 9.1 %collective-permute-start.6 = (bf16[64,1024]{0,1:T(8,128)(2,1)}, bf16[64,1024]{0,1:T(8,128)(2,1)}, u32[]{:S(2)}, u32[]{:S(2)}) collective-permute-start(bf16[64,1024]{0,1:T(8,128)(2,1)} %copy-done.11), channel_id=1, source_target_pairs={{0,192},{64,0},{128,64},{192,128},{1,193},{65,1},{129,65},{193,129... | collective-permute-start | bytes 393224 | tf_op jit(solution)/shard_map/ppermute | solution.py:19
  50.9 3.8 collective-permute-start.8
  74.9 28.2 %all-to-all-start = ((bf16[64,16,160]{2,0,1:T(8,128)(2,1)}), bf16[64,16,160]{2,0,1:T(8,128)(2,1)S(1)}, u32[]{:S(2)}, u32[]{:S(2)}) async-start(bf16[64,16,160]{2,0,1:T(8,128)(2,1)} %copy.41), calls=%async_computation | async-start | bytes 1048576 | tf_op jit(solution)/shard_map/all_to_all | solution.py:128
  113.2 4.4 collective-permute-start.10
  114.1 21.1 %collective-permute-start.9 = (bf16[320,5120]{1,0:T(8,128)(2,1)S(1)}, bf16[320,5120]{1,0:T(8,128)(2,1)S(1)}, u32[]{:S(2)}, u32[]{:S(2)}) collective-permute-start(bf16[320,5120]{1,0:T(8,128)(2,1)S(1)} %get-tuple-element.35), channel_id=1, source_target_pairs={{0,16},{16,0},{1,17},{17,1},{2,18},{18,2},{3,19},{19,3},{4,20},{20... | collective-permute-start | bytes 9830408 | tf_op jit(solution)/shard_map/ppermute | solution.py:19
  118.0 19.8 %copy-start.15 = (bf16[5120]{0:T(1024)(128)(2,1)S(1)}, bf16[5120]{0:T(1024)(128)(2,1)}, u32[]{:S(2)}) copy-start(bf16[5120]{0:T(1024)(128)(2,1)} %param.20) | copy-start | bytes 30724
  118.0 17.2 %collective-permute-start.14 = (bf16[64,5120]{1,0:T(8,128)(2,1)S(1)}, bf16[64,5120]{1,0:T(8,128)(2,1)S(1)}, u32[]{:S(2)}, u32[]{:S(2)}) collective-permute-start(bf16[64,5120]{1,0:T(8,128)(2,1)S(1)} %get-tuple-element.26), channel_id=1, source_target_pairs={{0,64},{64,128},{128,192},{192,0},{1,65},{65,129},{129,193},{193,1... | collective-permute-start | bytes 1966088 | tf_op jit(solution)/shard_map/ppermute | solution.py:19
  118.1 17.5 %collective-permute-start.11 = (bf16[64,5120]{1,0:T(8,128)(2,1)S(1)}, bf16[64,5120]{1,0:T(8,128)(2,1)S(1)}, u32[]{:S(2)}, u32[]{:S(2)}) collective-permute-start(bf16[64,5120]{1,0:T(8,128)(2,1)S(1)} %get-tuple-element.25), channel_id=1, source_target_pairs={{0,192},{64,0},{128,64},{192,128},{1,193},{65,1},{129,65},{193,129... | collective-permute-start | bytes 1966088 | tf_op jit(solution)/shard_map/ppermute | solution.py:19
  135.6 15.1 %collective-permute-start.12 = (bf16[64,5120]{1,0:T(8,128)(2,1)S(1)}, bf16[64,5120]{1,0:T(8,128)(2,1)S(1)}, u32[]{:S(2)}, u32[]{:S(2)}) collective-permute-start(bf16[64,5120]{1,0:T(8,128)(2,1)S(1)} %get-tuple-element.9), channel_id=1, source_target_pairs={{0,192},{64,0},{128,64},{192,128},{1,193},{65,1},{129,65},{193,129... | collective-permute-start | bytes 1966088 | tf_op jit(solution)/shard_map/ppermute | solution.py:19
  137.7 15.7 %collective-permute-start.15 = (bf16[64,5120]{1,0:T(8,128)(2,1)S(1)}, bf16[64,5120]{1,0:T(8,128)(2,1)S(1)}, u32[]{:S(2)}, u32[]{:S(2)}) collective-permute-start(bf16[64,5120]{1,0:T(8,128)(2,1)S(1)} %get-tuple-element.34), channel_id=1, source_target_pairs={{0,64},{64,128},{128,192},{192,0},{1,65},{65,129},{129,193},{193,1... | collective-permute-start | bytes 1966088 | tf_op jit(solution)/shard_map/ppermute | solution.py:19
  137.7 20.2 %copy-start.16 = (s32[1,64,1]{1,2,0:T(1,128)S(1)}, s32[1,64,1]{1,2,0:T(1,128)}, u32[]{:S(2)}) copy-start(s32[1,64,1]{1,2,0:T(1,128)} %param.22) | copy-start | bytes 772
  137.8 36.5 %copy-start.3 = (bf16[1,64,5120]{2,1,0:T(8,128)(2,1)S(1)}, bf16[1,64,5120]{2,1,0:T(8,128)(2,1)}, u32[]{:S(2)}) copy-start(bf16[1,64,5120]{2,1,0:T(8,128)(2,1)} %param.18) | copy-start | bytes 1966084
  154.4 20.6 %copy-start.19 = (bf16[5120,16]{0,1:T(8,128)(2,1)S(1)}, bf16[5120,16]{0,1:T(8,128)(2,1)}, u32[]{:S(2)}) copy-start(bf16[5120,16]{0,1:T(8,128)(2,1)} %param.21) | copy-start | bytes 491524
  154.4 14.9 %collective-permute-start.16 = (bf16[64,5120]{1,0:T(8,128)(2,1)S(1)}, bf16[64,5120]{1,0:T(8,128)(2,1)S(1)}, u32[]{:S(2)}, u32[]{:S(2)}) collective-permute-start(bf16[64,5120]{1,0:T(8,128)(2,1)S(1)} %get-tuple-element.10), channel_id=1, source_target_pairs={{0,64},{64,128},{128,192},{192,0},{1,65},{65,129},{129,193},{193,1... | collective-permute-start | bytes 1966088 | tf_op jit(solution)/shard_map/ppermute | solution.py:19
  154.5 14.8 %collective-permute-start.13 = (bf16[64,5120]{1,0:T(8,128)(2,1)S(1)}, bf16[64,5120]{1,0:T(8,128)(2,1)S(1)}, u32[]{:S(2)}, u32[]{:S(2)}) collective-permute-start(bf16[64,5120]{1,0:T(8,128)(2,1)S(1)} %get-tuple-element.22), channel_id=1, source_target_pairs={{0,192},{64,0},{128,64},{192,128},{1,193},{65,1},{129,65},{193,129... | collective-permute-start | bytes 1966088 | tf_op jit(solution)/shard_map/ppermute | solution.py:19
  157.2 17.1 %collective-permute-start.17 = (bf16[64,5120]{1,0:T(8,128)(2,1)S(1)}, bf16[64,5120]{1,0:T(8,128)(2,1)S(1)}, u32[]{:S(2)}, u32[]{:S(2)}) collective-permute-start(bf16[64,5120]{1,0:T(8,128)(2,1)S(1)} %get-tuple-element.23), channel_id=1, source_target_pairs={{0,32},{32,0},{1,33},{33,1},{2,34},{34,2},{3,35},{35,3},{4,36},{36... | collective-permute-start | bytes 1966088 | tf_op jit(solution)/shard_map/ppermute | solution.py:19
  236.2 21.9 %collective-permute-start.18 = (bf16[80,5120]{1,0:T(8,128)(2,1)}, bf16[80,5120]{1,0:T(8,128)(2,1)S(1)}, u32[]{:S(2)}, u32[]{:S(2)}) collective-permute-start(bf16[80,5120]{1,0:T(8,128)(2,1)} %reshape.262), channel_id=1, source_target_pairs={{0,32},{32,0},{1,33},{33,1},{2,34},{34,2},{3,35},{35,3},{4,36},{36... | collective-permute-start | bytes 2457608 | tf_op jit(solution)/shard_map/ppermute | solution.py:19
  237.1 23.9 %collective-permute-start.19 = (bf16[80,5120]{1,0:T(8,128)(2,1)}, bf16[80,5120]{1,0:T(8,128)(2,1)S(1)}, u32[]{:S(2)}, u32[]{:S(2)}) collective-permute-start(bf16[80,5120]{1,0:T(8,128)(2,1)} %reshape.262), channel_id=1, source_target_pairs={{0,64},{64,128},{128,192},{192,0},{1,65},{65,129},{129,193},{193,1... | collective-permute-start | bytes 2457608 | tf_op jit(solution)/shard_map/ppermute | solution.py:19
  238.4 37.6 %collective-permute-start.21 = (bf16[80,5120]{1,0:T(8,128)(2,1)}, bf16[80,5120]{1,0:T(8,128)(2,1)S(1)}, u32[]{:S(2)}, u32[]{:S(2)}) collective-permute-start(bf16[80,5120]{1,0:T(8,128)(2,1)} %reshape.262), channel_id=1, source_target_pairs={{0,192},{64,0},{128,64},{192,128},{1,193},{65,1},{129,65},{193,129... | collective-permute-start | bytes 2457608 | tf_op jit(solution)/shard_map/ppermute | solution.py:19
  258.1 17.8 %collective-permute-start.20 = (bf16[80,5120]{1,0:T(8,128)(2,1)S(1)}, bf16[80,5120]{1,0:T(8,128)(2,1)S(1)}, u32[]{:S(2)}, u32[]{:S(2)}) collective-permute-start(bf16[80,5120]{1,0:T(8,128)(2,1)S(1)} %collective-permute-done.18), channel_id=1, source_target_pairs={{0,64},{64,128},{128,192},{192,0},{1,65},{65,129},{129,193},{193,1... | collective-permute-start | bytes 2457608 | tf_op jit(solution)/shard_map/ppermute | solution.py:19
  258.1 18.1 %collective-permute-start.22 = (bf16[80,5120]{1,0:T(8,128)(2,1)S(1)}, bf16[80,5120]{1,0:T(8,128)(2,1)S(1)}, u32[]{:S(2)}, u32[]{:S(2)}) collective-permute-start(bf16[80,5120]{1,0:T(8,128)(2,1)S(1)} %collective-permute-done.18), channel_id=1, source_target_pairs={{0,192},{64,0},{128,64},{192,128},{1,193},{65,1},{129,65},{193,129... | collective-permute-start | bytes 2457608 | tf_op jit(solution)/shard_map/ppermute | solution.py:19
  276.4 25.3 %copy-start.13 = (bf16[640,5120]{1,0:T(8,128)(2,1)}, bf16[640,5120]{1,0:T(8,128)(2,1)S(1)}, u32[]{:S(2)}) copy-start(bf16[640,5120]{1,0:T(8,128)(2,1)S(1)} %get-tuple-element.41) | copy-start | bytes 19660804
  276.4 26.5 %collective-permute-start.25 = (bf16[480,5120]{1,0:T(8,128)(2,1)S(1)}, bf16[480,5120]{1,0:T(8,128)(2,1)S(1)}, u32[]{:S(2)}, u32[]{:S(2)}) collective-permute-start(bf16[480,5120]{1,0:T(8,128)(2,1)S(1)} %get-tuple-element.42), channel_id=1, source_target_pairs={{0,16},{16,0},{1,17},{17,1},{2,18},{18,2},{3,19},{19,3},{4,20},{20... | collective-permute-start | bytes 14745608 | tf_op jit(solution)/shard_map/ppermute | solution.py:19
  280.8 20.9 %collective-permute-start.23 = (bf16[80,5120]{1,0:T(8,128)(2,1)S(1)}, bf16[80,5120]{1,0:T(8,128)(2,1)S(1)}, u32[]{:S(2)}, u32[]{:S(2)}) collective-permute-start(bf16[80,5120]{1,0:T(8,128)(2,1)S(1)} %collective-permute-done.19), channel_id=1, source_target_pairs={{0,64},{64,128},{128,192},{192,0},{1,65},{65,129},{129,193},{193,1... | collective-permute-start | bytes 2457608 | tf_op jit(solution)/shard_map/ppermute | solution.py:19
  280.8 20.9 %collective-permute-start.24 = (bf16[80,5120]{1,0:T(8,128)(2,1)S(1)}, bf16[80,5120]{1,0:T(8,128)(2,1)S(1)}, u32[]{:S(2)}, u32[]{:S(2)}) collective-permute-start(bf16[80,5120]{1,0:T(8,128)(2,1)S(1)} %collective-permute-done.22), channel_id=1, source_target_pairs={{0,192},{64,0},{128,64},{192,128},{1,193},{65,1},{129,65},{193,129... | collective-permute-start | bytes 2457608 | tf_op jit(solution)/shard_map/ppermute | solution.py:19
  301.9 4.2 collective-permute-start.26
  331.3 7.6 %slice-start = ((s8[6553600]{0:T(1024)(128)(4,1)}), s8[4194304]{0:T(1024)(128)(4,1)S(1)}, s32[]{:S(2)}) async-start(s8[6553600]{0:T(1024)(128)(4,1)} %bitcast.115), calls=%async_computation.4 | async-start | bytes 8388608
  338.5 20.0 %collective-permute-start.28 = (bf16[240,5120]{1,0:T(8,128)(2,1)}, bf16[240,5120]{1,0:T(8,128)(2,1)}, u32[]{:S(2)}, u32[]{:S(2)}) collective-permute-start(bf16[240,5120]{1,0:T(8,128)(2,1)} %pad_maximum_fusion), channel_id=1, source_target_pairs={{0,16},{16,0},{1,17},{17,1},{2,18},{18,2},{3,19},{19,3},{4,20},{20... | collective-permute-start | bytes 7372808 | tf_op jit(solution)/shard_map/ppermute | solution.py:19
  338.9 42.8 %collective-permute-start.27 = (bf16[400,5120]{1,0:T(8,128)(2,1)}, bf16[400,5120]{1,0:T(8,128)(2,1)}, u32[]{:S(2)}, u32[]{:S(2)}) collective-permute-start(bf16[400,5120]{1,0:T(8,128)(2,1)} %get-tuple-element.29), channel_id=1, source_target_pairs={{0,16},{16,0},{1,17},{17,1},{2,18},{18,2},{3,19},{19,3},{4,20},{20... | collective-permute-start | bytes 12288008 | tf_op jit(solution)/shard_map/ppermute | solution.py:19
  358.5 46.8 %copy-start.2 = (bf16[640,5120]{1,0:T(8,128)(2,1)S(1)}, bf16[640,5120]{1,0:T(8,128)(2,1)}, u32[]{:S(2)}) copy-start(bf16[640,5120]{1,0:T(8,128)(2,1)} %convolution_convert_fusion.1) | copy-start | bytes 19660804
  361.0 20.7 %collective-permute-start.32 = (bf16[80,5120]{1,0:T(8,128)(2,1)S(1)}, bf16[80,5120]{1,0:T(8,128)(2,1)S(1)}, u32[]{:S(2)}, u32[]{:S(2)}) collective-permute-start(bf16[80,5120]{1,0:T(8,128)(2,1)S(1)} %get-tuple-element.21), channel_id=1, source_target_pairs={{0,64},{64,128},{128,192},{192,0},{1,65},{65,129},{129,193},{193,1... | collective-permute-start | bytes 2457608 | tf_op jit(solution)/shard_map/ppermute | solution.py:19
  361.5 22.7 %collective-permute-start.29 = (bf16[80,5120]{1,0:T(8,128)(2,1)S(1)}, bf16[80,5120]{1,0:T(8,128)(2,1)S(1)}, u32[]{:S(2)}, u32[]{:S(2)}) collective-permute-start(bf16[80,5120]{1,0:T(8,128)(2,1)S(1)} %get-tuple-element.20), channel_id=1, source_target_pairs={{0,192},{64,0},{128,64},{192,128},{1,193},{65,1},{129,65},{193,129... | collective-permute-start | bytes 2457608 | tf_op jit(solution)/shard_map/ppermute | solution.py:19
  384.2 18.7 %collective-permute-start.30 = (bf16[80,5120]{1,0:T(8,128)(2,1)S(1)}, bf16[80,5120]{1,0:T(8,128)(2,1)S(1)}, u32[]{:S(2)}, u32[]{:S(2)}) collective-permute-start(bf16[80,5120]{1,0:T(8,128)(2,1)S(1)} %get-tuple-element.11), channel_id=1, source_target_pairs={{0,192},{64,0},{128,64},{192,128},{1,193},{65,1},{129,65},{193,129... | collective-permute-start | bytes 2457608 | tf_op jit(solution)/shard_map/ppermute | solution.py:19
  385.7 19.5 %collective-permute-start.33 = (bf16[80,5120]{1,0:T(8,128)(2,1)S(1)}, bf16[80,5120]{1,0:T(8,128)(2,1)S(1)}, u32[]{:S(2)}, u32[]{:S(2)}) collective-permute-start(bf16[80,5120]{1,0:T(8,128)(2,1)S(1)} %get-tuple-element.28), channel_id=1, source_target_pairs={{0,64},{64,128},{128,192},{192,0},{1,65},{65,129},{129,193},{193,1... | collective-permute-start | bytes 2457608 | tf_op jit(solution)/shard_map/ppermute | solution.py:19
  408.1 18.9 %collective-permute-start.34 = (bf16[80,5120]{1,0:T(8,128)(2,1)S(1)}, bf16[80,5120]{1,0:T(8,128)(2,1)S(1)}, u32[]{:S(2)}, u32[]{:S(2)}) collective-permute-start(bf16[80,5120]{1,0:T(8,128)(2,1)S(1)} %get-tuple-element.12), channel_id=1, source_target_pairs={{0,64},{64,128},{128,192},{192,0},{1,65},{65,129},{129,193},{193,1... | collective-permute-start | bytes 2457608 | tf_op jit(solution)/shard_map/ppermute | solution.py:19
  408.4 18.6 %collective-permute-start.31 = (bf16[80,5120]{1,0:T(8,128)(2,1)S(1)}, bf16[80,5120]{1,0:T(8,128)(2,1)S(1)}, u32[]{:S(2)}, u32[]{:S(2)}) collective-permute-start(bf16[80,5120]{1,0:T(8,128)(2,1)S(1)} %get-tuple-element.17), channel_id=1, source_target_pairs={{0,192},{64,0},{128,64},{192,128},{1,193},{65,1},{129,65},{193,129... | collective-permute-start | bytes 2457608 | tf_op jit(solution)/shard_map/ppermute | solution.py:19
  411.0 20.8 %collective-permute-start.35 = (bf16[80,5120]{1,0:T(8,128)(2,1)S(1)}, bf16[80,5120]{1,0:T(8,128)(2,1)S(1)}, u32[]{:S(2)}, u32[]{:S(2)}) collective-permute-start(bf16[80,5120]{1,0:T(8,128)(2,1)S(1)} %get-tuple-element.18), channel_id=1, source_target_pairs={{0,32},{32,0},{1,33},{33,1},{2,34},{34,2},{3,35},{35,3},{4,36},{36... | collective-permute-start | bytes 2457608 | tf_op jit(solution)/shard_map/ppermute | solution.py:19
  436.7 70.4 %copy-start.5 = (bf16[64,5120]{1,0:T(8,128)(2,1)S(1)}, bf16[64,5120]{1,0:T(8,128)(2,1)}, u32[]{:S(2)}) copy-start(bf16[64,5120]{1,0:T(8,128)(2,1)} %copy-done.4) | copy-start | bytes 1966084
  (13 other events, 34.2 us)
Sparse Core Ops, SparseCore 0:
  19.3 71.4 all-gather.2

commit v9 on v6

--- a/solution.py
+++ b/solution.py
@@ -37,7 +37,8 @@
     r1 = _pp(b, "x", 4, -1)
     l1o = _pp(zo, "x", 4, 1)
     r1o = _pp(zo, "x", 4, -1)
-    l2 = _pp(l1, "x", 4, 1)
+    l2_src, _ = lax.optimization_barrier((l1, l1o))
+    l2 = _pp(l2_src, "x", 4, 1)
     r2o = _pp(r1o, "x", 4, -1)
     first = jnp.concatenate([b, zo, l1, l1o, r1, r1o], 0)
     last = jnp.concatenate([l2, r2o], 0)

time: 516 us -> 516 us (level)
  starting transfers between devices: 82.4 us -> 69.1 us
  blocking collectives: 113 us -> 125 us
    ppermute x34, starting transfers between devices: 69.5 us -> 56.3 us  [_pp(): return lax.ppermute(v, axis, [(i, (i + shift) % n) for i in range(n)])]
    all_to_all x1, blocking collectives: 55.6 us -> 68.8 us  [local(): lax.all_to_all(expert_out, EXP, split_axis=0, concat_axis=0, tiled=True)]
  transfers between devices with their start and end apart: 36 -> 36, of which waited for: 18 -> 17; matrix products, arithmetic and copies ran while one was open for 12% -> 12% of each run, Pallas kernels for 0% -> 0%
where the time goes in v9:
time: 516 us; the launch traced here: 508 us
  waiting for transfers between devices  188 us (36%)
  blocking collectives  125 us (24%)
  starting transfers between devices  69.1 us (13%)
  matrix products  50.2 us (10%)
  local copies, waits for them, and re-layouts  44.5 us (9%)
  other arithmetic  17.5 us (3%)
  between operations  14 us (3%)
    ppermute x34, waiting for transfers between devices, _pp(): return lax.ppermute(v, axis, [(i, (i + shift) % n) for i in range(n)])  172 us
    all_to_all x1, blocking collectives, local(): lax.all_to_all(expert_out, EXP, split_axis=0, concat_axis=0, tiled=True)  68.8 us
    ppermute x34, starting transfers between devices, _pp(): return lax.ppermute(v, axis, [(i, (i + shift) % n) for i in range(n)])  56.3 us
    all_to_all x1, blocking collectives, local(): lax.all_to_all(outgoing, EXP, split_axis=0, concat_axis=0, tiled=True)  56.2 us
    dot_general x2, matrix products, expert_rows(): jnp.dot(inner, down_local, preferred_element_type=jnp.float32)  26.7 us
    unnamed x49, local copies, waits for them, and re-layouts  16.9 us
    all_to_all x1, waiting for transfers between devices, local(): lax.all_to_all(attended.reshape(tok_rows, n_ctx, qwidth // n_ctx), CTX, s...  16 us
    all_to_all x1, starting transfers between devices, local(): lax.all_to_all(attended.reshape(tok_rows, n_ctx, qwidth // n_ctx), CTX, s...  12.7 us
  transfers between devices with their start and end apart: 36, of which 17 were waited for; matrix products, arithmetic and copies ran while one was open for 12% of the time, Pallas kernels for 0%

profile of v9, /device:TPU:1, one launch (start us, length us, event | category | flops | bytes accessed | tf_op | source)
XLA Modules:
  0.0 508.1 jit_solution(11744834154630027791)
XLA Ops:
  8.7 7.8 %collective-permute-start = (bf16[64,1024]{0,1:T(8,128)(2,1)S(1)}, bf16[64,1024]{0,1:T(8,128)(2,1)S(1)}, u32[]{:S(2)}, u32[]{:S(2)}) collective-permute-start(bf16[64,1024]{0,1:T(8,128)(2,1)S(1)} %pad_maximum_fusion.1), channel_id=1, source_target_pairs={{0,32},{32,0},{1,33},{33,1},{2,34},{34,2},{3,35},{35,3},{4,36},{36... | collective-permute-start | bytes 393224 | tf_op jit(solution)/shard_map/ppermute | solution.py:19
  19.9 3.1 collective-permute-done
  26.1 4.7 collective-permute-done.2
  31.5 3.8 concatenate.63
  35.3 2.5 collective-permute-start.7
  40.9 6.1 %collective-permute-done.5 = bf16[64,1024]{0,1:T(8,128)(2,1)} collective-permute-done((bf16[64,1024]{0,1:T(8,128)(2,1)S(1)}, bf16[64,1024]{0,1:T(8,128)(2,1)}, u32[]{:S(2)}, u32[]{:S(2)}) %collective-permute-start.5) | collective-permute-done | bytes 131104 | tf_op jit(solution)/shard_map/ppermute | solution.py:19
  52.6 5.6 %concatenate.65 = bf16[1024,1024]{0,1:T(8,128)(2,1)} concatenate(bf16[64,1024]{0,1:T(8,128)(2,1)S(1)} %pad_maximum_fusion.1, bf16[64,1024]{0,1:T(8,128)(2,1)S(1)} %collective-permute-done, bf16[64,1024]{0,1:T(8,128)(2,1)S(1)} %collective-permute-done.1, bf16[64,1024]{0,1:T(8,128)(2,1)} %copy-done.10, bf16[64,1024]{0,1:T(8,128)(2,1)} %collective-permute-done.3, ...), dimensions={0} | concatenate | bytes 4194304 | tf_op jit(solution)/shard_map/concatenate | solution.py:45
  58.3 3.1 fusion.86
  61.3 4.9 fusion.88
  66.3 2.9 fusion.26
  72.8 12.7 %all-to-all-start = ((bf16[64,16,160]{2,0,1:T(8,128)(2,1)}), bf16[64,16,160]{2,0,1:T(8,128)(2,1)S(1)}, u32[]{:S(2)}, u32[]{:S(2)}) async-start(bf16[64,16,160]{2,0,1:T(8,128)(2,1)} %copy.41), calls=%async_computation | async-start | bytes 1048576 | tf_op jit(solution)/shard_map/all_to_all | solution.py:125
  85.7 16.0 %all-to-all-done = bf16[64,16,160]{2,0,1:T(8,128)(2,1)S(1)} async-done(((bf16[64,16,160]{2,0,1:T(8,128)(2,1)}), bf16[64,16,160]{2,0,1:T(8,128)(2,1)S(1)}, u32[]{:S(2)}, u32[]{:S(2)}) %all-to-all-start) | async-done | bytes 327712 | tf_op jit(solution)/shard_map/all_to_all | solution.py:125
  105.0 4.1 reshape.274
  109.1 3.1 convolution_convert_fusion.2
  114.3 6.8 %collective-permute-done.9 = bf16[512,5120]{1,0:T(8,128)(2,1)S(1)} collective-permute-done((bf16[512,5120]{1,0:T(8,128)(2,1)S(1)}, bf16[512,5120]{1,0:T(8,128)(2,1)S(1)}, u32[]{:S(2)}, u32[]{:S(2)}) %collective-permute-start.9) | collective-permute-done | bytes 5242912 | tf_op jit(solution)/shard_map/ppermute | solution.py:19
  121.9 2.5 collective-permute-start.10
  124.5 14.5 %collective-permute-done.13 = bf16[64,5120]{1,0:T(8,128)(2,1)S(1)} collective-permute-done((bf16[64,5120]{1,0:T(8,128)(2,1)S(1)}, bf16[64,5120]{1,0:T(8,128)(2,1)S(1)}, u32[]{:S(2)}, u32[]{:S(2)}) %collective-permute-start.13) | collective-permute-done | bytes 655392 | tf_op jit(solution)/shard_map/ppermute | solution.py:19
  139.4 2.7 collective-permute-start.11
  142.1 13.6 %collective-permute-done.14 = bf16[64,5120]{1,0:T(8,128)(2,1)S(1)} collective-permute-done((bf16[64,5120]{1,0:T(8,128)(2,1)S(1)}, bf16[64,5120]{1,0:T(8,128)(2,1)S(1)}, u32[]{:S(2)}, u32[]{:S(2)}) %collective-permute-start.14) | collective-permute-done | bytes 655392 | tf_op jit(solution)/shard_map/ppermute | solution.py:19
  156.8 2.7 collective-permute-start.12
  161.4 10.8 %collective-permute-done.15 = bf16[64,5120]{1,0:T(8,128)(2,1)S(1)} collective-permute-done((bf16[64,5120]{1,0:T(8,128)(2,1)S(1)}, bf16[64,5120]{1,0:T(8,128)(2,1)S(1)}, u32[]{:S(2)}, u32[]{:S(2)}) %collective-permute-start.15) | collective-permute-done | bytes 655392 | tf_op jit(solution)/shard_map/ppermute | solution.py:19
  172.2 5.0 collective-permute-done.16
  179.3 56.2 %all_to_all.25 = bf16[16,5,5120]{2,1,0:T(8,128)(2,1)} all-to-all(bf16[16,5,5120]{2,1,0:T(8,128)(2,1)S(1)} %copy.42), channel_id=1, replica_groups=mesh['x'=4,'zh'=2,'core'=2,'zl'=4,'y'=4] {'zl','y'}, dimensions={0} | all-to-all | bytes 1638400 | tf_op jit(solution)/shard_map/all_to_all | solution.py:160
  239.8 2.7 collective-permute-start.20
  242.5 17.2 %collective-permute-done.17 = bf16[80,5120]{1,0:T(8,128)(2,1)S(1)} collective-permute-done((bf16[80,5120]{1,0:T(8,128)(2,1)}, bf16[80,5120]{1,0:T(8,128)(2,1)S(1)}, u32[]{:S(2)}, u32[]{:S(2)}) %collective-permute-start.17) | collective-permute-done | bytes 819232 | tf_op jit(solution)/shard_map/ppermute | solution.py:19
  259.7 2.7 collective-permute-start.21
  262.6 15.0 %collective-permute-done.19 = bf16[80,5120]{1,0:T(8,128)(2,1)S(1)} collective-permute-done((bf16[80,5120]{1,0:T(8,128)(2,1)S(1)}, bf16[80,5120]{1,0:T(8,128)(2,1)S(1)}, u32[]{:S(2)}, u32[]{:S(2)}) %collective-permute-start.19) | collective-permute-done | bytes 819232 | tf_op jit(solution)/shard_map/ppermute | solution.py:19
  278.1 2.6 copy-done.12
  280.7 3.9 collective-permute-start.24
  284.6 2.9 collective-permute-start.23
  287.5 18.1 %collective-permute-done.22 = bf16[80,5120]{1,0:T(8,128)(2,1)S(1)} collective-permute-done((bf16[80,5120]{1,0:T(8,128)(2,1)S(1)}, bf16[80,5120]{1,0:T(8,128)(2,1)S(1)}, u32[]{:S(2)}, u32[]{:S(2)}) %collective-permute-start.22) | collective-permute-done | bytes 819232 | tf_op jit(solution)/shard_map/ppermute | solution.py:19
  307.1 2.7 collective-permute-done.25
  310.0 2.8 copy-done.6
  312.7 2.7 fusion.7
  315.5 13.4 %convolution_convert_fusion = bf16[640,5120]{1,0:T(8,128)(2,1)} fusion(bf16[1,256,5120]{2,1,0:T(8,128)(2,1)S(1)} %copy-done, f32[640,256]{1,0:T(8,128)} %fusion.7, bf16[640,5120]{1,0:T(8,128)(2,1)} %copy-done.6, bf16[1,5120,256]{2,1,0:T(8,128)(2,1)} %param.23), kind=kOutput, calls=%fused_computation.2 | convolution fusion | flops 3359703040 | bytes 19005440 | tf_op jit(solution)/shard_map/dot_general | solution.py:172
  333.8 5.6 %fusion.9 = f32[640,256]{1,0:T(8,128)} fusion(bf16[640,5120]{1,0:T(8,128)(2,1)} %constant_dynamic-update-slice_fusion, bf16[1,5120,256]{2,1,0:T(8,128)(2,1)S(1)} %copy-done.16), kind=kOutput, calls=%fused_computation.18 | convolution fusion | flops 1677721600 | bytes 9830400 | tf_op jit(solution)/shard_map/dot_general | solution.py:170
  339.4 13.4 %convolution_convert_fusion.1 = bf16[640,5120]{1,0:T(8,128)(2,1)} fusion(bf16[1,256,5120]{2,1,0:T(8,128)(2,1)S(1)} %copy-done, f32[640,256]{1,0:T(8,128)} %fusion.9, bf16[640,5120]{1,0:T(8,128)(2,1)} %constant_dynamic-update-slice_fusion, bf16[1,5120,256]{2,1,0:T(8,128)(2,1)} %param.23), kind=kOutput, calls=%fused_computation.3 | convolution fusion | flops 3359703040 | bytes 19005440 | tf_op jit(solution)/shard_map/dot_general | solution.py:172
  352.8 3.3 add_convert_fusion.7
  359.2 18.1 %collective-permute-done.30 = bf16[80,5120]{1,0:T(8,128)(2,1)S(1)} collective-permute-done((bf16[80,5120]{1,0:T(8,128)(2,1)S(1)}, bf16[80,5120]{1,0:T(8,128)(2,1)S(1)}, u32[]{:S(2)}, u32[]{:S(2)}) %collective-permute-start.30) | collective-permute-done | bytes 819232 | tf_op jit(solution)/shard_map/ppermute | solution.py:19
  378.8 2.8 collective-permute-start.28
  381.6 17.2 %collective-permute-done.31 = bf16[80,5120]{1,0:T(8,128)(2,1)S(1)} collective-permute-done((bf16[80,5120]{1,0:T(8,128)(2,1)S(1)}, bf16[80,5120]{1,0:T(8,128)(2,1)S(1)}, u32[]{:S(2)}, u32[]{:S(2)}) %collective-permute-start.31) | collective-permute-done | bytes 819232 | tf_op jit(solution)/shard_map/ppermute | solution.py:19
  398.8 2.9 add_convert_fusion.5
  401.8 2.7 collective-permute-start.29
  404.4 2.4 collective-permute-start.33
  406.8 14.0 %collective-permute-done.32 = bf16[80,5120]{1,0:T(8,128)(2,1)S(1)} collective-permute-done((bf16[80,5120]{1,0:T(8,128)(2,1)S(1)}, bf16[80,5120]{1,0:T(8,128)(2,1)S(1)}, u32[]{:S(2)}, u32[]{:S(2)}) %collective-permute-start.32) | collective-permute-done | bytes 819232 | tf_op jit(solution)/shard_map/ppermute | solution.py:19
  420.9 4.8 collective-permute-done.33
  425.7 2.7 add_convert_fusion
  430.6 68.8 %all_to_all.26 = bf16[16,5,5120]{2,1,0:T(8,128)(2,1)S(1)} all-to-all(bf16[16,5,5120]{2,1,0:T(8,128)(2,1)} %reshape.263), channel_id=1, replica_groups=mesh['x'=4,'zh'=2,'core'=2,'zl'=4,'y'=4] {'zl','y'}, dimensions={0} | all-to-all | bytes 1638400 | tf_op jit(solution)/shard_map/all_to_all | solution.py:178
  (135 shorter events, 53.7 us)
Async XLA Ops:
  6.5 308.9 %copy-start = (bf16[1,256,5120]{2,1,0:T(8,128)(2,1)S(1)}, bf16[1,256,5120]{2,1,0:T(8,128)(2,1)}, u32[]{:S(2)}) copy-start(bf16[1,256,5120]{2,1,0:T(8,128)(2,1)} %param.25) | copy-start | bytes 7864324
  6.5 34.0 %copy-start.18 = (s32[1,4]{1,0:T(1,128)S(1)}, s32[1,4]{1,0:T(1,128)}, u32[]{:S(2)}) copy-start(s32[1,4]{1,0:T(1,128)} %param.17) | copy-start | bytes 52
  6.5 98.4 %all-gather.3.cloned.1.call-start = ((), (), s32[]{:S(2)}) async-start(), calls=%async_computation.3 | async-start | bytes 2785280 | tf_op jit(solution)/shard_map/all_gather | solution.py:124
  8.7 14.4 %collective-permute-start = (bf16[64,1024]{0,1:T(8,128)(2,1)S(1)}, bf16[64,1024]{0,1:T(8,128)(2,1)S(1)}, u32[]{:S(2)}, u32[]{:S(2)}) collective-permute-start(bf16[64,1024]{0,1:T(8,128)(2,1)S(1)} %pad_maximum_fusion.1), channel_id=1, source_target_pairs={{0,32},{32,0},{1,33},{33,1},{2,34},{34,2},{3,35},{35,3},{4,36},{36... | collective-permute-start | bytes 393224 | tf_op jit(solution)/shard_map/ppermute | solution.py:19
  16.5 9.6 %collective-permute-start.1 = (bf16[64,1024]{0,1:T(8,128)(2,1)S(1)}, bf16[64,1024]{0,1:T(8,128)(2,1)S(1)}, u32[]{:S(2)}, u32[]{:S(2)}) collective-permute-start(bf16[64,1024]{0,1:T(8,128)(2,1)S(1)} %pad_maximum_fusion.1), channel_id=1, source_target_pairs={{0,64},{64,128},{128,192},{192,0},{1,65},{65,129},{129,193},{193,1... | collective-permute-start | bytes 393224 | tf_op jit(solution)/shard_map/ppermute | solution.py:19
  17.7 8.4 %collective-permute-start.3 = (bf16[64,1024]{0,1:T(8,128)(2,1)S(1)}, bf16[64,1024]{0,1:T(8,128)(2,1)}, u32[]{:S(2)}, u32[]{:S(2)}) collective-permute-start(bf16[64,1024]{0,1:T(8,128)(2,1)S(1)} %pad_maximum_fusion.1), channel_id=1, source_target_pairs={{0,192},{64,0},{128,64},{192,128},{1,193},{65,1},{129,65},{193,129... | collective-permute-start | bytes 393224 | tf_op jit(solution)/shard_map/ppermute | solution.py:19
  23.1 7.7 %collective-permute-start.2 = (bf16[64,1024]{0,1:T(8,128)(2,1)S(1)}, bf16[64,1024]{0,1:T(8,128)(2,1)S(1)}, u32[]{:S(2)}, u32[]{:S(2)}) collective-permute-start(bf16[64,1024]{0,1:T(8,128)(2,1)S(1)} %collective-permute-done), channel_id=1, source_target_pairs={{0,64},{64,128},{128,192},{192,0},{1,65},{65,129},{129,193},{193,1... | collective-permute-start | bytes 393224 | tf_op jit(solution)/shard_map/ppermute | solution.py:19
  24.7 6.8 %collective-permute-start.4 = (bf16[64,1024]{0,1:T(8,128)(2,1)S(1)}, bf16[64,1024]{0,1:T(8,128)(2,1)}, u32[]{:S(2)}, u32[]{:S(2)}) collective-permute-start(bf16[64,1024]{0,1:T(8,128)(2,1)S(1)} %collective-permute-done), channel_id=1, source_target_pairs={{0,192},{64,0},{128,64},{192,128},{1,193},{65,1},{129,65},{193,129... | collective-permute-start | bytes 393224 | tf_op jit(solution)/shard_map/ppermute | solution.py:19
  35.3 17.3 %collective-permute-start.7 = (bf16[384,1024]{0,1:T(8,128)(2,1)}, bf16[384,1024]{0,1:T(8,128)(2,1)}, u32[]{:S(2)}, u32[]{:S(2)}) collective-permute-start(bf16[384,1024]{0,1:T(8,128)(2,1)} %concatenate.63), channel_id=1, source_target_pairs={{0,16},{16,0},{1,17},{17,1},{2,18},{18,2},{3,19},{19,3},{4,20},{20... | collective-permute-start | bytes 2359304 | tf_op jit(solution)/shard_map/ppermute | solution.py:19
  37.8 9.1 %collective-permute-start.5 = (bf16[64,1024]{0,1:T(8,128)(2,1)S(1)}, bf16[64,1024]{0,1:T(8,128)(2,1)}, u32[]{:S(2)}, u32[]{:S(2)}) collective-permute-start(bf16[64,1024]{0,1:T(8,128)(2,1)S(1)} %collective-permute-done.1), channel_id=1, source_target_pairs={{0,64},{64,128},{128,192},{192,0},{1,65},{65,129},{129,193},{193,1... | collective-permute-start | bytes 393224 | tf_op jit(solution)/shard_map/ppermute | solution.py:19
  38.6 8.4 %collective-permute-start.6 = (bf16[64,1024]{0,1:T(8,128)(2,1)}, bf16[64,1024]{0,1:T(8,128)(2,1)}, u32[]{:S(2)}, u32[]{:S(2)}) collective-permute-start(bf16[64,1024]{0,1:T(8,128)(2,1)} %collective-permute-done.4), channel_id=1, source_target_pairs={{0,192},{64,0},{128,64},{192,128},{1,193},{65,1},{129,65},{193,129... | collective-permute-start | bytes 393224 | tf_op jit(solution)/shard_map/ppermute | solution.py:19
  48.9 3.8 collective-permute-start.8
  72.8 28.9 %all-to-all-start = ((bf16[64,16,160]{2,0,1:T(8,128)(2,1)}), bf16[64,16,160]{2,0,1:T(8,128)(2,1)S(1)}, u32[]{:S(2)}, u32[]{:S(2)}) async-start(bf16[64,16,160]{2,0,1:T(8,128)(2,1)} %copy.41), calls=%async_computation | async-start | bytes 1048576 | tf_op jit(solution)/shard_map/all_to_all | solution.py:125
  105.0 4.1 copy-start.9
  109.1 3.7 copy-start.1
  112.2 8.9 %collective-permute-start.9 = (bf16[512,5120]{1,0:T(8,128)(2,1)S(1)}, bf16[512,5120]{1,0:T(8,128)(2,1)S(1)}, u32[]{:S(2)}, u32[]{:S(2)}) collective-permute-start(bf16[512,5120]{1,0:T(8,128)(2,1)S(1)} %convolution_convert_fusion.2), channel_id=1, source_target_pairs={{0,16},{16,0},{1,17},{17,1},{2,18},{18,2},{3,19},{19,3},{4,20},{20... | collective-permute-start | bytes 15728648 | tf_op jit(solution)/shard_map/ppermute | solution.py:19
  121.7 20.4 %copy-start.13 = (bf16[5120]{0:T(1024)(128)(2,1)S(1)}, bf16[5120]{0:T(1024)(128)(2,1)}, u32[]{:S(2)}) copy-start(bf16[5120]{0:T(1024)(128)(2,1)} %param.20) | copy-start | bytes 30724
  121.7 17.2 %collective-permute-start.13 = (bf16[64,5120]{1,0:T(8,128)(2,1)S(1)}, bf16[64,5120]{1,0:T(8,128)(2,1)S(1)}, u32[]{:S(2)}, u32[]{:S(2)}) collective-permute-start(bf16[64,5120]{1,0:T(8,128)(2,1)S(1)} %get-tuple-element.31), channel_id=1, source_target_pairs={{0,64},{64,128},{128,192},{192,0},{1,65},{65,129},{129,193},{193,1... | collective-permute-start | bytes 1966088 | tf_op jit(solution)/shard_map/ppermute | solution.py:19
  121.9 17.5 %collective-permute-start.10 = (bf16[64,5120]{1,0:T(8,128)(2,1)S(1)}, bf16[64,5120]{1,0:T(8,128)(2,1)S(1)}, u32[]{:S(2)}, u32[]{:S(2)}) collective-permute-start(bf16[64,5120]{1,0:T(8,128)(2,1)S(1)} %get-tuple-element.32), channel_id=1, source_target_pairs={{0,192},{64,0},{128,64},{192,128},{1,193},{65,1},{129,65},{193,129... | collective-permute-start | bytes 1966088 | tf_op jit(solution)/shard_map/ppermute | solution.py:19
  139.2 16.5 %collective-permute-start.14 = (bf16[64,5120]{1,0:T(8,128)(2,1)S(1)}, bf16[64,5120]{1,0:T(8,128)(2,1)S(1)}, u32[]{:S(2)}, u32[]{:S(2)}) collective-permute-start(bf16[64,5120]{1,0:T(8,128)(2,1)S(1)} %add_convert_fusion.10), channel_id=1, source_target_pairs={{0,64},{64,128},{128,192},{192,0},{1,65},{65,129},{129,193},{193,1... | collective-permute-start | bytes 1966088 | tf_op jit(solution)/shard_map/ppermute | solution.py:19
  139.4 16.3 %collective-permute-start.11 = (bf16[64,5120]{1,0:T(8,128)(2,1)S(1)}, bf16[64,5120]{1,0:T(8,128)(2,1)S(1)}, u32[]{:S(2)}, u32[]{:S(2)}) collective-permute-start(bf16[64,5120]{1,0:T(8,128)(2,1)S(1)} %get-tuple-element.12), channel_id=1, source_target_pairs={{0,192},{64,0},{128,64},{192,128},{1,193},{65,1},{129,65},{193,129... | collective-permute-start | bytes 1966088 | tf_op jit(solution)/shard_map/ppermute | solution.py:19
  142.1 19.0 %copy-start.14 = (s32[1,64,1]{1,2,0:T(1,128)S(1)}, s32[1,64,1]{1,2,0:T(1,128)}, u32[]{:S(2)}) copy-start(s32[1,64,1]{1,2,0:T(1,128)} %param.22) | copy-start | bytes 772
  142.1 35.0 %copy-start.3 = (bf16[1,64,5120]{2,1,0:T(8,128)(2,1)S(1)}, bf16[1,64,5120]{2,1,0:T(8,128)(2,1)}, u32[]{:S(2)}) copy-start(bf16[1,64,5120]{2,1,0:T(8,128)(2,1)} %param.18) | copy-start | bytes 1966084
  156.6 21.2 %copy-start.17 = (bf16[5120,16]{0,1:T(8,128)(2,1)S(1)}, bf16[5120,16]{0,1:T(8,128)(2,1)}, u32[]{:S(2)}) copy-start(bf16[5120,16]{0,1:T(8,128)(2,1)} %param.21) | copy-start | bytes 491524
  156.7 15.5 %collective-permute-start.15 = (bf16[64,5120]{1,0:T(8,128)(2,1)S(1)}, bf16[64,5120]{1,0:T(8,128)(2,1)S(1)}, u32[]{:S(2)}, u32[]{:S(2)}) collective-permute-start(bf16[64,5120]{1,0:T(8,128)(2,1)S(1)} %get-tuple-element.13), channel_id=1, source_target_pairs={{0,64},{64,128},{128,192},{192,0},{1,65},{65,129},{129,193},{193,1... | collective-permute-start | bytes 1966088 | tf_op jit(solution)/shard_map/ppermute | solution.py:19
  156.8 15.4 %collective-permute-start.12 = (bf16[64,5120]{1,0:T(8,128)(2,1)S(1)}, bf16[64,5120]{1,0:T(8,128)(2,1)S(1)}, u32[]{:S(2)}, u32[]{:S(2)}) collective-permute-start(bf16[64,5120]{1,0:T(8,128)(2,1)S(1)} %get-tuple-element.27), channel_id=1, source_target_pairs={{0,192},{64,0},{128,64},{192,128},{1,193},{65,1},{129,65},{193,129... | collective-permute-start | bytes 1966088 | tf_op jit(solution)/shard_map/ppermute | solution.py:19
  159.4 17.7 %collective-permute-start.16 = (bf16[64,5120]{1,0:T(8,128)(2,1)S(1)}, bf16[64,5120]{1,0:T(8,128)(2,1)S(1)}, u32[]{:S(2)}, u32[]{:S(2)}) collective-permute-start(bf16[64,5120]{1,0:T(8,128)(2,1)S(1)} %get-tuple-element.28), channel_id=1, source_target_pairs={{0,32},{32,0},{1,33},{33,1},{2,34},{34,2},{3,35},{35,3},{4,36},{36... | collective-permute-start | bytes 1966088 | tf_op jit(solution)/shard_map/ppermute | solution.py:19
  237.7 22.0 %collective-permute-start.17 = (bf16[80,5120]{1,0:T(8,128)(2,1)}, bf16[80,5120]{1,0:T(8,128)(2,1)S(1)}, u32[]{:S(2)}, u32[]{:S(2)}) collective-permute-start(bf16[80,5120]{1,0:T(8,128)(2,1)} %reshape.262), channel_id=1, source_target_pairs={{0,32},{32,0},{1,33},{33,1},{2,34},{34,2},{3,35},{35,3},{4,36},{36... | collective-permute-start | bytes 2457608 | tf_op jit(solution)/shard_map/ppermute | solution.py:19
  238.5 24.1 %collective-permute-start.18 = (bf16[80,5120]{1,0:T(8,128)(2,1)}, bf16[80,5120]{1,0:T(8,128)(2,1)S(1)}, u32[]{:S(2)}, u32[]{:S(2)}) collective-permute-start(bf16[80,5120]{1,0:T(8,128)(2,1)} %reshape.262), channel_id=1, source_target_pairs={{0,64},{64,128},{128,192},{192,0},{1,65},{65,129},{129,193},{193,1... | collective-permute-start | bytes 2457608 | tf_op jit(solution)/shard_map/ppermute | solution.py:19
  239.8 38.0 %collective-permute-start.20 = (bf16[80,5120]{1,0:T(8,128)(2,1)}, bf16[80,5120]{1,0:T(8,128)(2,1)S(1)}, u32[]{:S(2)}, u32[]{:S(2)}) collective-permute-start(bf16[80,5120]{1,0:T(8,128)(2,1)} %reshape.262), channel_id=1, source_target_pairs={{0,192},{64,0},{128,64},{192,128},{1,193},{65,1},{129,65},{193,129... | collective-permute-start | bytes 2457608 | tf_op jit(solution)/shard_map/ppermute | solution.py:19
  259.7 18.0 %collective-permute-start.19 = (bf16[80,5120]{1,0:T(8,128)(2,1)S(1)}, bf16[80,5120]{1,0:T(8,128)(2,1)S(1)}, u32[]{:S(2)}, u32[]{:S(2)}) collective-permute-start(bf16[80,5120]{1,0:T(8,128)(2,1)S(1)} %collective-permute-done.17), channel_id=1, source_target_pairs={{0,64},{64,128},{128,192},{192,0},{1,65},{65,129},{129,193},{193,1... | collective-permute-start | bytes 2457608 | tf_op jit(solution)/shard_map/ppermute | solution.py:19
  259.7 18.3 %collective-permute-start.21 = (bf16[80,5120]{1,0:T(8,128)(2,1)S(1)}, bf16[80,5120]{1,0:T(8,128)(2,1)S(1)}, u32[]{:S(2)}, u32[]{:S(2)}) collective-permute-start(bf16[80,5120]{1,0:T(8,128)(2,1)S(1)} %collective-permute-done.17), channel_id=1, source_target_pairs={{0,192},{64,0},{128,64},{192,128},{1,193},{65,1},{129,65},{193,129... | collective-permute-start | bytes 2457608 | tf_op jit(solution)/shard_map/ppermute | solution.py:19
  280.7 26.1 %collective-permute-start.24 = (bf16[480,5120]{1,0:T(8,128)(2,1)S(1)}, bf16[480,5120]{1,0:T(8,128)(2,1)S(1)}, u32[]{:S(2)}, u32[]{:S(2)}) collective-permute-start(bf16[480,5120]{1,0:T(8,128)(2,1)S(1)} %get-tuple-element.36), channel_id=1, source_target_pairs={{0,16},{16,0},{1,17},{17,1},{2,18},{18,2},{3,19},{19,3},{4,20},{20... | collective-permute-start | bytes 14745608 | tf_op jit(solution)/shard_map/ppermute | solution.py:19
  284.6 21.0 %collective-permute-start.22 = (bf16[80,5120]{1,0:T(8,128)(2,1)S(1)}, bf16[80,5120]{1,0:T(8,128)(2,1)S(1)}, u32[]{:S(2)}, u32[]{:S(2)}) collective-permute-start(bf16[80,5120]{1,0:T(8,128)(2,1)S(1)} %collective-permute-done.18), channel_id=1, source_target_pairs={{0,64},{64,128},{128,192},{192,0},{1,65},{65,129},{129,193},{193,1... | collective-permute-start | bytes 2457608 | tf_op jit(solution)/shard_map/ppermute | solution.py:19
  284.6 21.0 %collective-permute-start.23 = (bf16[80,5120]{1,0:T(8,128)(2,1)S(1)}, bf16[80,5120]{1,0:T(8,128)(2,1)S(1)}, u32[]{:S(2)}, u32[]{:S(2)}) collective-permute-start(bf16[80,5120]{1,0:T(8,128)(2,1)S(1)} %collective-permute-done.21), channel_id=1, source_target_pairs={{0,192},{64,0},{128,64},{192,128},{1,193},{65,1},{129,65},{193,129... | collective-permute-start | bytes 2457608 | tf_op jit(solution)/shard_map/ppermute | solution.py:19
  305.8 4.1 collective-permute-start.25
  307.1 5.6 %copy-start.15 = (bf16[1,5120,256]{2,1,0:T(8,128)(2,1)S(1)}, bf16[1,5120,256]{2,1,0:T(8,128)(2,1)}, u32[]{:S(2)}) copy-start(bf16[1,5120,256]{2,1,0:T(8,128)(2,1)} %param.24) | copy-start | bytes 7864324
  328.9 5.0 copy-start.16
  328.9 24.0 %collective-permute-start.26 = (bf16[640,5120]{1,0:T(8,128)(2,1)}, bf16[640,5120]{1,0:T(8,128)(2,1)}, u32[]{:S(2)}, u32[]{:S(2)}) collective-permute-start(bf16[640,5120]{1,0:T(8,128)(2,1)} %convolution_convert_fusion), channel_id=1, source_target_pairs={{0,16},{16,0},{1,17},{17,1},{2,18},{18,2},{3,19},{19,3},{4,20},{20... | collective-permute-start | bytes 19660808 | tf_op jit(solution)/shard_map/ppermute | solution.py:19
  352.8 24.5 %copy-start.2 = (bf16[640,5120]{1,0:T(8,128)(2,1)S(1)}, bf16[640,5120]{1,0:T(8,128)(2,1)}, u32[]{:S(2)}) copy-start(bf16[640,5120]{1,0:T(8,128)(2,1)} %convolution_convert_fusion.1) | copy-start | bytes 19660804
  356.2 21.1 %collective-permute-start.30 = (bf16[80,5120]{1,0:T(8,128)(2,1)S(1)}, bf16[80,5120]{1,0:T(8,128)(2,1)S(1)}, u32[]{:S(2)}, u32[]{:S(2)}) collective-permute-start(bf16[80,5120]{1,0:T(8,128)(2,1)S(1)} %get-tuple-element.25), channel_id=1, source_target_pairs={{0,64},{64,128},{128,192},{192,0},{1,65},{65,129},{129,193},{193,1... | collective-permute-start | bytes 2457608 | tf_op jit(solution)/shard_map/ppermute | solution.py:19
  357.0 21.8 %collective-permute-start.27 = (bf16[80,5120]{1,0:T(8,128)(2,1)S(1)}, bf16[80,5120]{1,0:T(8,128)(2,1)S(1)}, u32[]{:S(2)}, u32[]{:S(2)}) collective-permute-start(bf16[80,5120]{1,0:T(8,128)(2,1)S(1)} %get-tuple-element.26), channel_id=1, source_target_pairs={{0,192},{64,0},{128,64},{192,128},{1,193},{65,1},{129,65},{193,129... | collective-permute-start | bytes 2457608 | tf_op jit(solution)/shard_map/ppermute | solution.py:19
  378.7 20.1 %collective-permute-start.31 = (bf16[80,5120]{1,0:T(8,128)(2,1)S(1)}, bf16[80,5120]{1,0:T(8,128)(2,1)S(1)}, u32[]{:S(2)}, u32[]{:S(2)}) collective-permute-start(bf16[80,5120]{1,0:T(8,128)(2,1)S(1)} %add_convert_fusion.2), channel_id=1, source_target_pairs={{0,64},{64,128},{128,192},{192,0},{1,65},{65,129},{129,193},{193,1... | collective-permute-start | bytes 2457608 | tf_op jit(solution)/shard_map/ppermute | solution.py:19
  378.8 20.0 %collective-permute-start.28 = (bf16[80,5120]{1,0:T(8,128)(2,1)S(1)}, bf16[80,5120]{1,0:T(8,128)(2,1)S(1)}, u32[]{:S(2)}, u32[]{:S(2)}) collective-permute-start(bf16[80,5120]{1,0:T(8,128)(2,1)S(1)} %get-tuple-element.15), channel_id=1, source_target_pairs={{0,192},{64,0},{128,64},{192,128},{1,193},{65,1},{129,65},{193,129... | collective-permute-start | bytes 2457608 | tf_op jit(solution)/shard_map/ppermute | solution.py:19
  401.7 19.2 %collective-permute-start.32 = (bf16[80,5120]{1,0:T(8,128)(2,1)S(1)}, bf16[80,5120]{1,0:T(8,128)(2,1)S(1)}, u32[]{:S(2)}, u32[]{:S(2)}) collective-permute-start(bf16[80,5120]{1,0:T(8,128)(2,1)S(1)} %get-tuple-element.16), channel_id=1, source_target_pairs={{0,64},{64,128},{128,192},{192,0},{1,65},{65,129},{129,193},{193,1... | collective-permute-start | bytes 2457608 | tf_op jit(solution)/shard_map/ppermute | solution.py:19
  401.8 19.1 %collective-permute-start.29 = (bf16[80,5120]{1,0:T(8,128)(2,1)S(1)}, bf16[80,5120]{1,0:T(8,128)(2,1)S(1)}, u32[]{:S(2)}, u32[]{:S(2)}) collective-permute-start(bf16[80,5120]{1,0:T(8,128)(2,1)S(1)} %get-tuple-element.21), channel_id=1, source_target_pairs={{0,192},{64,0},{128,64},{192,128},{1,193},{65,1},{129,65},{193,129... | collective-permute-start | bytes 2457608 | tf_op jit(solution)/shard_map/ppermute | solution.py:19
  404.4 21.3 %collective-permute-start.33 = (bf16[80,5120]{1,0:T(8,128)(2,1)S(1)}, bf16[80,5120]{1,0:T(8,128)(2,1)S(1)}, u32[]{:S(2)}, u32[]{:S(2)}) collective-permute-start(bf16[80,5120]{1,0:T(8,128)(2,1)S(1)} %get-tuple-element.22), channel_id=1, source_target_pairs={{0,32},{32,0},{1,33},{33,1},{2,34},{34,2},{3,35},{35,3},{4,36},{36... | collective-permute-start | bytes 2457608 | tf_op jit(solution)/shard_map/ppermute | solution.py:19
  430.6 68.8 %copy-start.5 = (bf16[64,5120]{1,0:T(8,128)(2,1)S(1)}, bf16[64,5120]{1,0:T(8,128)(2,1)}, u32[]{:S(2)}) copy-start(bf16[64,5120]{1,0:T(8,128)(2,1)} %copy-done.4) | copy-start | bytes 1966084
  (7 other events, 12.9 us)
Sparse Core Ops, SparseCore 0:
  19.3 71.4 all-gather.2
